TPU v7x, 256 devices: a whole 4x4x8 slice. The times are simulated.
256 devices in a mesh: ctx: 64 (over y, z, core), tp: 4 (over x).
Axes of the slice: x: 4, y: 4, z: 8, core: 2. Of those that a mesh axis runs over, the one named last changes fastest.
Arguments:
- queries: bfloat16 [32768, 4096], P('ctx', 'tp'), may hold values from -160 to 160
- keys: bfloat16 [32768, 512], P('ctx', 'tp'), may hold values from -5 to 5
- values: bfloat16 [32768, 512], P('ctx', 'tp'), may hold values from -6.5 to 6.5
- evicted: int32 [32768, 4], P('ctx', 'tp'), may hold values 0 or 1
- block_lists: int32 [256, 2], P('ctx'), may hold values from 0 to 6, as said below
- map_query: bfloat16 [4, 128, 64], P('tp'), may hold values from -0.5 to 0.5
- map_key: bfloat16 [4, 128, 64], P('tp'), may hold values from -0.5 to 0.5
- state_gain: float32 [4], P('tp'), may hold values from 0.001953125 to 0.0078125
- out_weight: bfloat16 [4096, 8192], P('tp', 'ctx'), may hold values from -0.09375 to 0.09375
Outputs:
- layer_out: bfloat16 [32768, 8192], P('ctx', 'tp')
Inputs may be any that keep to these rules, and one draw needn't show every extreme that they name: `block_lists`: query block b with local index i = b % (4) lists entry 0 = 4 + i - 1 and entry 1 in 0 to 4 + i - 2, so the two entries differ and lie before the diagonal block.
All inputs are finite; a program needn't handle non-finite values. No bound on the sum of `evicted` on one device may be relied on, other than what follows from the above.
Results may differ from a plain program's by a relative error of at most 0.012.
Values may be sent and summed in bfloat16 or wider, within the bound.
No kernel may reach another device: no remote copies, remote signals or barrier semaphores. Data moves between devices by JAX's collectives and lax.ppermute only.
A program may use at most 128 MiB of HBM per device.

v0:
```python
import jax
import jax.numpy as jnp
from jax import lax
from jax.sharding import Mesh
from jax.sharding import PartitionSpec as P

CTX = ("ctx_0", "ctx_1", "ctx_2")


def passed_along(block, axis, distance):
    devices = range(lax.axis_size(axis))
    route = [(i - distance, i) for i in devices if i - distance in devices]
    return lax.ppermute(block, axis, route)


def neutral_like(shard, identity):
    return jax.tree.map(
        lambda a, e: jnp.broadcast_to(jnp.asarray(e, a.dtype), a.shape), shard, identity
    )


def all_in_one(shard, axis):
    leaves = jax.tree.leaves(shard)
    order = sorted(range(len(leaves)), key=lambda k: -leaves[k].size)
    width = (1, *leaves[order[0]].shape)[-1]
    lines = [
        jnp.pad(leaves[k].reshape(-1), (0, -leaves[k].size % width)).reshape(-1, width)
        for k in order
    ]
    both, at, found = (lax.all_gather(jnp.concatenate(lines), axis), 0, {})
    for k, line in zip(order, lines):
        slab = both[:, at : at + len(line)].reshape(len(both), -1)
        found[k] = slab[:, : leaves[k].size].reshape(-1, *leaves[k].shape)
        at += len(line)
    numbers = iter(range(len(leaves)))
    return jax.tree.map(lambda _: found[next(numbers)], shard)


def carried_in(shard, axes, combine, identity):
    before = start = neutral_like(shard, identity)
    running = shard
    for axis in reversed(axes):
        devices, here = (lax.axis_size(axis), lax.axis_index(axis))
        pieces = all_in_one(
            jax.tree.map(
                lambda part, kind: part.astype(kind), running, (jnp.bfloat16, jnp.bfloat16)
            ),
            axis,
        )
        inside, running = (start, start)
        for k in range(devices):
            passed = k < here
            running = combine(
                running, jax.tree.map(lambda part, own: part[k].astype(own.dtype), pieces, shard)
            )
            inside = jax.tree.map(lambda new, old: jnp.where(passed, new, old), running, inside)
        before = combine(inside, before)
    return before


def feature(inputs, kernel):
    return jax.nn.elu(jnp.dot(inputs, kernel, preferred_element_type=jnp.float32)) + 1.0


def add_pair(earlier, later):
    return (earlier[0] + later[0], earlier[1] + later[1])


def body(queries, keys, values, evicted, block_lists, map_query, map_key, state_gain, out_weight):
    tok_rows = keys.shape[0]
    groups_here = map_key.shape[0]
    head_dim = map_key.shape[1]
    blocks_dev = block_lists.shape[0]
    block_rows = tok_rows // blocks_dev
    group_size = queries.shape[1] // (groups_here * head_dim)
    highest = lax.Precision.HIGHEST
    device = lax.axis_index(CTX)
    width_kv = groups_here * head_dim
    neighbour = passed_along(jnp.concatenate([keys, values], axis=1), CTX, 1)
    left_keys = neighbour[:, :width_kv]
    left_values = neighbour[:, width_kv:]
    group = 0
    key_feats = feature(keys, map_key[group]) * evicted.astype(jnp.float32)
    state_terms = [
        jnp.einsum("tr,th->rh", key_feats, values.astype(jnp.float32), precision=highest)
    ]
    norm_terms = [jnp.sum(key_feats, axis=0)]
    totals = jnp.stack(state_terms)
    counts = jnp.stack(norm_terms)
    states, norms = carried_in(
        (totals, counts), CTX, add_pair, (jnp.zeros_like(totals), jnp.zeros_like(counts))
    )
    scale = head_dim ** (-0.5)
    offsets = jnp.arange(block_rows, dtype=jnp.int32)
    group = 0
    window_keys = jnp.concatenate([left_keys, keys], axis=0).reshape(
        2 * blocks_dev, block_rows, head_dim
    )
    window_values = jnp.concatenate([left_values, values], axis=0).reshape(
        2 * blocks_dev, block_rows, head_dim
    )
    query_group = queries.reshape(tok_rows, group_size, head_dim)
    query_feats = feature(query_group, map_query[group])
    reads = jnp.einsum("qhr,rd->qhd", query_feats, states[group], precision=highest)
    mass = jnp.einsum("qhr,r->qh", query_feats, norms[group], precision=highest)
    row_pieces = []
    for local in range(blocks_dev):
        chosen = jnp.concatenate(
            [block_lists[local], jnp.full((1,), blocks_dev + local, jnp.int32)]
        )
        key_rows = jnp.take(window_keys, chosen, axis=0).reshape(-1, head_dim)
        value_rows = jnp.take(window_values, chosen, axis=0).reshape(-1, head_dim)
        positions = (
            ((device - 1) * tok_rows + chosen * block_rows)[:, None] + offsets[None, :]
        ).reshape(-1)
        query_pos = device * tok_rows + local * block_rows + offsets
        valid = (positions[None, :] >= 0) & (positions[None, :] <= query_pos[:, None])
        rows_here = slice(local * block_rows, (local + 1) * block_rows)
        query = query_group[rows_here]
        scores = (
            jnp.einsum("qhd,kd->qhk", query, key_rows, preferred_element_type=jnp.float32) * scale
        )
        scores = jnp.where(valid[:, None, :], scores, -jnp.inf)
        top = jnp.max(scores, axis=2)
        weights = jnp.exp(scores - top[:, :, None])
        total = jnp.sum(weights, axis=2)
        probs = weights.astype(jnp.bfloat16)
        numer = jnp.einsum("qhk,kd->qhd", probs, value_rows, preferred_element_type=jnp.float32)
        damping = jnp.exp(-top) * state_gain[group]
        mixed = (numer + damping[:, :, None] * reads[rows_here]) / (
            total + damping * mass[rows_here]
        )[:, :, None]
        row_pieces.append(mixed.reshape(block_rows, group_size * head_dim).astype(jnp.bfloat16))
    group_cols = jnp.concatenate(row_pieces, axis=0)
    partial_value = jnp.dot(
        group_cols,
        lax.all_gather(out_weight, CTX, axis=1, tiled=True),
        preferred_element_type=jnp.float32,
    )
    summed = lax.psum_scatter(
        partial_value.astype(jnp.bfloat16), "tp", scatter_dimension=1, tiled=True
    )
    return summed


def solution(mesh):
    finer = Mesh(mesh.devices.reshape(4, 8, 2, mesh.shape["tp"]), ("ctx_0", "ctx_1", "ctx_2", "tp"))
    placed = (
        P(CTX, "tp"),
        P(CTX, "tp"),
        P(CTX, "tp"),
        P(CTX, "tp"),
        P(CTX, None),
        P("tp", None, None),
        P("tp", None, None),
        P("tp"),
        P("tp", CTX),
    )
    return jax.shard_map(body, mesh=finer, in_specs=placed, out_specs=P(CTX, "tp"), check_vma=False)
```

profile of v0, /device:TPU:1, one launch (start us, length us, event | category | flops | bytes accessed | tf_op | source)
XLA Modules:
  0.0 225.4 jit_solution(12021237498190135664)
XLA Ops:
  6.5 0.7 all-gather.8.cloned.1.call-update
  7.3 1.7 pad_maximum_fusion
  9.0 4.9 %collective-permute-start = (bf16[512,256]{1,0:T(8,128)(2,1)}, bf16[512,256]{1,0:T(8,128)(2,1)}, u32[]{:S(2)}, u32[]{:S(2)}) collective-permute-start(bf16[512,256]{1,0:T(8,128)(2,1)} %pad_maximum_fusion), channel_id=1, source_target_pairs={{0,4},{4,8},{8,12},{12,16},{16,20},{20,24},{24,28},{28,32},{32,36}... | collective-permute-start | bytes 786440 | tf_op jit(solution)/shard_map/ppermute | solution.py:13
  14.0 0.7 convert_element_type.238
  14.6 1.2 fusion.54
  15.9 1.2 convolution_convert_fusion.1
  17.1 1.8 all-gather.3
  19.0 22.5 %all-gather.4 = bf16[8,65,128]{2,1,0:T(8,128)(2,1)S(1)} all-gather(bf16[1,65,128]{2,1,0:T(8,128)(2,1)S(1)} %maximum_bitcast_fusion.1), channel_id=3, replica_groups=mesh['ctx_0'=4,'ctx_1'=8,'ctx_2'=2,'tp'=4] {'ctx_1'}, dimensions={0}, use_global_device_ids=true | all-gather | bytes 149760 | tf_op jit(solution)/shard_map/all_gather | solution.py:30
  41.5 9.3 %all-gather.5 = bf16[4,65,128]{2,1,0:T(8,128)(2,1)S(1)} all-gather(bf16[1,65,128]{2,1,0:T(8,128)(2,1)S(1)} %maximum_bitcast_fusion.2), channel_id=4, replica_groups=mesh['ctx_0'=4,'ctx_1'=8,'ctx_2'=2,'tp'=4] {'ctx_0'}, dimensions={0}, use_global_device_ids=true | all-gather | bytes 83200 | tf_op jit(solution)/shard_map/all_gather | solution.py:30
  51.3 0.7 compare_and_fusion.6
  51.9 0.7 compare_and_fusion.4
  52.6 0.6 pad_clamp_fusion.2
  53.2 0.6 pad_clamp_fusion.1
  53.8 0.6 pad_clamp_fusion.3
  54.4 0.6 pad_clamp_fusion
  55.2 0.6 broadcast_compare_fusion
  56.1 0.7 add_bitcast_fusion
  56.7 0.8 compare_and_fusion.2
  57.5 0.8 compare_and_fusion.1
  58.3 0.8 compare_and_fusion.3
  59.2 0.5 fusion.48
  59.7 3.7 %fusion.38 = f32[1,512,8]{0,1,2:T(8,128)S(1)} fusion(f32[512,8,64]{0,2,1:T(8,128)S(1)} %get-tuple-element.52, u8[512,64]{0,1:T(8,128)(4,1)S(1)} %get-tuple-element.51, pred[]{:T(512)S(6)} %gt.55, pred[]{:T(512)S(6)} %gt.57, pred[]{:T(512)S(6)} %gt.58, pred[]{:T(512)S(6)} %gt.59, f32[1,64]{1,0:T(1,128)S(1)} %get-tuple-element.25, pred[]{:T(512)S(6)} %gt.60, ...), kind=kOutput, calls=%fused_computation.58 | convolution fusion | flops 4983104 | bytes 1104910 | tf_op jit(solution)/shard_map/qhr,r->qh/dot_general | solution.py:105
  63.4 3.8 %fusion.40 = f32[512,8,128]{0,2,1:T(8,128)} fusion(f32[512,8,64]{0,2,1:T(8,128)S(1)} %get-tuple-element.52, u8[512,64]{0,1:T(8,128)(4,1)S(1)} %get-tuple-element.51, bf16[4,65,128]{2,1,0:T(8,128)(2,1)S(1)} %all-gather.5, pred[]{:T(512)S(6)} %gt.69, pred[]{:T(512)S(6)} %gt.68, pred[]{:T(512)S(6)} %gt.67, pred[]{:T(512)S(6)} %gt.66, pred[]{:T(512)S(6)} %gt.65, ...), kind=kOutput, calls=%fused_computation.59 | convolution fusion | flops 404824064 | bytes 3407886 | tf_op jit(solution)/shard_map/qhr,rd->qhd/dot_general | solution.py:104
  67.2 0.5 iota_add_fusion
  68.5 1.2 copy.102
  70.6 1.0 fusion.152
  71.6 0.7 gather_fusion.2
  72.3 0.7 gather_fusion.3
  73.0 0.7 gather_fusion.4
  73.7 0.7 gather_fusion.5
  74.4 0.7 gather_fusion
  75.1 0.7 gather_fusion.1
  75.8 0.7 gather_fusion.7
  76.5 0.7 gather_fusion.6
  77.3 0.4 fusion.156
  78.1 0.4 fusion.155
  78.5 0.2 fusion.4
  78.9 0.4 fusion.154
  79.3 0.2 fusion
  79.7 0.4 fusion.153
  80.4 1.2 copy-done.2
  81.7 0.4 fusion.12
  82.1 0.4 fusion.13
  82.5 0.4 fusion.14
  82.9 0.6 fusion.15
  83.5 36.6 %all-gather.8.cloned.1.call-done = bf16[1024,8192]{1,0:T(8,128)(2,1)} async-done(((bf16[1024,128]{1,0:T(8,128)(2,1)}), bf16[1024,8192]{1,0:T(8,128)(2,1)}) %all-gather.8.cloned.1.call-update) | async-done | bytes 16777232 | tf_op jit(solution)/shard_map/all_gather | solution.py:137
  120.1 17.4 %convolution_convert_fusion = bf16[512,8192]{1,0:T(8,128)(2,1)} fusion(bf16[1024,8192]{1,0:T(8,128)(2,1)} %all-gather.8.cloned.1.call-done, bf16[128,1024]{0,1:T(8,128)(2,1)S(1)} %bitcast.166, bf16[128,1024]{0,1:T(8,128)(2,1)S(1)} %bitcast.165, bf16[128,1024]{0,1:T(8,128)(2,1)S(1)} %bitcast.164, bf16[128,1024]{0,1:T(8,128)(2,1)S(1)} %bitcast.163), kind=kOutput, calls=%fused_computation.8 | convolution fusion | flops 8598323200 | bytes 26214400 | tf_op jit(solution)/shard_map/dot_general | solution.py:135
  137.5 81.0 %reduce-scatter.2.cloned.1.call-done = bf16[512,2048]{1,0:T(8,128)(2,1)} async-done(((bf16[512,8192]{1,0:T(8,128)(2,1)}), bf16[512,2048]{1,0:T(8,128)(2,1)}) %reduce-scatter.2.cloned.1.call-update) | async-done | bytes 2097168 | tf_op jit(solution)/shard_map/reduce_scatter | solution.py:140
  (80 shorter events, 3.2 us)
Async XLA Ops:
  6.5 52.6 %copy-start = (bf16[1,128,64]{1,2,0:T(8,128)(2,1)S(1)}, bf16[1,128,64]{1,2,0:T(8,128)(2,1)}, u32[]{:S(2)}) copy-start(bf16[1,128,64]{1,2,0:T(8,128)(2,1)} %param.16) | copy-start | bytes 49156
  6.5 44.4 %copy-start.9 = (s32[4,2]{0,1:T(2,128)S(1)}, s32[4,2]{0,1:T(2,128)}, u32[]{:S(2)}) copy-start(s32[4,2]{0,1:T(2,128)} %param.15) | copy-start | bytes 100
  6.5 52.5 %copy-start.1 = (bf16[512,1024]{1,0:T(8,128)(2,1)S(1)}, bf16[512,1024]{1,0:T(8,128)(2,1)}, u32[]{:S(2)}) copy-start(bf16[512,1024]{1,0:T(8,128)(2,1)} %param.11) | copy-start | bytes 3145732
  6.5 113.5 %all-gather.8.cloned.1.call-start = ((), (), s32[]{:S(2)}) async-start(), calls=%async_computation.1 | async-start | bytes 17039360 | tf_op jit(solution)/shard_map/all_gather | solution.py:137
  7.3 211.3 %reduce-scatter.2.cloned.1.call-start = ((), (), s32[]{:S(2)}) async-start(), calls=%async_computation.2 | async-start | bytes 10485760 | tf_op jit(solution)/shard_map/reduce_scatter | solution.py:140
  9.0 61.6 %collective-permute-start = (bf16[512,256]{1,0:T(8,128)(2,1)}, bf16[512,256]{1,0:T(8,128)(2,1)}, u32[]{:S(2)}, u32[]{:S(2)}) collective-permute-start(bf16[512,256]{1,0:T(8,128)(2,1)} %pad_maximum_fusion), channel_id=1, source_target_pairs={{0,4},{4,8},{8,12},{12,16},{16,20},{20,24},{24,28},{28,32},{32,36}... | collective-permute-start | bytes 786440 | tf_op jit(solution)/shard_map/ppermute | solution.py:13
  68.3 3.3 %copy-start.3 = (bf16[512,128]{1,0:T(8,128)(2,1)S(1)}, bf16[512,128]{1,0:T(8,128)(2,1)}, u32[]{:S(2)}) copy-start(bf16[512,128]{1,0:T(8,128)(2,1)} %param.12) | copy-start | bytes 393220
  68.4 1.9 copy-start.10
  68.5 1.9 copy-start.15
  68.5 1.9 copy-start.16
  68.5 3.8 %copy-start.4 = (bf16[512,128]{1,0:T(8,128)(2,1)S(1)}, bf16[512,128]{1,0:T(8,128)(2,1)}, u32[]{:S(2)}) copy-start(bf16[512,128]{1,0:T(8,128)(2,1)} %param.13) | copy-start | bytes 393220
  70.6 6.7 %copy-start.14 = (pred[3]{0:T(512)(128)(4,1)S(1)}, pred[3]{0:T(512)(128)(4,1)}, u32[]{:S(2)}) copy-start(pred[3]{0:T(512)(128)(4,1)} %get-tuple-element.16) | copy-start | bytes 13
  71.6 5.7 %copy-start.7 = (pred[128,384]{0,1:T(8,128)(4,1)S(1)}, pred[128,384]{0,1:T(8,128)(4,1)}, u32[]{:S(2)}) copy-start(pred[128,384]{0,1:T(8,128)(4,1)} %compare_and_fusion.2) | copy-start | bytes 147460
  77.3 0.7 copy-start.13
  77.3 0.8 copy-start.6
  78.1 0.6 copy-start.12
  78.1 0.8 copy-start.5
  78.9 0.7 copy-start.11
  79.7 0.7 copy-start.8
  79.7 2.0 copy-start.2
Sparse Core Ops, SparseCore 0:
  9.9 110.1 all-gather.7
  137.7 80.8 reduce-scatter.1
where the time goes:
time: 226 us; the launch traced here: 225 us
  waiting for transfers between devices  118 us (52%)
  blocking collectives  33.6 us (15%)
  matrix products  31.1 us (14%)
  between operations  14.6 us (6%)
  other arithmetic  12.4 us (5%)
  local copies, waits for them, and re-layouts  10.4 us (5%)
  starting transfers between devices  4.95 us (2%)
    reduce_scatter x1, waiting for transfers between devices, body(): lax.psum_scatter(partial_value.astype(jnp.bfloat16), 'tp', scatter_dimens...  81 us
    all_gather x1, waiting for transfers between devices, body(): lax.all_gather(out_weight, CTX, axis=1, tiled=True)  36.6 us
    all_gather x3, blocking collectives, all_in_one(): both, at, found = (lax.all_gather(jnp.concatenate(lines), axis), 0, {})  33.6 us
    dot_general x1, matrix products, body(): jnp.dot(group_cols, lax.all_gather(out_weight, CTX, axis=1, tiled=True),...  17.4 us
    ppermute x1, starting transfers between devices, passed_along(): return lax.ppermute(block, axis, route)  4.91 us
  transfers between devices with their start and end apart: 3, of which 2 were waited for; matrix products, arithmetic and copies ran while one was open for 15% of the time, Pallas kernels for 0%

commit v1 on v0

--- a/solution.py
+++ b/solution.py
@@ -132,15 +132,30 @@
         )[:, :, None]
         row_pieces.append(mixed.reshape(block_rows, group_size * head_dim).astype(jnp.bfloat16))
     group_cols = jnp.concatenate(row_pieces, axis=0)
-    partial_value = jnp.dot(
-        group_cols,
-        lax.all_gather(out_weight, CTX, axis=1, tiled=True),
-        preferred_element_type=jnp.float32,
-    )
-    summed = lax.psum_scatter(
-        partial_value.astype(jnp.bfloat16), "tp", scatter_dimension=1, tiled=True
-    )
-    return summed
+    n_tp = lax.axis_size("tp")
+    swap = [
+        (rows * n_tp + group, ((rows - group) % n_tp) * n_tp + rows)
+        for group in range(n_tp)
+        for rows in range(n_tp)
+    ]
+    moved = lax.ppermute(out_weight, ("ctx_0", "tp"), swap)
+    gathered = lax.all_gather(moved, CTX, axis=1, tiled=True)
+    width = gathered.shape[1] // n_tp
+    summed = None
+    for shift in range(n_tp):
+        if shift == 0:
+            rows_in = group_cols
+        else:
+            rows_in = lax.ppermute(
+                group_cols, "tp", [(i, (i + shift) % n_tp) for i in range(n_tp)]
+            )
+        term = jnp.dot(
+            rows_in,
+            gathered[:, shift * width : (shift + 1) * width],
+            preferred_element_type=jnp.float32,
+        )
+        summed = term if summed is None else summed + term
+    return summed.astype(jnp.bfloat16)
 
 
 def solution(mesh):

time: 226 us -> 173 us (0.77)
  the two profiles are of different devices: /device:TPU:1 before, /device:TPU:8 now
where the time goes in v1:
time: 173 us
  waiting for transfers between devices  47.6 us (28%)
  blocking collectives  41.6 us (24%)
  matrix products  34 us (20%)
  between operations  14.8 us (9%)
  other arithmetic  12.5 us (7%)
  starting transfers between devices  11.6 us (7%)
  local copies, waits for them, and re-layouts  10.7 us (6%)
    all_gather x3, blocking collectives, all_in_one(): both, at, found = (lax.all_gather(jnp.concatenate(lines), axis), 0, {})  41.6 us
    ppermute x3, waiting for transfers between devices, body(): lax.ppermute(group_cols, 'tp', [(i, (i + shift) % n_tp) for i in range(n_...  33.1 us
    dot_general x4, matrix products, body(): jnp.dot(rows_in, gathered[:, shift * width:(shift + 1) * width], preferre...  20.5 us
    ppermute x1, waiting for transfers between devices, body(): moved = lax.ppermute(out_weight, ('ctx_0', 'tp'), swap)  14.5 us
    ppermute x3, starting transfers between devices, body(): lax.ppermute(group_cols, 'tp', [(i, (i + shift) % n_tp) for i in range(n_...  6.19 us
    dot_general x1, matrix products, body(): jnp.einsum('qhr,rd->qhd', query_feats, states[group], precision=highest)  3.76 us
    dot_general x1, matrix products, body(): mass = jnp.einsum('qhr,r->qh', query_feats, norms[group], precision=highest)  3.73 us
    ppermute x1, starting transfers between devices, body(): moved = lax.ppermute(out_weight, ('ctx_0', 'tp'), swap)  3.53 us
  transfers between devices with their start and end apart: 6, of which 3 were waited for; matrix products, arithmetic and copies ran while one was open for 28% of the time, Pallas kernels for 0%

profile of v1, /device:TPU:8, one launch (start us, length us, event | category | flops | bytes accessed | tf_op | source)
XLA Modules:
  0.0 172.8 jit_solution(16580181285796449305)
XLA Ops:
  6.5 3.5 %collective-permute-start.1 = (bf16[1024,128]{1,0:T(8,128)(2,1)}, bf16[1024,128]{1,0:T(8,128)(2,1)S(1)}, u32[]{:S(2)}, u32[]{:S(2)}) collective-permute-start(bf16[1024,128]{1,0:T(8,128)(2,1)} %param.19), channel_id=1, source_target_pairs={{0,0},{64,65},{128,130},{192,195},{1,192},{65,1},{129,66},{193,131... | collective-permute-start | bytes 786440 | tf_op jit(solution)/shard_map/ppermute | solution.py:141
  10.1 14.5 %collective-permute-done.1 = bf16[1024,128]{1,0:T(8,128)(2,1)S(1)} collective-permute-done((bf16[1024,128]{1,0:T(8,128)(2,1)}, bf16[1024,128]{1,0:T(8,128)(2,1)S(1)}, u32[]{:S(2)}, u32[]{:S(2)}) %collective-permute-start.1) | collective-permute-done | bytes 262176 | tf_op jit(solution)/shard_map/ppermute | solution.py:141
  24.6 0.7 copy-done.5
  25.3 1.7 pad_maximum_fusion.1
  27.0 1.9 %collective-permute-start = (bf16[512,256]{1,0:T(8,128)(2,1)}, bf16[512,256]{1,0:T(8,128)(2,1)}, u32[]{:S(2)}, u32[]{:S(2)}) collective-permute-start(bf16[512,256]{1,0:T(8,128)(2,1)} %pad_maximum_fusion.1), channel_id=1, source_target_pairs={{0,4},{4,8},{8,12},{12,16},{16,20},{20,24},{24,28},{28,32},{32,36}... | collective-permute-start | bytes 786440 | tf_op jit(solution)/shard_map/ppermute | solution.py:13
  28.9 0.7 convert_element_type.238
  29.6 1.2 fusion.55
  30.9 1.2 convolution_convert_fusion
  32.1 3.5 %all-gather.3 = bf16[2,65,128]{2,1,0:T(8,128)(2,1)S(1)} all-gather(bf16[1,65,128]{2,1,0:T(8,128)(2,1)S(1)} %maximum_bitcast_fusion), channel_id=2, replica_groups=mesh['ctx_0'=4,'ctx_1'=8,'ctx_2'=2,'tp'=4] {'ctx_2'}, dimensions={0}, use_global_device_ids=true | all-gather | bytes 49920 | tf_op jit(solution)/shard_map/all_gather | solution.py:30
  35.6 27.4 %all-gather.4 = bf16[8,65,128]{2,1,0:T(8,128)(2,1)S(1)} all-gather(bf16[1,65,128]{2,1,0:T(8,128)(2,1)S(1)} %maximum_bitcast_fusion.1), channel_id=3, replica_groups=mesh['ctx_0'=4,'ctx_1'=8,'ctx_2'=2,'tp'=4] {'ctx_1'}, dimensions={0}, use_global_device_ids=true | all-gather | bytes 149760 | tf_op jit(solution)/shard_map/all_gather | solution.py:30
  63.1 10.7 %all-gather.5 = bf16[4,65,128]{2,1,0:T(8,128)(2,1)S(1)} all-gather(bf16[1,65,128]{2,1,0:T(8,128)(2,1)S(1)} %maximum_bitcast_fusion.2), channel_id=4, replica_groups=mesh['ctx_0'=4,'ctx_1'=8,'ctx_2'=2,'tp'=4] {'ctx_0'}, dimensions={0}, use_global_device_ids=true | all-gather | bytes 83200 | tf_op jit(solution)/shard_map/all_gather | solution.py:30
  74.2 0.6 compare_and_fusion.4
  74.9 0.7 compare_and_fusion.6
  75.5 0.6 pad_clamp_fusion.2
  76.1 0.6 pad_clamp_fusion.3
  76.7 0.6 pad_clamp_fusion
  77.3 0.6 pad_clamp_fusion.1
  78.1 0.6 broadcast_compare_fusion.1
  78.7 0.6 add_bitcast_fusion.1
  79.6 0.8 compare_and_fusion.2
  80.4 0.8 compare_and_fusion.3
  81.2 0.8 compare_and_fusion
  82.0 0.5 fusion.49
  82.6 3.7 %fusion.39 = f32[1,512,8]{0,1,2:T(8,128)S(1)} fusion(f32[512,8,64]{0,2,1:T(8,128)S(1)} %get-tuple-element.52, u8[512,64]{0,1:T(8,128)(4,1)S(1)} %get-tuple-element.51, pred[]{:T(512)S(6)} %gt.55, pred[]{:T(512)S(6)} %gt.57, pred[]{:T(512)S(6)} %gt.58, pred[]{:T(512)S(6)} %gt.59, f32[1,64]{1,0:T(1,128)S(1)} %get-tuple-element.25, pred[]{:T(512)S(6)} %gt.60, ...), kind=kOutput, calls=%fused_computation.60 | convolution fusion | flops 4983104 | bytes 1104910 | tf_op jit(solution)/shard_map/qhr,r->qh/dot_general | solution.py:105
  86.3 3.8 %fusion.41 = f32[512,8,128]{0,2,1:T(8,128)} fusion(f32[512,8,64]{0,2,1:T(8,128)S(1)} %get-tuple-element.52, u8[512,64]{0,1:T(8,128)(4,1)S(1)} %get-tuple-element.51, bf16[4,65,128]{2,1,0:T(8,128)(2,1)S(1)} %all-gather.5, pred[]{:T(512)S(6)} %gt.69, pred[]{:T(512)S(6)} %gt.68, pred[]{:T(512)S(6)} %gt.67, pred[]{:T(512)S(6)} %gt.66, pred[]{:T(512)S(6)} %gt.65, ...), kind=kOutput, calls=%fused_computation.61 | convolution fusion | flops 404824064 | bytes 3407886 | tf_op jit(solution)/shard_map/qhr,rd->qhd/dot_general | solution.py:104
  90.1 0.6 iota_add_fusion.1
  92.1 1.2 copy.102
  93.5 1.0 fusion.152
  94.5 0.7 gather_fusion.6
  95.2 0.7 gather_fusion.4
  96.0 0.7 gather_fusion.7
  96.7 0.7 gather_fusion.5
  97.3 0.7 gather_fusion.2
  98.0 0.7 gather_fusion.3
  98.7 0.7 gather_fusion
  99.4 0.7 gather_fusion.1
  103.3 0.9 copy-done.2
  104.2 0.4 fusion.21
  104.6 0.4 fusion.22
  106.1 3.4 %collective-permute-start.2 = (bf16[512,1024]{0,1:T(8,128)(2,1)S(1)}, bf16[512,1024]{0,1:T(8,128)(2,1)}, u32[]{:S(2)}, u32[]{:S(2)}) collective-permute-start(bf16[512,1024]{0,1:T(8,128)(2,1)S(1)} %pad_maximum_fusion), channel_id=1, source_target_pairs={{0,1},{1,2},{2,3},{3,0},{4,5},{5,6},{6,7},{7,4},{8,9},{9,10},{10,1... | collective-permute-start | bytes 3145736 | tf_op jit(solution)/shard_map/ppermute | solution.py:149
  109.5 1.6 collective-permute-start.3
  111.2 1.2 collective-permute-start.4
  112.3 20.8 %collective-permute-done.2 = bf16[512,1024]{0,1:T(8,128)(2,1)} collective-permute-done((bf16[512,1024]{0,1:T(8,128)(2,1)S(1)}, bf16[512,1024]{0,1:T(8,128)(2,1)}, u32[]{:S(2)}, u32[]{:S(2)}) %collective-permute-start.2) | collective-permute-done | bytes 1048608 | tf_op jit(solution)/shard_map/ppermute | solution.py:149
  133.1 4.9 %fusion.4 = f32[512,2048]{1,0:T(8,128)S(1)} fusion(bf16[512,1024]{0,1:T(8,128)(2,1)} %collective-permute-done.2, bf16[1024,8192]{1,0:T(8,128)(2,1)} %all-gather.8.cloned.1.call-done), kind=kOutput, calls=%fused_computation.12 | convolution fusion | flops 2147483648 | bytes 9437184 | tf_op jit(solution)/shard_map/dot_general | solution.py:152
  138.0 12.3 %collective-permute-done.3 = bf16[512,1024]{0,1:T(8,128)(2,1)} collective-permute-done((bf16[512,1024]{0,1:T(8,128)(2,1)S(1)}, bf16[512,1024]{0,1:T(8,128)(2,1)}, u32[]{:S(2)}, u32[]{:S(2)}) %collective-permute-start.3) | collective-permute-done | bytes 1048608 | tf_op jit(solution)/shard_map/ppermute | solution.py:149
  150.3 4.9 %fusion.2 = f32[512,2048]{1,0:T(8,128)S(1)} fusion(bf16[512,1024]{0,1:T(8,128)(2,1)} %collective-permute-done.3, bf16[1024,8192]{1,0:T(8,128)(2,1)} %all-gather.8.cloned.1.call-done), kind=kOutput, calls=%fused_computation.10 | convolution fusion | flops 2147483648 | bytes 9437184 | tf_op jit(solution)/shard_map/dot_general | solution.py:152
  155.2 4.6 %fusion.6 = f32[512,2048]{1,0:T(8,128)S(1)} fusion(bf16[1024,8192]{1,0:T(8,128)(2,1)} %all-gather.8.cloned.1.call-done, bf16[128,1024]{0,1:T(8,128)(2,1)S(1)} %bitcast.158, bf16[128,1024]{0,1:T(8,128)(2,1)S(1)} %bitcast.156, bf16[128,1024]{0,1:T(8,128)(2,1)S(1)} %bitcast.154, bf16[128,1024]{0,1:T(8,128)(2,1)S(1)} %bitcast.160), kind=kOutput, calls=%fused_computation.14 | convolution fusion | flops 2151677952 | bytes 9437184 | tf_op jit(solution)/shard_map/dot_general | solution.py:152
  159.7 6.2 %add_convert_fusion = bf16[512,2048]{1,0:T(8,128)(2,1)} fusion(f32[512,2048]{1,0:T(8,128)S(1)} %fusion.2, f32[512,2048]{1,0:T(8,128)S(1)} %fusion.6, f32[512,2048]{1,0:T(8,128)S(1)} %fusion.4, bf16[512,1024]{0,1:T(8,128)(2,1)S(1)} %collective-permute-done.4, bf16[1024,8192]{1,0:T(8,128)(2,1)} %all-gather.8.cloned.1.call-done), kind=kOutput, calls=%fused_computation.16 | convolution fusion | flops 2151677952 | bytes 19922944 | tf_op jit(solution)/shard_map/dot_general | solution.py:152
  (91 shorter events, 6.0 us)
Async XLA Ops:
  6.5 75.5 %copy-start = (bf16[1,128,64]{1,2,0:T(8,128)(2,1)S(1)}, bf16[1,128,64]{1,2,0:T(8,128)(2,1)}, u32[]{:S(2)}) copy-start(bf16[1,128,64]{1,2,0:T(8,128)(2,1)} %param.16) | copy-start | bytes 49156
  6.5 67.3 %copy-start.10 = (s32[4,2]{0,1:T(2,128)S(1)}, s32[4,2]{0,1:T(2,128)}, u32[]{:S(2)}) copy-start(s32[4,2]{0,1:T(2,128)} %param.15) | copy-start | bytes 100
  6.5 75.4 %copy-start.1 = (bf16[512,1024]{1,0:T(8,128)(2,1)S(1)}, bf16[512,1024]{1,0:T(8,128)(2,1)}, u32[]{:S(2)}) copy-start(bf16[512,1024]{1,0:T(8,128)(2,1)} %param.11) | copy-start | bytes 3145732
  6.5 126.6 %all-gather.8.cloned.1.call-start = ((), (), s32[]{:S(2)}) async-start(), calls=%async_computation | async-start | bytes 17039360 | tf_op jit(solution)/shard_map/all_gather | solution.py:142
  6.5 18.0 %collective-permute-start.1 = (bf16[1024,128]{1,0:T(8,128)(2,1)}, bf16[1024,128]{1,0:T(8,128)(2,1)S(1)}, u32[]{:S(2)}, u32[]{:S(2)}) collective-permute-start(bf16[1024,128]{1,0:T(8,128)(2,1)} %param.19), channel_id=1, source_target_pairs={{0,0},{64,65},{128,130},{192,195},{1,192},{65,1},{129,66},{193,131... | collective-permute-start | bytes 786440 | tf_op jit(solution)/shard_map/ppermute | solution.py:141
  24.6 0.7 copy-start.5
  27.0 66.5 %collective-permute-start = (bf16[512,256]{1,0:T(8,128)(2,1)}, bf16[512,256]{1,0:T(8,128)(2,1)}, u32[]{:S(2)}, u32[]{:S(2)}) collective-permute-start(bf16[512,256]{1,0:T(8,128)(2,1)} %pad_maximum_fusion.1), channel_id=1, source_target_pairs={{0,4},{4,8},{8,12},{12,16},{16,20},{20,24},{24,28},{28,32},{32,36}... | collective-permute-start | bytes 786440 | tf_op jit(solution)/shard_map/ppermute | solution.py:13
  91.8 2.7 %copy-start.3 = (bf16[512,128]{1,0:T(8,128)(2,1)S(1)}, bf16[512,128]{1,0:T(8,128)(2,1)}, u32[]{:S(2)}) copy-start(bf16[512,128]{1,0:T(8,128)(2,1)} %param.12) | copy-start | bytes 393220
  92.0 1.3 copy-start.11
  92.0 1.3 copy-start.16
  92.0 1.2 copy-start.17
  92.1 3.9 %copy-start.4 = (bf16[512,128]{1,0:T(8,128)(2,1)S(1)}, bf16[512,128]{1,0:T(8,128)(2,1)}, u32[]{:S(2)}) copy-start(bf16[512,128]{1,0:T(8,128)(2,1)} %param.13) | copy-start | bytes 393220
  93.5 6.7 %copy-start.15 = (pred[3]{0:T(512)(128)(4,1)S(1)}, pred[3]{0:T(512)(128)(4,1)}, u32[]{:S(2)}) copy-start(pred[3]{0:T(512)(128)(4,1)} %get-tuple-element.27) | copy-start | bytes 13
  94.5 5.7 %copy-start.8 = (pred[128,384]{0,1:T(8,128)(4,1)S(1)}, pred[128,384]{0,1:T(8,128)(4,1)}, u32[]{:S(2)}) copy-start(pred[128,384]{0,1:T(8,128)(4,1)} %compare_and_fusion) | copy-start | bytes 147460
  100.2 0.7 copy-start.14
  100.3 0.8 copy-start.7
  101.1 0.6 copy-start.13
  101.8 0.7 copy-start.12
  101.8 0.8 copy-start.6
  102.6 0.7 copy-start.9
  102.6 1.6 copy-start.2
  106.1 27.0 %collective-permute-start.2 = (bf16[512,1024]{0,1:T(8,128)(2,1)S(1)}, bf16[512,1024]{0,1:T(8,128)(2,1)}, u32[]{:S(2)}, u32[]{:S(2)}) collective-permute-start(bf16[512,1024]{0,1:T(8,128)(2,1)S(1)} %pad_maximum_fusion), channel_id=1, source_target_pairs={{0,1},{1,2},{2,3},{3,0},{4,5},{5,6},{6,7},{7,4},{8,9},{9,10},{10,1... | collective-permute-start | bytes 3145736 | tf_op jit(solution)/shard_map/ppermute | solution.py:149
  109.5 40.7 %collective-permute-start.3 = (bf16[512,1024]{0,1:T(8,128)(2,1)S(1)}, bf16[512,1024]{0,1:T(8,128)(2,1)}, u32[]{:S(2)}, u32[]{:S(2)}) collective-permute-start(bf16[512,1024]{0,1:T(8,128)(2,1)S(1)} %pad_maximum_fusion), channel_id=1, source_target_pairs={{0,2},{1,3},{2,0},{3,1},{4,6},{5,7},{6,4},{7,5},{8,10},{9,11},{10,... | collective-permute-start | bytes 3145736 | tf_op jit(solution)/shard_map/ppermute | solution.py:149
  111.2 48.6 %collective-permute-start.4 = (bf16[512,1024]{0,1:T(8,128)(2,1)S(1)}, bf16[512,1024]{0,1:T(8,128)(2,1)S(1)}, u32[]{:S(2)}, u32[]{:S(2)}) collective-permute-start(bf16[512,1024]{0,1:T(8,128)(2,1)S(1)} %pad_maximum_fusion), channel_id=1, source_target_pairs={{0,3},{1,0},{2,1},{3,2},{4,7},{5,4},{6,5},{7,6},{8,11},{9,8},{10,9... | collective-permute-start | bytes 3145736 | tf_op jit(solution)/shard_map/ppermute | solution.py:149
Sparse Core Ops, SparseCore 0:
  25.4 106.2 all-gather.7

commit v2 on v0

--- a/solution.py
+++ b/solution.py
@@ -87,9 +87,22 @@
     norm_terms = [jnp.sum(key_feats, axis=0)]
     totals = jnp.stack(state_terms)
     counts = jnp.stack(norm_terms)
-    states, norms = carried_in(
-        (totals, counts), CTX, add_pair, (jnp.zeros_like(totals), jnp.zeros_like(counts))
-    )
+    packed = jnp.concatenate(
+        [totals[0], jnp.pad(counts, ((0, 0), (0, totals.shape[2] - counts.shape[1])))], axis=0
+    )
+    packed = packed.astype(jnp.float32)
+    n_ctx = lax.axis_size(CTX)
+    running = packed
+    distance = 1
+    while distance < n_ctx:
+        arrived = lax.ppermute(
+            running, CTX, [(i, i + distance) for i in range(n_ctx - distance)]
+        )
+        running = running + arrived
+        distance *= 2
+    before = running - packed
+    states = before[None, : totals.shape[1]]
+    norms = before[None, totals.shape[1], : counts.shape[1]]
     scale = head_dim ** (-0.5)
     offsets = jnp.arange(block_rows, dtype=jnp.int32)
     group = 0
@@ -132,15 +145,52 @@
         )[:, :, None]
         row_pieces.append(mixed.reshape(block_rows, group_size * head_dim).astype(jnp.bfloat16))
     group_cols = jnp.concatenate(row_pieces, axis=0)
-    partial_value = jnp.dot(
-        group_cols,
-        lax.all_gather(out_weight, CTX, axis=1, tiled=True),
-        preferred_element_type=jnp.float32,
-    )
-    summed = lax.psum_scatter(
-        partial_value.astype(jnp.bfloat16), "tp", scatter_dimension=1, tiled=True
-    )
-    return summed
+    n_tp = lax.axis_size("tp")
+    n_z = lax.axis_size("ctx_1")
+    n_core = lax.axis_size("ctx_2")
+    every = ("ctx_0", "ctx_1", "ctx_2", "tp")
+
+    def flat(y, z, core, x):
+        return ((y * n_z + z) * n_core + core) * n_tp + x
+
+    swap = []
+    for y in range(n_tp):
+        for z in range(n_z):
+            for core in range(n_core):
+                for x in range(n_tp):
+                    piece = z * n_core + core
+                    swap.append(
+                        (
+                            flat(y, z, core, x),
+                            flat((y - x) % n_tp, piece % n_z, piece // n_z, y),
+                        )
+                    )
+    moved = lax.ppermute(out_weight, every, swap)
+    own_half = lax.all_gather(moved, ("ctx_0", "ctx_1"), axis=1, tiled=True)
+    own_half, _ = lax.optimization_barrier((own_half, group_cols))
+    other_half = lax.ppermute(own_half, "ctx_2", [(0, 1), (1, 0)])
+    width = own_half.shape[1] // n_tp
+    rows_by_shift = [group_cols] + [
+        lax.ppermute(group_cols, "tp", [(i, (i + shift) % n_tp) for i in range(n_tp)])
+        for shift in range(1, n_tp)
+    ]
+
+    def project(half):
+        summed = None
+        for shift in range(n_tp):
+            term = jnp.dot(
+                rows_by_shift[shift],
+                half[:, shift * width : (shift + 1) * width],
+                preferred_element_type=jnp.float32,
+            )
+            summed = term if summed is None else summed + term
+        return summed
+
+    mine = project(own_half)
+    theirs = project(other_half)
+    core = lax.axis_index("ctx_2")
+    halves = jnp.where(core == 0, jnp.stack([mine, theirs]), jnp.stack([theirs, mine]))
+    return jnp.concatenate([halves[0], halves[1]], axis=1).astype(jnp.bfloat16)
 
 
 def solution(mesh):

time: 226 us -> 213 us (0.942)
  starting transfers between devices: 4.95 us -> 54.7 us
  waiting for transfers between devices: 118 us -> 77.3 us
  blocking collectives: 33.6 us -> 0 us
  local copies, waits for them, and re-layouts: 10.4 us -> 17.2 us
  matrix products: 31.1 us -> 33.6 us
    reduce_scatter x1 -> x0, waiting for transfers between devices: 81 us -> none  [body(): lax.psum_scatter(partial_value.astype(jnp.bfloat16), 'tp', scatter_dimens...]
    ppermute x0 -> x11, waiting for transfers between devices: none -> 53.3 us  [the longest x3 41.7 us: body(): lax.ppermute(group_cols, 'tp', [(i, (i + shift) % n_tp) for i in range(n_...]
    ppermute x0 -> x11, starting transfers between devices: none -> 49.2 us  [the longest x6 35.6 us: body(): lax.ppermute(running, CTX, [(i, i + distance) for i in range(n_ctx - dist...]
    all_gather x3 -> x0, blocking collectives: 33.6 us -> none  [all_in_one(): both, at, found = (lax.all_gather(jnp.concatenate(lines), axis), 0, {})]
    all_gather x1, waiting for transfers between devices: 36.6 us -> 24 us  [body(): own_half = lax.all_gather(moved, ('ctx_0', 'ctx_1'), axis=1, tiled=True)]
    unnamed x41 -> x58, local copies, waits for them, and re-layouts: 2.34 us -> 4.92 us
    dot_general x1 -> x8, matrix products: 17.4 us -> 19.9 us  [project(): jnp.dot(rows_by_shift[shift], half[:, shift * width:(shift + 1) * width],...]
  transfers between devices with their start and end apart: 3 -> 13, of which waited for: 2 -> 8; matrix products, arithmetic and copies ran while one was open for 15% -> 23% of each run, Pallas kernels for 0% -> 0%
where the time goes in v2:
time: 213 us; the launch traced here: 212 us
  waiting for transfers between devices  77.3 us (36%)
  starting transfers between devices  54.7 us (26%)
  matrix products  33.6 us (16%)
  local copies, waits for them, and re-layouts  17.2 us (8%)
  between operations  14.8 us (7%)
  other arithmetic  14.3 us (7%)
    ppermute x3, waiting for transfers between devices, body(): lax.ppermute(group_cols, 'tp', [(i, (i + shift) % n_tp) for i in range(n_...  41.7 us
    ppermute x6, starting transfers between devices, body(): lax.ppermute(running, CTX, [(i, i + distance) for i in range(n_ctx - dist...  35.6 us
    all_gather x1, waiting for transfers between devices, body(): own_half = lax.all_gather(moved, ('ctx_0', 'ctx_1'), axis=1, tiled=True)  24 us
    dot_general x8, matrix products, project(): jnp.dot(rows_by_shift[shift], half[:, shift * width:(shift + 1) * width],...  19.9 us
    ppermute x1, waiting for transfers between devices, body(): moved = lax.ppermute(out_weight, every, swap)  9.52 us
    ppermute x1, starting transfers between devices, passed_along(): return lax.ppermute(block, axis, route)  5.48 us
    ppermute x1, starting transfers between devices, body(): moved = lax.ppermute(out_weight, every, swap)  5.04 us
    unnamed x58, local copies, waits for them, and re-layouts  4.92 us
  transfers between devices with their start and end apart: 13, of which 8 were waited for; matrix products, arithmetic and copies ran while one was open for 23% of the time, Pallas kernels for 0%

profile of v2, /device:TPU:1, one launch (start us, length us, event | category | flops | bytes accessed | tf_op | source)
XLA Modules:
  0.0 211.9 jit_solution(13957906416965611551)
XLA Ops:
  6.5 5.0 %collective-permute-start.7 = (bf16[1024,128]{1,0:T(8,128)(2,1)}, bf16[1024,128]{1,0:T(8,128)(2,1)S(1)}, u32[]{:S(2)}, u32[]{:S(2)}) collective-permute-start(bf16[1024,128]{1,0:T(8,128)(2,1)} %param.19), channel_id=1, source_target_pairs={{0,0},{1,192},{2,128},{3,64},{4,8},{5,200},{6,136},{7,72},{8,16},{... | collective-permute-start | bytes 786440 | tf_op jit(solution)/shard_map/ppermute | solution.py:168
  11.6 9.5 %collective-permute-done.7 = bf16[1024,128]{1,0:T(8,128)(2,1)S(1)} collective-permute-done((bf16[1024,128]{1,0:T(8,128)(2,1)}, bf16[1024,128]{1,0:T(8,128)(2,1)S(1)}, u32[]{:S(2)}, u32[]{:S(2)}) %collective-permute-start.7) | collective-permute-done | bytes 262176 | tf_op jit(solution)/shard_map/ppermute | solution.py:168
  22.5 1.2 fusion.64
  23.8 1.2 fusion.65
  24.9 1.9 collective-permute-start.1
  26.9 1.7 pad_maximum_fusion.2
  28.6 5.5 %collective-permute-start = (bf16[512,256]{1,0:T(8,128)(2,1)}, bf16[512,256]{1,0:T(8,128)(2,1)}, u32[]{:S(2)}, u32[]{:S(2)}) collective-permute-start(bf16[512,256]{1,0:T(8,128)(2,1)} %pad_maximum_fusion.2), channel_id=1, source_target_pairs={{0,4},{4,8},{8,12},{12,16},{16,20},{20,24},{24,28},{28,32},{32,36}... | collective-permute-start | bytes 786440 | tf_op jit(solution)/shard_map/ppermute | solution.py:13
  34.1 1.0 slice_reduce_fusion.3
  35.9 0.8 compare_and_fusion.2
  36.7 0.8 compare_and_fusion.3
  38.3 0.8 compare_and_fusion.1
  40.4 4.9 %collective-permute-start.2 = (f32[65,128]{1,0:T(8,128)S(1)}, f32[65,128]{1,0:T(8,128)S(1)}, u32[]{:S(2)}, u32[]{:S(2)}) collective-permute-start(f32[65,128]{1,0:T(8,128)S(1)} %fusion.85), channel_id=1, source_target_pairs={{0,8},{4,12},{8,16},{12,20},{16,24},{20,28},{24,32},{28,36},{32,40... | collective-permute-start | bytes 99848 | tf_op jit(solution)/shard_map/ppermute | solution.py:98
  45.9 0.8 collective-permute-done.2
  46.7 5.0 %collective-permute-start.3 = (f32[65,128]{1,0:T(8,128)S(1)}, f32[65,128]{1,0:T(8,128)S(1)}, u32[]{:S(2)}, u32[]{:S(2)}) collective-permute-start(f32[65,128]{1,0:T(8,128)S(1)} %add.278), channel_id=1, source_target_pairs={{0,16},{4,20},{8,24},{12,28},{16,32},{20,36},{24,40},{28,44},{32,4... | collective-permute-start | bytes 99848 | tf_op jit(solution)/shard_map/ppermute | solution.py:98
  52.8 9.8 %collective-permute-start.4 = (f32[65,128]{1,0:T(8,128)S(1)}, f32[65,128]{1,0:T(8,128)S(1)}, u32[]{:S(2)}, u32[]{:S(2)}) collective-permute-start(f32[65,128]{1,0:T(8,128)S(1)} %add.279), channel_id=1, source_target_pairs={{0,32},{4,36},{8,40},{12,44},{16,48},{20,52},{24,56},{28,60},{32,6... | collective-permute-start | bytes 99848 | tf_op jit(solution)/shard_map/ppermute | solution.py:98
  63.6 8.6 %collective-permute-start.5 = (f32[65,128]{1,0:T(8,128)S(1)}, f32[65,128]{1,0:T(8,128)S(1)}, u32[]{:S(2)}, u32[]{:S(2)}) collective-permute-start(f32[65,128]{1,0:T(8,128)S(1)} %add.280), channel_id=1, source_target_pairs={{0,64},{4,68},{8,72},{12,76},{16,80},{20,84},{24,88},{28,92},{32,9... | collective-permute-start | bytes 99848 | tf_op jit(solution)/shard_map/ppermute | solution.py:98
  73.2 5.5 %collective-permute-start.6 = (f32[65,128]{1,0:T(8,128)S(1)}, f32[65,128]{1,0:T(8,128)S(1)}, u32[]{:S(2)}, u32[]{:S(2)}) collective-permute-start(f32[65,128]{1,0:T(8,128)S(1)} %add.281), channel_id=1, source_target_pairs={{0,128},{4,132},{8,136},{12,140},{16,144},{20,148},{24,152},{28,15... | collective-permute-start | bytes 99848 | tf_op jit(solution)/shard_map/ppermute | solution.py:98
  80.1 0.9 copy.55
  81.0 0.8 copy.54
  81.8 0.8 copy.56
  83.2 3.7 %fusion.48 = f32[1,512,8]{0,1,2:T(8,128)S(1)} fusion(f32[512,8,64]{0,2,1:T(8,128)S(1)} %get-tuple-element.53, u8[512,64]{0,1:T(8,128)(4,1)S(1)} %get-tuple-element.52, f32[65,128]{1,0:T(8,128)S(1)} %add_subtract_fusion), kind=kOutput, calls=%fused_computation.73 | convolution fusion | flops 4980736 | bytes 1098240 | tf_op jit(solution)/shard_map/qhr,r->qh/dot_general | solution.py:118
  87.0 1.2 copy.39
  88.2 3.2 %fusion.50 = f32[512,8,128]{0,2,1:T(8,128)S(1)} fusion(f32[512,8,64]{0,2,1:T(8,128)S(1)} %get-tuple-element.53, u8[512,64]{0,1:T(8,128)(4,1)} %copy-done.11, f32[65,128]{1,0:T(8,128)} %copy-done.22), kind=kOutput, calls=%fused_computation.74 | convolution fusion | flops 404488192 | bytes 3211264 | tf_op jit(solution)/shard_map/qhr,rd->qhd/dot_general | solution.py:117
  91.4 1.0 fusion.87
  92.5 1.3 gather_fusion.6
  93.8 1.3 gather_fusion.4
  95.1 1.3 gather_fusion.7
  97.1 1.3 gather_fusion.2
  98.5 1.3 gather_fusion.3
  100.5 0.8 gather_fusion.1
  101.3 1.1 broadcast_select_fusion.1
  102.4 1.2 fusion.88
  108.7 24.0 %all-gather.2.cloned.1.call-done = bf16[1024,4096]{1,0:T(8,128)(2,1)} async-done(((bf16[1024,128]{1,0:T(8,128)(2,1)}), bf16[1024,4096]{1,0:T(8,128)(2,1)}) %all-gather.2.cloned.1.call-update) | async-done | bytes 8388624 | tf_op jit(solution)/shard_map/all_gather | solution.py:169
  132.7 3.9 %collective-permute-start.11 = (bf16[1024,4096]{1,0:T(8,128)(2,1)}, bf16[1024,4096]{1,0:T(8,128)(2,1)}, u32[]{:S(2)}, u32[]{:S(2)}) collective-permute-start(bf16[1024,4096]{1,0:T(8,128)(2,1)} %all-gather.2.cloned.1.call-done), channel_id=1, source_target_pairs={{0,4},{4,0},{1,5},{5,1},{2,6},{6,2},{3,7},{7,3},{8,12},{12,8},{9,1... | collective-permute-start | bytes 25165832 | tf_op jit(solution)/shard_map/ppermute | solution.py:171
  136.6 1.2 collective-permute-start.8
  137.8 2.5 %collective-permute-start.9 = (bf16[512,1024]{0,1:T(8,128)(2,1)S(1)}, bf16[512,1024]{0,1:T(8,128)(2,1)S(1)}, u32[]{:S(2)}, u32[]{:S(2)}) collective-permute-start(bf16[512,1024]{0,1:T(8,128)(2,1)S(1)} %pad_maximum_fusion.1), channel_id=1, source_target_pairs={{0,2},{1,3},{2,0},{3,1},{4,6},{5,7},{6,4},{7,5},{8,10},{9,11},{10,... | collective-permute-start | bytes 3145736 | tf_op jit(solution)/shard_map/ppermute | solution.py:174
  140.3 1.0 collective-permute-start.10
  141.3 21.2 %collective-permute-done.8 = bf16[512,1024]{0,1:T(8,128)(2,1)S(1)} collective-permute-done((bf16[512,1024]{0,1:T(8,128)(2,1)S(1)}, bf16[512,1024]{0,1:T(8,128)(2,1)S(1)}, u32[]{:S(2)}, u32[]{:S(2)}) %collective-permute-start.8) | collective-permute-done | bytes 1048608 | tf_op jit(solution)/shard_map/ppermute | solution.py:174
  162.5 3.0 %fusion.13 = f32[512,1024]{1,0:T(8,128)S(1)} fusion(bf16[512,1024]{0,1:T(8,128)(2,1)S(1)} %collective-permute-done.8, bf16[1024,4096]{1,0:T(8,128)(2,1)} %all-gather.2.cloned.1.call-done), kind=kOutput, calls=%fused_computation.25 | convolution fusion | flops 1073741824 | bytes 5242880 | tf_op jit(solution)/shard_map/dot_general | solution.py:181
  165.6 20.5 %collective-permute-done.9 = bf16[512,1024]{0,1:T(8,128)(2,1)S(1)} collective-permute-done((bf16[512,1024]{0,1:T(8,128)(2,1)S(1)}, bf16[512,1024]{0,1:T(8,128)(2,1)S(1)}, u32[]{:S(2)}, u32[]{:S(2)}) %collective-permute-start.9) | collective-permute-done | bytes 1048608 | tf_op jit(solution)/shard_map/ppermute | solution.py:174
  186.0 2.9 %fusion.11 = f32[512,1024]{1,0:T(8,128)S(1)} fusion(bf16[512,1024]{0,1:T(8,128)(2,1)S(1)} %collective-permute-done.9, bf16[1024,4096]{1,0:T(8,128)(2,1)} %all-gather.2.cloned.1.call-done), kind=kOutput, calls=%fused_computation.23 | convolution fusion | flops 1073741824 | bytes 5242880 | tf_op jit(solution)/shard_map/dot_general | solution.py:181
  188.9 1.3 fusion.15
  190.2 1.3 add_bitcast_fusion.1
  191.5 2.9 %fusion.3 = f32[512,1024]{1,0:T(8,128)S(1)} fusion(bf16[512,1024]{0,1:T(8,128)(2,1)S(1)} %collective-permute-done.9, bf16[1024,4096]{1,0:T(8,128)(2,1)} %collective-permute-done.11), kind=kOutput, calls=%fused_computation.12 | convolution fusion | flops 1073741824 | bytes 5242880 | tf_op jit(solution)/shard_map/dot_general | solution.py:181
  194.4 2.9 %fusion.5 = f32[512,1024]{1,0:T(8,128)S(1)} fusion(bf16[512,1024]{0,1:T(8,128)(2,1)S(1)} %collective-permute-done.8, bf16[1024,4096]{1,0:T(8,128)(2,1)} %collective-permute-done.11), kind=kOutput, calls=%fused_computation.14 | convolution fusion | flops 1073741824 | bytes 5242880 | tf_op jit(solution)/shard_map/dot_general | solution.py:181
  197.2 2.9 %fusion.7 = f32[512,1024]{1,0:T(8,128)S(1)} fusion(bf16[1024,4096]{1,0:T(8,128)(2,1)} %collective-permute-done.11, bf16[128,1024]{0,1:T(8,128)(2,1)S(1)} %bitcast.143, bf16[128,1024]{0,1:T(8,128)(2,1)S(1)} %bitcast.140, bf16[128,1024]{0,1:T(8,128)(2,1)S(1)} %bitcast.137, bf16[128,1024]{0,1:T(8,128)(2,1)S(1)} %bitcast.146), kind=kOutput, calls=%fused_computation.16 | convolution fusion | flops 1077936128 | bytes 5242880 | tf_op jit(solution)/shard_map/dot_general | solution.py:181
  200.1 2.9 %add_bitcast_fusion = bf16[1,512,1024]{2,1,0:T(8,128)(2,1)S(1)} fusion(f32[512,1024]{1,0:T(8,128)S(1)} %fusion.3, f32[512,1024]{1,0:T(8,128)S(1)} %fusion.7, f32[512,1024]{1,0:T(8,128)S(1)} %fusion.5, bf16[512,1024]{0,1:T(8,128)(2,1)S(1)} %collective-permute-done.10, bf16[1024,4096]{1,0:T(8,128)(2,1)} %collective-permute-done.11), kind=kOutput, calls=%fused_computation.19 | convolution fusion | flops 1075838976 | bytes 10485760 | tf_op jit(solution)/shard_map/dot_general | solution.py:181
  203.6 1.5 pad_maximum_fusion
  (118 shorter events, 16.2 us)
Async XLA Ops:
  6.5 32.6 %copy-start = (bf16[1,128,64]{1,2,0:T(8,128)(2,1)S(1)}, bf16[1,128,64]{1,2,0:T(8,128)(2,1)}, u32[]{:S(2)}) copy-start(bf16[1,128,64]{1,2,0:T(8,128)(2,1)} %param.16) | copy-start | bytes 49156
  6.5 32.6 %copy-start.2 = (bf16[512,1024]{1,0:T(8,128)(2,1)S(1)}, bf16[512,1024]{1,0:T(8,128)(2,1)}, u32[]{:S(2)}) copy-start(bf16[512,1024]{1,0:T(8,128)(2,1)} %param.11) | copy-start | bytes 3145732
  6.5 126.2 %all-gather.2.cloned.1.call-start = ((), (), s32[]{:S(2)}) async-start(), calls=%async_computation | async-start | bytes 8650752 | tf_op jit(solution)/shard_map/all_gather | solution.py:169
  6.5 14.6 %collective-permute-start.7 = (bf16[1024,128]{1,0:T(8,128)(2,1)}, bf16[1024,128]{1,0:T(8,128)(2,1)S(1)}, u32[]{:S(2)}, u32[]{:S(2)}) collective-permute-start(bf16[1024,128]{1,0:T(8,128)(2,1)} %param.19), channel_id=1, source_target_pairs={{0,0},{1,192},{2,128},{3,64},{4,8},{5,200},{6,136},{7,72},{8,16},{... | collective-permute-start | bytes 786440 | tf_op jit(solution)/shard_map/ppermute | solution.py:168
  21.1 0.7 copy-start.12
  24.9 15.4 %collective-permute-start.1 = (f32[65,128]{1,0:T(8,128)S(1)}, f32[65,128]{1,0:T(8,128)S(1)}, u32[]{:S(2)}, u32[]{:S(2)}) collective-permute-start(f32[65,128]{1,0:T(8,128)S(1)} %select_maximum_fusion), channel_id=1, source_target_pairs={{0,4},{4,8},{8,12},{12,16},{16,20},{20,24},{24,28},{28,32},{32,36}... | collective-permute-start | bytes 99848 | tf_op jit(solution)/shard_map/ppermute | solution.py:98
  28.6 62.8 %collective-permute-start = (bf16[512,256]{1,0:T(8,128)(2,1)}, bf16[512,256]{1,0:T(8,128)(2,1)}, u32[]{:S(2)}, u32[]{:S(2)}) collective-permute-start(bf16[512,256]{1,0:T(8,128)(2,1)} %pad_maximum_fusion.2), channel_id=1, source_target_pairs={{0,4},{4,8},{8,12},{12,16},{16,20},{20,24},{24,28},{28,32},{32,36}... | collective-permute-start | bytes 786440 | tf_op jit(solution)/shard_map/ppermute | solution.py:13
  39.7 47.3 %copy-start.11 = (u8[512,64]{0,1:T(8,128)(4,1)}, u8[512,64]{0,1:T(8,128)(4,1)S(1)}, u32[]{:S(2)}) copy-start(u8[512,64]{0,1:T(8,128)(4,1)S(1)} %get-tuple-element.52) | copy-start | bytes 98308
  40.4 6.3 %collective-permute-start.2 = (f32[65,128]{1,0:T(8,128)S(1)}, f32[65,128]{1,0:T(8,128)S(1)}, u32[]{:S(2)}, u32[]{:S(2)}) collective-permute-start(f32[65,128]{1,0:T(8,128)S(1)} %fusion.85), channel_id=1, source_target_pairs={{0,8},{4,12},{8,16},{12,20},{16,24},{20,28},{24,32},{28,36},{32,40... | collective-permute-start | bytes 99848 | tf_op jit(solution)/shard_map/ppermute | solution.py:98
  46.7 6.1 %collective-permute-start.3 = (f32[65,128]{1,0:T(8,128)S(1)}, f32[65,128]{1,0:T(8,128)S(1)}, u32[]{:S(2)}, u32[]{:S(2)}) collective-permute-start(f32[65,128]{1,0:T(8,128)S(1)} %add.278), channel_id=1, source_target_pairs={{0,16},{4,20},{8,24},{12,28},{16,32},{20,36},{24,40},{28,44},{32,4... | collective-permute-start | bytes 99848 | tf_op jit(solution)/shard_map/ppermute | solution.py:98
  52.8 10.8 %collective-permute-start.4 = (f32[65,128]{1,0:T(8,128)S(1)}, f32[65,128]{1,0:T(8,128)S(1)}, u32[]{:S(2)}, u32[]{:S(2)}) collective-permute-start(f32[65,128]{1,0:T(8,128)S(1)} %add.279), channel_id=1, source_target_pairs={{0,32},{4,36},{8,40},{12,44},{16,48},{20,52},{24,56},{28,60},{32,6... | collective-permute-start | bytes 99848 | tf_op jit(solution)/shard_map/ppermute | solution.py:98
  63.6 9.6 %collective-permute-start.5 = (f32[65,128]{1,0:T(8,128)S(1)}, f32[65,128]{1,0:T(8,128)S(1)}, u32[]{:S(2)}, u32[]{:S(2)}) collective-permute-start(f32[65,128]{1,0:T(8,128)S(1)} %add.280), channel_id=1, source_target_pairs={{0,64},{4,68},{8,72},{12,76},{16,80},{20,84},{24,88},{28,92},{32,9... | collective-permute-start | bytes 99848 | tf_op jit(solution)/shard_map/ppermute | solution.py:98
  73.2 9.4 %collective-permute-start.6 = (f32[65,128]{1,0:T(8,128)S(1)}, f32[65,128]{1,0:T(8,128)S(1)}, u32[]{:S(2)}, u32[]{:S(2)}) collective-permute-start(f32[65,128]{1,0:T(8,128)S(1)} %add.281), channel_id=1, source_target_pairs={{0,128},{4,132},{8,136},{12,140},{16,144},{20,148},{24,152},{28,15... | collective-permute-start | bytes 99848 | tf_op jit(solution)/shard_map/ppermute | solution.py:98
  82.6 0.6 copy-start.22
  88.2 4.2 %copy-start.6 = (bf16[512,128]{1,0:T(8,128)(2,1)S(1)}, bf16[512,128]{1,0:T(8,128)(2,1)}, u32[]{:S(2)}) copy-start(bf16[512,128]{1,0:T(8,128)(2,1)} %param.12) | copy-start | bytes 393220
  88.2 6.9 %copy-start.7 = (bf16[512,128]{1,0:T(8,128)(2,1)S(1)}, bf16[512,128]{1,0:T(8,128)(2,1)}, u32[]{:S(2)}) copy-start(bf16[512,128]{1,0:T(8,128)(2,1)} %param.13) | copy-start | bytes 393220
  91.4 11.0 %copy-start.5 = (bf16[128,1024]{0,1:T(8,128)(2,1)S(1)}, bf16[128,1024]{0,1:T(8,128)(2,1)}, u32[]{:S(2)}) copy-start(bf16[128,1024]{0,1:T(8,128)(2,1)} %copy.56) | copy-start | bytes 786436
  100.5 3.4 %copy-start.9 = (bf16[3,128,128]{2,1,0:T(8,128)(2,1)S(1)}, bf16[3,128,128]{2,1,0:T(8,128)(2,1)}, u32[]{:S(2)}) copy-start(bf16[3,128,128]{2,1,0:T(8,128)(2,1)} %gather_fusion.2) | copy-start | bytes 294916
  100.5 3.4 %copy-start.10 = (bf16[3,128,128]{2,1,0:T(8,128)(2,1)S(1)}, bf16[3,128,128]{2,1,0:T(8,128)(2,1)}, u32[]{:S(2)}) copy-start(bf16[3,128,128]{2,1,0:T(8,128)(2,1)} %gather_fusion.3) | copy-start | bytes 294916
  100.5 3.4 %copy-start.25 = (pred[3]{0:T(512)(128)(4,1)S(1)}, pred[3]{0:T(512)(128)(4,1)}, u32[]{:S(2)}) copy-start(pred[3]{0:T(512)(128)(4,1)} %get-tuple-element.18) | copy-start | bytes 13
  101.3 2.7 %copy-start.4 = (bf16[128,1024]{0,1:T(8,128)(2,1)S(1)}, bf16[128,1024]{0,1:T(8,128)(2,1)}, u32[]{:S(2)}) copy-start(bf16[128,1024]{0,1:T(8,128)(2,1)} %copy.54) | copy-start | bytes 786436
  101.3 2.7 %copy-start.21 = (pred[128,384]{0,1:T(8,128)(4,1)S(1)}, pred[128,384]{0,1:T(8,128)(4,1)}, u32[]{:S(2)}) copy-start(pred[128,384]{0,1:T(8,128)(4,1)} %compare_and_fusion.2) | copy-start | bytes 147460
  103.8 0.9 copy-start.8
  103.8 0.9 copy-start.26
  103.9 1.0 copy-start.3
  103.9 1.0 copy-start.20
  104.6 0.9 copy-start.24
  104.7 0.8 copy-start.19
  105.5 0.7 copy-start.23
  107.1 0.9 copy-start.13
  107.5 0.7 copy-start.15
  107.9 0.7 copy-start.17
  132.7 58.8 %collective-permute-start.11 = (bf16[1024,4096]{1,0:T(8,128)(2,1)}, bf16[1024,4096]{1,0:T(8,128)(2,1)}, u32[]{:S(2)}, u32[]{:S(2)}) collective-permute-start(bf16[1024,4096]{1,0:T(8,128)(2,1)} %all-gather.2.cloned.1.call-done), channel_id=1, source_target_pairs={{0,4},{4,0},{1,5},{5,1},{2,6},{6,2},{3,7},{7,3},{8,12},{12,8},{9,1... | collective-permute-start | bytes 25165832 | tf_op jit(solution)/shard_map/ppermute | solution.py:171
  136.6 25.9 %collective-permute-start.8 = (bf16[512,1024]{0,1:T(8,128)(2,1)S(1)}, bf16[512,1024]{0,1:T(8,128)(2,1)S(1)}, u32[]{:S(2)}, u32[]{:S(2)}) collective-permute-start(bf16[512,1024]{0,1:T(8,128)(2,1)S(1)} %pad_maximum_fusion.1), channel_id=1, source_target_pairs={{0,1},{1,2},{2,3},{3,0},{4,5},{5,6},{6,7},{7,4},{8,9},{9,10},{10,1... | collective-permute-start | bytes 3145736 | tf_op jit(solution)/shard_map/ppermute | solution.py:174
  137.8 48.3 %collective-permute-start.9 = (bf16[512,1024]{0,1:T(8,128)(2,1)S(1)}, bf16[512,1024]{0,1:T(8,128)(2,1)S(1)}, u32[]{:S(2)}, u32[]{:S(2)}) collective-permute-start(bf16[512,1024]{0,1:T(8,128)(2,1)S(1)} %pad_maximum_fusion.1), channel_id=1, source_target_pairs={{0,2},{1,3},{2,0},{3,1},{4,6},{5,7},{6,4},{7,5},{8,10},{9,11},{10,... | collective-permute-start | bytes 3145736 | tf_op jit(solution)/shard_map/ppermute | solution.py:174
  140.3 49.9 %collective-permute-start.10 = (bf16[512,1024]{0,1:T(8,128)(2,1)S(1)}, bf16[512,1024]{0,1:T(8,128)(2,1)S(1)}, u32[]{:S(2)}, u32[]{:S(2)}) collective-permute-start(bf16[512,1024]{0,1:T(8,128)(2,1)S(1)} %pad_maximum_fusion.1), channel_id=1, source_target_pairs={{0,3},{1,0},{2,1},{3,2},{4,7},{5,4},{6,5},{7,6},{8,11},{9,8},{10,9... | collective-permute-start | bytes 3145736 | tf_op jit(solution)/shard_map/ppermute | solution.py:174
  162.5 26.4 %copy-start.1 = (bf16[1024,4096]{1,0:T(8,128)(2,1)S(1)}, bf16[1024,4096]{1,0:T(8,128)(2,1)}, u32[]{:S(2)}) copy-start(bf16[1024,4096]{1,0:T(8,128)(2,1)} %all-gather.2.cloned.1.call-done) | copy-start | bytes 25165828
  165.5 23.4 %copy-start.14 = (bf16[128,8,128]{0,2,1:T(8,128)(2,1)S(1)}, bf16[128,8,128]{0,2,1:T(8,128)(2,1)}, u32[]{:S(2)}) copy-start(bf16[128,8,128]{0,2,1:T(8,128)(2,1)} %copy-done.13) | copy-start | bytes 786436
  165.5 23.4 %copy-start.16 = (bf16[128,8,128]{0,2,1:T(8,128)(2,1)S(1)}, bf16[128,8,128]{0,2,1:T(8,128)(2,1)}, u32[]{:S(2)}) copy-start(bf16[128,8,128]{0,2,1:T(8,128)(2,1)} %copy-done.15) | copy-start | bytes 786436
  165.5 23.4 %copy-start.18 = (bf16[128,8,128]{0,2,1:T(8,128)(2,1)S(1)}, bf16[128,8,128]{0,2,1:T(8,128)(2,1)}, u32[]{:S(2)}) copy-start(bf16[128,8,128]{0,2,1:T(8,128)(2,1)} %copy-done.17) | copy-start | bytes 786436
Sparse Core Ops, SparseCore 0:
  22.0 110.7 all-gather.1

commit v3 on v1

--- a/solution.py
+++ b/solution.py
@@ -87,9 +87,15 @@
     norm_terms = [jnp.sum(key_feats, axis=0)]
     totals = jnp.stack(state_terms)
     counts = jnp.stack(norm_terms)
-    states, norms = carried_in(
-        (totals, counts), CTX, add_pair, (jnp.zeros_like(totals), jnp.zeros_like(counts))
+    packed = jnp.concatenate(
+        [totals[0], jnp.pad(counts, ((0, 0), (0, totals.shape[2] - counts.shape[1])))], axis=0
     )
+    every_state = lax.all_gather(packed.astype(jnp.float32), CTX, axis=0)
+    earlier = jnp.arange(every_state.shape[0], dtype=jnp.int32) < device
+    before = jnp.sum(jnp.where(earlier[:, None, None], every_state, 0.0), axis=0)
+    states = before[None, : totals.shape[1]]
+    norms = before[None, totals.shape[1], : counts.shape[1]]
+    out_weight, _ = lax.optimization_barrier((out_weight, packed))
     scale = head_dim ** (-0.5)
     offsets = jnp.arange(block_rows, dtype=jnp.int32)
     group = 0
@@ -139,22 +145,28 @@
         for rows in range(n_tp)
     ]
     moved = lax.ppermute(out_weight, ("ctx_0", "tp"), swap)
-    gathered = lax.all_gather(moved, CTX, axis=1, tiled=True)
-    width = gathered.shape[1] // n_tp
+    depth = moved.shape[0]
+    halves = 2
+    step = depth // halves
+    rows_by_shift = [group_cols] + [
+        lax.ppermute(group_cols, "tp", [(i, (i + shift) % n_tp) for i in range(n_tp)])
+        for shift in range(1, n_tp)
+    ]
     summed = None
-    for shift in range(n_tp):
-        if shift == 0:
-            rows_in = group_cols
-        else:
-            rows_in = lax.ppermute(
-                group_cols, "tp", [(i, (i + shift) % n_tp) for i in range(n_tp)]
+    for half in range(halves):
+        gathered = lax.all_gather(
+            moved[half * step : (half + 1) * step], CTX, axis=1, tiled=True
+        )
+        if summed is not None:
+            gathered, summed = lax.optimization_barrier((gathered, summed))
+        width = gathered.shape[1] // n_tp
+        for shift in range(n_tp):
+            term = jnp.dot(
+                rows_by_shift[shift][:, half * step : (half + 1) * step],
+                gathered[:, shift * width : (shift + 1) * width],
+                preferred_element_type=jnp.float32,
             )
-        term = jnp.dot(
-            rows_in,
-            gathered[:, shift * width : (shift + 1) * width],
-            preferred_element_type=jnp.float32,
-        )
-        summed = term if summed is None else summed + term
+            summed = term if summed is None else summed + term
     return summed.astype(jnp.bfloat16)
 
 

time: 173 us -> 285 us (1.65)
  the two profiles are of different devices: /device:TPU:8 before, /device:TPU:1 now
where the time goes in v3:
time: 285 us
  waiting for transfers between devices  193 us (68%)
  matrix products  36.6 us (13%)
  other arithmetic  15.6 us (5%)
  between operations  14.4 us (5%)
  local copies, waits for them, and re-layouts  13.7 us (5%)
  starting transfers between devices  11.4 us (4%)
    all_gather x2, waiting for transfers between devices, body(): lax.all_gather(moved[half * step:(half + 1) * step], CTX, axis=1, tiled=T...  144 us
    all_gather x1, waiting for transfers between devices, body(): every_state = lax.all_gather(packed.astype(jnp.float32), CTX, axis=0)  48.5 us
    dot_general x8, matrix products, body(): jnp.dot(rows_by_shift[shift][:, half * step:(half + 1) * step], gathered[...  23.5 us
  transfers between devices with their start and end apart: 8, of which 3 were waited for; matrix products, arithmetic and copies ran while one was open for 16% of the time, Pallas kernels for 0%

profile of v3, /device:TPU:1, one launch (start us, length us, event | category | flops | bytes accessed | tf_op | source)
XLA Modules:
  0.0 284.6 jit_solution(9354290622231265482)
XLA Ops:
  6.5 0.8 convert_element_type.45
  7.3 1.2 fusion.75
  8.5 1.2 fusion.76
  10.4 1.6 collective-permute-start
  12.0 0.7 fusion.99
  12.8 0.7 all-gather.6.cloned.1.call-update
  13.5 1.7 pad_maximum_fusion.1
  15.2 4.9 %collective-permute-start.1 = (bf16[512,256]{1,0:T(8,128)(2,1)}, bf16[512,256]{1,0:T(8,128)(2,1)}, u32[]{:S(2)}, u32[]{:S(2)}) collective-permute-start(bf16[512,256]{1,0:T(8,128)(2,1)} %pad_maximum_fusion.1), channel_id=1, source_target_pairs={{0,4},{4,8},{8,12},{12,16},{16,20},{20,24},{24,28},{28,32},{32,36}... | collective-permute-start | bytes 786440 | tf_op jit(solution)/shard_map/ppermute | solution.py:13
  22.6 0.7 compare_and_fusion.6
  23.2 0.7 compare_and_fusion.4
  26.9 0.8 compare_and_fusion.2
  27.7 0.8 compare_and_fusion.1
  29.3 1.0 fusion.98
  30.4 0.7 gather_fusion.2
  31.1 0.7 gather_fusion.3
  31.8 0.7 gather_fusion.4
  32.5 0.7 gather_fusion.5
  33.2 0.7 gather_fusion
  33.9 0.7 gather_fusion.1
  34.6 0.7 gather_fusion.6
  35.3 0.7 gather_fusion.7
  36.0 0.7 broadcast_select_fusion.5
  36.7 1.2 fusion.103
  37.9 1.0 fusion.22
  39.7 0.9 broadcast_select_fusion.7
  41.3 0.8 copy-done.11
  42.5 1.1 copy-done.9
  43.9 48.5 %all-gather.10.cloned.1.call-done = f32[64,65,128]{2,1,0:T(8,128)} async-done(((f32[1,65,128]{2,1,0:T(8,128)}), f32[64,65,128]{2,1,0:T(8,128)}) %all-gather.10.cloned.1.call-update) | async-done | bytes 2129936 | tf_op jit(solution)/shard_map/all_gather | solution.py:93
  92.4 1.9 select_reduce_fusion
  94.3 3.7 %fusion.51 = f32[1,512,8]{0,1,2:T(8,128)S(1)} fusion(f32[512,8,64]{0,2,1:T(8,128)S(1)} %get-tuple-element.57, u8[512,64]{0,1:T(8,128)(4,1)S(1)} %get-tuple-element.56, f32[65,128]{1,0:T(8,128)S(1)} %select_reduce_fusion), kind=kOutput, calls=%fused_computation.69 | convolution fusion | flops 4980736 | bytes 1098240 | tf_op jit(solution)/shard_map/qhr,r->qh/dot_general | solution.py:111
  98.0 0.6 copy.56
  98.7 2.4 fusion.53
  101.5 0.9 copy-done.6
  103.5 0.9 copy-done.10
  105.1 1.2 collective-permute-start.2
  106.3 2.4 collective-permute-start.3
  108.7 1.2 collective-permute-start.4
  109.9 67.6 %all-gather.8.cloned.1.call-done = bf16[512,8192]{1,0:T(8,128)(2,1)} async-done(((bf16[512,128]{1,0:T(8,128)(2,1)}), bf16[512,8192]{1,0:T(8,128)(2,1)}) %all-gather.8.cloned.1.call-update) | async-done | bytes 8388624 | tf_op jit(solution)/shard_map/all_gather | solution.py:157
  177.5 3.0 %fusion.8 = f32[512,2048]{1,0:T(8,128)S(1)} fusion(bf16[512,8192]{1,0:T(8,128)(2,1)} %all-gather.8.cloned.1.call-done, bf16[512,1024]{0,1:T(8,128)(2,1)S(1)} %pad_maximum_fusion), kind=kOutput, calls=%fused_computation.17 | convolution fusion | flops 1073741824 | bytes 6815744 | tf_op jit(solution)/shard_map/dot_general | solution.py:164
  180.6 2.9 %fusion.6 = f32[512,2048]{1,0:T(8,128)S(1)} fusion(bf16[512,8192]{1,0:T(8,128)(2,1)} %all-gather.8.cloned.1.call-done, bf16[512,1024]{0,1:T(8,128)(2,1)S(1)} %collective-permute-done.2), kind=kOutput, calls=%fused_computation.15 | convolution fusion | flops 1073741824 | bytes 6815744 | tf_op jit(solution)/shard_map/dot_general | solution.py:164
  183.5 1.3 fusion.4
  184.8 4.7 %add_add_fusion = f32[512,2048]{1,0:T(8,128)} fusion(f32[512,2048]{1,0:T(8,128)S(1)} %fusion.4, f32[512,2048]{1,0:T(8,128)S(1)} %fusion.8, f32[512,2048]{1,0:T(8,128)S(1)} %fusion.6, bf16[512,8192]{1,0:T(8,128)(2,1)S(1)} %copy-done.3, bf16[512,1024]{0,1:T(8,128)(2,1)} %collective-permute-done.4), kind=kOutput, calls=%fused_computation.9 | convolution fusion | flops 1076887552 | bytes 19398656 | tf_op jit(solution)/shard_map/dot_general | solution.py:164
  189.4 76.1 %all-gather.6.cloned.1.call-done = bf16[512,8192]{1,0:T(8,128)(2,1)} async-done(((bf16[512,128]{1,0:T(8,128)(2,1)}), bf16[512,8192]{1,0:T(8,128)(2,1)}) %all-gather.6.cloned.1.call-update) | async-done | bytes 8388624 | tf_op jit(solution)/shard_map/all_gather | solution.py:157
  265.5 3.0 %fusion.18 = f32[512,2048]{1,0:T(8,128)S(1)} fusion(bf16[512,8192]{1,0:T(8,128)(2,1)} %all-gather.6.cloned.1.call-done, bf16[512,1024]{0,1:T(8,128)(2,1)S(1)} %pad_maximum_fusion), kind=kOutput, calls=%fused_computation.25 | convolution fusion | flops 1073741824 | bytes 6815744 | tf_op jit(solution)/shard_map/dot_general | solution.py:164
  268.5 2.9 %fusion.16 = f32[512,2048]{1,0:T(8,128)S(1)} fusion(bf16[512,8192]{1,0:T(8,128)(2,1)} %all-gather.6.cloned.1.call-done, bf16[512,1024]{0,1:T(8,128)(2,1)S(1)} %collective-permute-done.2), kind=kOutput, calls=%fused_computation.23 | convolution fusion | flops 1073741824 | bytes 6815744 | tf_op jit(solution)/shard_map/dot_general | solution.py:164
  271.4 1.3 fusion.14
  272.7 0.9 copy-done.2
  273.6 4.5 %add_convert_fusion = bf16[512,2048]{1,0:T(8,128)(2,1)} fusion(f32[512,2048]{1,0:T(8,128)S(1)} %fusion.14, f32[512,2048]{1,0:T(8,128)S(1)} %fusion.16, f32[512,2048]{1,0:T(8,128)S(1)} %copy-done.2, f32[512,2048]{1,0:T(8,128)S(1)} %fusion.18, bf16[512,8192]{1,0:T(8,128)(2,1)S(1)} %copy-done.4, bf16[512,1024]{0,1:T(8,128)(2,1)} %collective-permute-done.4), kind=kOutput, calls=%fused_computation.8 | convolution fusion | flops 1078984704 | bytes 21495808 | tf_op jit(solution)/shard_map/dot_general | solution.py:164
  (102 shorter events, 10.4 us)
Async XLA Ops:
  6.5 22.2 %copy-start = (bf16[1,128,64]{1,2,0:T(8,128)(2,1)S(1)}, bf16[1,128,64]{1,2,0:T(8,128)(2,1)}, u32[]{:S(2)}) copy-start(bf16[1,128,64]{1,2,0:T(8,128)(2,1)} %param.16) | copy-start | bytes 49156
  6.5 13.6 %copy-start.13 = (bf16[512,1024]{1,0:T(8,128)(2,1)S(1)}, bf16[512,1024]{1,0:T(8,128)(2,1)}, u32[]{:S(2)}) copy-start(bf16[512,1024]{1,0:T(8,128)(2,1)} %param.11) | copy-start | bytes 3145732
  6.5 85.8 %all-gather.10.cloned.1.call-start = ((), (), s32[]{:S(2)}) async-start(), calls=%async_computation.2 | async-start | bytes 2396160 | tf_op jit(solution)/shard_map/all_gather | solution.py:93
  10.3 167.2 %all-gather.8.cloned.1.call-start = ((), (), s32[]{:S(2)}) async-start(), calls=%async_computation.1 | async-start | bytes 8519680 | tf_op jit(solution)/shard_map/all_gather | solution.py:157
  10.4 1.6 collective-permute-start
  12.8 252.7 %all-gather.6.cloned.1.call-start = ((), (), s32[]{:S(2)}) async-start(), calls=%async_computation | async-start | bytes 8519680 | tf_op jit(solution)/shard_map/all_gather | solution.py:157
  15.2 14.1 %collective-permute-start.1 = (bf16[512,256]{1,0:T(8,128)(2,1)}, bf16[512,256]{1,0:T(8,128)(2,1)}, u32[]{:S(2)}, u32[]{:S(2)}) collective-permute-start(bf16[512,256]{1,0:T(8,128)(2,1)} %pad_maximum_fusion.1), channel_id=1, source_target_pairs={{0,4},{4,8},{8,12},{12,16},{16,20},{20,24},{24,28},{28,32},{32,36}... | collective-permute-start | bytes 786440 | tf_op jit(solution)/shard_map/ppermute | solution.py:13
  20.2 2.0 copy-start.20
  20.6 9.7 %copy-start.14 = (bf16[512,128]{1,0:T(8,128)(2,1)S(1)}, bf16[512,128]{1,0:T(8,128)(2,1)}, u32[]{:S(2)}) copy-start(bf16[512,128]{1,0:T(8,128)(2,1)} %param.12) | copy-start | bytes 393220
  20.8 10.3 %copy-start.15 = (bf16[512,128]{1,0:T(8,128)(2,1)S(1)}, bf16[512,128]{1,0:T(8,128)(2,1)}, u32[]{:S(2)}) copy-start(bf16[512,128]{1,0:T(8,128)(2,1)} %param.13) | copy-start | bytes 393220
  29.3 6.7 %copy-start.24 = (pred[3]{0:T(512)(128)(4,1)S(1)}, pred[3]{0:T(512)(128)(4,1)}, u32[]{:S(2)}) copy-start(pred[3]{0:T(512)(128)(4,1)} %get-tuple-element.22) | copy-start | bytes 13
  35.3 3.7 %copy-start.23 = (pred[3]{0:T(512)(128)(4,1)S(1)}, pred[3]{0:T(512)(128)(4,1)}, u32[]{:S(2)}) copy-start(pred[3]{0:T(512)(128)(4,1)} %get-tuple-element.66) | copy-start | bytes 13
  36.0 3.1 %copy-start.16 = (pred[128,384]{0,1:T(8,128)(4,1)S(1)}, pred[128,384]{0,1:T(8,128)(4,1)}, u32[]{:S(2)}) copy-start(pred[128,384]{0,1:T(8,128)(4,1)} %compare_and_fusion.1) | copy-start | bytes 147460
  37.9 1.8 copy-start.5
  38.9 0.7 copy-start.22
  39.4 1.8 copy-start.7
  39.7 1.6 copy-start.21
  41.0 1.2 copy-start.11
  41.2 51.2 %copy-start.25 = (pred[64]{0:T(512)(128)(4,1)S(1)}, pred[64]{0:T(512)(128)(4,1)}, u32[]{:S(2)}) copy-start(pred[64]{0:T(512)(128)(4,1)} %iota_compare_fusion.1) | copy-start | bytes 196
  42.5 1.1 copy-start.9
  94.3 4.4 %copy-start.19 = (f32[128,8]{0,1:T(8,128)S(1)}, f32[128,8]{0,1:T(8,128)}, u32[]{:S(2)}) copy-start(f32[128,8]{0,1:T(8,128)} %fusion.22) | copy-start | bytes 12292
  98.6 2.4 copy-start.12
  98.6 2.4 copy-start.18
  101.0 1.4 copy-start.6
  101.1 1.4 copy-start.17
  101.5 1.6 copy-start.8
  102.9 1.5 copy-start.10
  105.1 75.5 %collective-permute-start.2 = (bf16[512,1024]{0,1:T(8,128)(2,1)S(1)}, bf16[512,1024]{0,1:T(8,128)(2,1)S(1)}, u32[]{:S(2)}, u32[]{:S(2)}) collective-permute-start(bf16[512,1024]{0,1:T(8,128)(2,1)S(1)} %pad_maximum_fusion), channel_id=1, source_target_pairs={{0,1},{1,2},{2,3},{3,0},{4,5},{5,6},{6,7},{7,4},{8,9},{9,10},{10,1... | collective-permute-start | bytes 3145736 | tf_op jit(solution)/shard_map/ppermute | solution.py:152
  106.3 77.1 %collective-permute-start.3 = (bf16[512,1024]{0,1:T(8,128)(2,1)S(1)}, bf16[512,1024]{0,1:T(8,128)(2,1)S(1)}, u32[]{:S(2)}, u32[]{:S(2)}) collective-permute-start(bf16[512,1024]{0,1:T(8,128)(2,1)S(1)} %pad_maximum_fusion), channel_id=1, source_target_pairs={{0,2},{1,3},{2,0},{3,1},{4,6},{5,7},{6,4},{7,5},{8,10},{9,11},{10,... | collective-permute-start | bytes 3145736 | tf_op jit(solution)/shard_map/ppermute | solution.py:152
  108.7 76.0 %collective-permute-start.4 = (bf16[512,1024]{0,1:T(8,128)(2,1)S(1)}, bf16[512,1024]{0,1:T(8,128)(2,1)}, u32[]{:S(2)}, u32[]{:S(2)}) collective-permute-start(bf16[512,1024]{0,1:T(8,128)(2,1)S(1)} %pad_maximum_fusion), channel_id=1, source_target_pairs={{0,3},{1,0},{2,1},{3,2},{4,7},{5,4},{6,5},{7,6},{8,11},{9,8},{10,9... | collective-permute-start | bytes 3145736 | tf_op jit(solution)/shard_map/ppermute | solution.py:152
  177.5 5.9 %copy-start.3 = (bf16[512,8192]{1,0:T(8,128)(2,1)S(1)}, bf16[512,8192]{1,0:T(8,128)(2,1)}, u32[]{:S(2)}) copy-start(bf16[512,8192]{1,0:T(8,128)(2,1)} %all-gather.8.cloned.1.call-done) | copy-start | bytes 25165828
  265.5 5.9 %copy-start.4 = (bf16[512,8192]{1,0:T(8,128)(2,1)S(1)}, bf16[512,8192]{1,0:T(8,128)(2,1)}, u32[]{:S(2)}) copy-start(bf16[512,8192]{1,0:T(8,128)(2,1)} %all-gather.6.cloned.1.call-done) | copy-start | bytes 25165828
  271.4 2.2 copy-start.2
  273.6 4.5 %copy-start.1 = (bf16[1,128,64]{1,2,0:T(8,128)(2,1)S(1)}, bf16[1,128,64]{1,2,0:T(8,128)(2,1)}, u32[]{:S(2)}) copy-start(bf16[1,128,64]{1,2,0:T(8,128)(2,1)} %param.16) | copy-start | bytes 49156
Sparse Core Ops, SparseCore 0:
  10.5 81.8 all-gather.9
  94.9 82.5 all-gather.7
  180.1 85.3 all-gather.5

commit v4 on v1

--- a/solution.py
+++ b/solution.py
@@ -141,20 +141,17 @@
     moved = lax.ppermute(out_weight, ("ctx_0", "tp"), swap)
     gathered = lax.all_gather(moved, CTX, axis=1, tiled=True)
     width = gathered.shape[1] // n_tp
-    summed = None
-    for shift in range(n_tp):
-        if shift == 0:
-            rows_in = group_cols
-        else:
-            rows_in = lax.ppermute(
-                group_cols, "tp", [(i, (i + shift) % n_tp) for i in range(n_tp)]
-            )
-        term = jnp.dot(
-            rows_in,
-            gathered[:, shift * width : (shift + 1) * width],
-            preferred_element_type=jnp.float32,
-        )
-        summed = term if summed is None else summed + term
+    rows_by_shift = [group_cols] + [
+        lax.ppermute(group_cols, "tp", [(i, (i + shift) % n_tp) for i in range(n_tp)])
+        for shift in range(1, n_tp)
+    ]
+    every_group = jnp.stack(rows_by_shift, axis=1)
+    summed = jnp.einsum(
+        "tsk,ksn->tn",
+        every_group,
+        gathered.reshape(gathered.shape[0], n_tp, width),
+        preferred_element_type=jnp.float32,
+    )
     return summed.astype(jnp.bfloat16)
 
 

time: 173 us -> 189 us (1.092)
  the two profiles are of different devices: /device:TPU:8 before, /device:TPU:1 now
where the time goes in v4:
time: 189 us; the launch traced here: 187 us
  blocking collectives  49.4 us (26%)
  waiting for transfers between devices  43.4 us (23%)
  matrix products  33.5 us (18%)
  local copies, waits for them, and re-layouts  18.8 us (10%)
  other arithmetic  15.7 us (8%)
  between operations  14.6 us (8%)
  starting transfers between devices  11.9 us (6%)
    all_gather x3, blocking collectives, all_in_one(): both, at, found = (lax.all_gather(jnp.concatenate(lines), axis), 0, {})  49.4 us
    ppermute x3, waiting for transfers between devices, body(): lax.ppermute(group_cols, 'tp', [(i, (i + shift) % n_tp) for i in range(n_...  43.4 us
    dot_general x1, matrix products, body(): jnp.einsum('tsk,ksn->tn', every_group, gathered.reshape(gathered.shape[0]...  13.6 us
    dot_general x4, matrix products, body(): jnp.einsum('qhk,kd->qhd', probs, value_rows, preferred_element_type=jnp.f...  8.16 us
    ppermute x3, starting transfers between devices, body(): lax.ppermute(group_cols, 'tp', [(i, (i + shift) % n_tp) for i in range(n_...  6.24 us
    ppermute x1, starting transfers between devices, passed_along(): return lax.ppermute(block, axis, route)  4.91 us
    unnamed x66, local copies, waits for them, and re-layouts  4.82 us
    dot_general x1, matrix products, body(): jnp.einsum('qhr,rd->qhd', query_feats, states[group], precision=highest)  4.5 us
  transfers between devices with their start and end apart: 6, of which 3 were waited for; matrix products, arithmetic and copies ran while one was open for 28% of the time, Pallas kernels for 0%

profile of v4, /device:TPU:1, one launch (start us, length us, event | category | flops | bytes accessed | tf_op | source)
XLA Modules:
  0.0 187.4 jit_solution(5050854078151889543)
XLA Ops:
  6.6 1.2 copy.125
  7.8 0.7 collective-permute-start.4
  8.5 0.7 copy-done.12
  9.2 1.7 pad_maximum_fusion.1
  10.9 4.9 %collective-permute-start = (bf16[512,256]{1,0:T(8,128)(2,1)}, bf16[512,256]{1,0:T(8,128)(2,1)}, u32[]{:S(2)}, u32[]{:S(2)}) collective-permute-start(bf16[512,256]{1,0:T(8,128)(2,1)} %pad_maximum_fusion.1), channel_id=1, source_target_pairs={{0,4},{4,8},{8,12},{12,16},{16,20},{20,24},{24,28},{28,32},{32,36}... | collective-permute-start | bytes 786440 | tf_op jit(solution)/shard_map/ppermute | solution.py:13
  15.9 0.7 convert_element_type.238
  16.5 1.2 fusion.57
  18.1 1.8 all-gather.3
  20.0 35.5 %all-gather.4 = bf16[8,65,128]{2,1,0:T(8,128)(2,1)S(1)} all-gather(bf16[1,65,128]{2,1,0:T(8,128)(2,1)S(1)} %maximum_bitcast_fusion.1), channel_id=3, replica_groups=mesh['ctx_0'=4,'ctx_1'=8,'ctx_2'=2,'tp'=4] {'ctx_1'}, dimensions={0}, use_global_device_ids=true | all-gather | bytes 149760 | tf_op jit(solution)/shard_map/all_gather | solution.py:30
  55.5 12.1 %all-gather.5 = bf16[4,65,128]{2,1,0:T(8,128)(2,1)S(1)} all-gather(bf16[1,65,128]{2,1,0:T(8,128)(2,1)S(1)} %maximum_bitcast_fusion.2), channel_id=4, replica_groups=mesh['ctx_0'=4,'ctx_1'=8,'ctx_2'=2,'tp'=4] {'ctx_0'}, dimensions={0}, use_global_device_ids=true | all-gather | bytes 83200 | tf_op jit(solution)/shard_map/all_gather | solution.py:30
  68.1 0.7 compare_and_fusion.6
  71.9 0.6 broadcast_compare_fusion
  73.4 0.8 compare_and_fusion.2
  74.2 0.8 compare_and_fusion.1
  75.0 0.8 compare_and_fusion.3
  76.4 3.7 %fusion.41 = f32[1,512,8]{0,1,2:T(8,128)S(1)} fusion(f32[512,8,64]{0,2,1:T(8,128)S(1)} %get-tuple-element.54, u8[512,64]{0,1:T(8,128)(4,1)S(1)} %get-tuple-element.53, pred[]{:T(512)S(6)} %gt.55, pred[]{:T(512)S(6)} %gt.57, pred[]{:T(512)S(6)} %gt.58, pred[]{:T(512)S(6)} %gt.59, f32[1,64]{1,0:T(1,128)S(1)} %get-tuple-element.25, pred[]{:T(512)S(6)} %gt.60, ...), kind=kOutput, calls=%fused_computation.60 | convolution fusion | flops 4983104 | bytes 1104910 | tf_op jit(solution)/shard_map/qhr,r->qh/dot_general | solution.py:105
  80.1 4.5 %fusion.43 = f32[512,8,128]{0,2,1:T(8,128)} fusion(f32[512,8,64]{0,2,1:T(8,128)S(1)} %get-tuple-element.54, u8[512,64]{0,1:T(8,128)(4,1)S(1)} %get-tuple-element.53, bf16[4,65,128]{2,1,0:T(8,128)(2,1)} %copy-done.17, pred[]{:T(512)S(6)} %gt.69, pred[]{:T(512)S(6)} %gt.68, pred[]{:T(512)S(6)} %gt.67, pred[]{:T(512)S(6)} %gt.66, pred[]{:T(512)S(6)} %gt.65, ...), kind=kOutput, calls=%fused_computation.61 | convolution fusion | flops 404824064 | bytes 3407886 | tf_op jit(solution)/shard_map/qhr,rd->qhd/dot_general | solution.py:104
  85.3 0.9 copy.150
  86.2 0.8 copy.148
  87.2 1.2 copy.130
  89.1 0.8 compare_and_fusion
  89.9 1.0 fusion.156
  90.9 0.7 gather_fusion.2
  91.7 0.7 gather_fusion.3
  92.3 0.7 gather_fusion.4
  93.0 0.7 gather_fusion.5
  93.7 1.3 gather_fusion
  95.0 1.3 gather_fusion.1
  96.4 0.7 gather_fusion.6
  97.0 1.3 gather_fusion.7
  98.4 0.7 broadcast_select_fusion.5
  99.7 0.7 broadcast_select_fusion.3
  102.4 0.7 broadcast_select_fusion.1
  103.9 0.8 fusion.123
  104.7 2.2 %fusion.22 = bf16[128,8,128]{0,2,1:T(8,128)(2,1)} fusion(bf16[384,128,1]{1,0,2:T(8,128)(2,1)S(1)} %bitcast.166, f32[128,8,384]{0,2,1:T(8,128)S(1)} %get-tuple-element.58, f32[128,8]{0,1:T(8,128)S(1)} %get-tuple-element.57, f32[512,8,128]{0,2,1:T(8,128)} %fusion.43, f32[128,8]{0,1:T(8,128)S(1)} %get-tuple-element.10, f32[128,8]{0,1:T(8,128)S(1)} %get-tuple-element.11), kind=kOutput, calls=%fused_computation.41 | convolution fusion | flops 101974016 | bytes 2469888 | tf_op jit(solution)/shard_map/qhk,kd->qhd/dot_general | solution.py:128
  106.9 1.1 copy.121
  108.0 2.2 %fusion.23 = bf16[128,8,128]{0,2,1:T(8,128)(2,1)} fusion(bf16[384,128,1]{1,0,2:T(8,128)(2,1)S(1)} %bitcast.163, f32[128,8,384]{0,2,1:T(8,128)S(1)} %get-tuple-element.62, f32[128,8]{0,1:T(8,128)S(1)} %get-tuple-element.61, f32[512,8,128]{0,2,1:T(8,128)} %fusion.43, f32[128,8]{0,1:T(8,128)S(1)} %get-tuple-element.41, f32[128,8]{0,1:T(8,128)} %get-tuple-element.42), kind=kOutput, calls=%fused_computation.42 | convolution fusion | flops 101974016 | bytes 2469888 | tf_op jit(solution)/shard_map/qhk,kd->qhd/dot_general | solution.py:128
  110.2 1.8 copy.122
  112.0 2.3 %fusion.24 = bf16[128,8,128]{0,2,1:T(8,128)(2,1)} fusion(bf16[384,128,1]{1,0,2:T(8,128)(2,1)} %bitcast.164, f32[128,8,384]{0,2,1:T(8,128)S(1)} %get-tuple-element.60, f32[128,8]{0,1:T(8,128)S(1)} %get-tuple-element.59, f32[512,8,128]{0,2,1:T(8,128)} %fusion.43, f32[128,8]{0,1:T(8,128)S(1)} %get-tuple-element.39, f32[128,8]{0,1:T(8,128)S(1)} %get-tuple-element.40), kind=kOutput, calls=%fused_computation.43 | convolution fusion | flops 101974016 | bytes 2469888 | tf_op jit(solution)/shard_map/qhk,kd->qhd/dot_general | solution.py:128
  114.3 1.1 copy.123
  115.4 1.5 fusion.25
  117.2 3.7 %collective-permute-start.1 = (bf16[512,1024]{1,0:T(8,128)(2,1)S(1)}, bf16[512,1024]{1,0:T(8,128)(2,1)S(1)}, u32[]{:S(2)}, u32[]{:S(2)}) collective-permute-start(bf16[512,1024]{1,0:T(8,128)(2,1)S(1)} %get-tuple-element.30), channel_id=1, source_target_pairs={{0,1},{1,2},{2,3},{3,0},{4,5},{5,6},{6,7},{7,4},{8,9},{9,10},{10,1... | collective-permute-start | bytes 3145736 | tf_op jit(solution)/shard_map/ppermute | solution.py:145
  121.0 1.3 collective-permute-start.2
  122.3 1.2 collective-permute-start.3
  123.5 14.6 %collective-permute-done.1 = bf16[512,1024]{1,0:T(8,128)(2,1)S(1)} collective-permute-done((bf16[512,1024]{1,0:T(8,128)(2,1)S(1)}, bf16[512,1024]{1,0:T(8,128)(2,1)S(1)}, u32[]{:S(2)}, u32[]{:S(2)}) %collective-permute-start.1) | collective-permute-done | bytes 1048608 | tf_op jit(solution)/shard_map/ppermute | solution.py:145
  138.1 23.4 %collective-permute-done.2 = bf16[512,1024]{1,0:T(8,128)(2,1)S(1)} collective-permute-done((bf16[512,1024]{1,0:T(8,128)(2,1)S(1)}, bf16[512,1024]{1,0:T(8,128)(2,1)S(1)}, u32[]{:S(2)}, u32[]{:S(2)}) %collective-permute-start.2) | collective-permute-done | bytes 1048608 | tf_op jit(solution)/shard_map/ppermute | solution.py:145
  161.5 5.4 %collective-permute-done.3 = bf16[512,1024]{1,0:T(8,128)(2,1)} collective-permute-done((bf16[512,1024]{1,0:T(8,128)(2,1)S(1)}, bf16[512,1024]{1,0:T(8,128)(2,1)}, u32[]{:S(2)}, u32[]{:S(2)}) %collective-permute-start.3) | collective-permute-done | bytes 1048608 | tf_op jit(solution)/shard_map/ppermute | solution.py:145
  166.9 13.6 %bitcast_convert_fusion = bf16[512,2048]{1,0:T(8,128)(2,1)} fusion(bf16[1024,4,2048]{0,2,1:T(8,128)(2,1)} %bitcast.175, bf16[512,1,1024]{2,0,1:T(8,128)(2,1)} %bitcast.58, bf16[512,1,1024]{2,0,1:T(8,128)(2,1)S(1)} %bitcast.177, bf16[512,1,1024]{2,0,1:T(8,128)(2,1)S(1)} %bitcast.176, bf16[512,1,1024]{2,0,1:T(8,128)(2,1)S(1)} %get-tuple-element.29), kind=kOutput, calls=%fused_computation.16 | convolution fusion | flops 8597274624 | bytes 23068672 | tf_op jit(solution)/shard_map/tsk,ksn->tn/dot_general | solution.py:149
  (115 shorter events, 9.9 us)
Async XLA Ops:
  6.5 69.3 %copy-start = (bf16[1,128,64]{1,2,0:T(8,128)(2,1)S(1)}, bf16[1,128,64]{1,2,0:T(8,128)(2,1)}, u32[]{:S(2)}) copy-start(bf16[1,128,64]{1,2,0:T(8,128)(2,1)} %param.16) | copy-start | bytes 49156
  6.5 11.2 %copy-start.8 = (bf16[512,128]{1,0:T(8,128)(2,1)S(1)}, bf16[512,128]{1,0:T(8,128)(2,1)}, u32[]{:S(2)}) copy-start(bf16[512,128]{1,0:T(8,128)(2,1)} %param.13) | copy-start | bytes 393220
  6.5 61.2 %copy-start.21 = (s32[4,2]{0,1:T(2,128)S(1)}, s32[4,2]{0,1:T(2,128)}, u32[]{:S(2)}) copy-start(s32[4,2]{0,1:T(2,128)} %param.15) | copy-start | bytes 100
  6.5 69.2 %copy-start.3 = (bf16[512,1024]{1,0:T(8,128)(2,1)S(1)}, bf16[512,1024]{1,0:T(8,128)(2,1)}, u32[]{:S(2)}) copy-start(bf16[512,1024]{1,0:T(8,128)(2,1)} %param.11) | copy-start | bytes 3145732
  6.5 160.3 %all-gather.8.cloned.1.call-start = ((), (), s32[]{:S(2)}) async-start(), calls=%async_computation | async-start | bytes 17039360 | tf_op jit(solution)/shard_map/all_gather | solution.py:142
  7.8 0.7 collective-permute-start.4
  8.5 0.7 copy-start.12
  10.9 79.0 %collective-permute-start = (bf16[512,256]{1,0:T(8,128)(2,1)}, bf16[512,256]{1,0:T(8,128)(2,1)}, u32[]{:S(2)}, u32[]{:S(2)}) collective-permute-start(bf16[512,256]{1,0:T(8,128)(2,1)} %pad_maximum_fusion.1), channel_id=1, source_target_pairs={{0,4},{4,8},{8,12},{12,16},{16,20},{20,24},{24,28},{28,32},{32,36}... | collective-permute-start | bytes 786440 | tf_op jit(solution)/shard_map/ppermute | solution.py:13
  67.6 8.7 %copy-start.17 = (bf16[4,65,128]{2,1,0:T(8,128)(2,1)}, bf16[4,65,128]{2,1,0:T(8,128)(2,1)S(1)}, u32[]{:S(2)}) copy-start(bf16[4,65,128]{2,1,0:T(8,128)(2,1)S(1)} %all-gather.5) | copy-start | bytes 199684
  86.2 2.9 %copy-start.22 = (s32[384]{0:T(512)S(1)}, s32[384]{0:T(512)}, u32[]{:S(2)}) copy-start(s32[384]{0:T(512)} %add_bitcast_fusion) | copy-start | bytes 4612
  86.2 2.9 %copy-start.27 = (pred[384]{0:T(512)(128)(4,1)S(1)}, pred[384]{0:T(512)(128)(4,1)}, u32[]{:S(2)}) copy-start(pred[384]{0:T(512)(128)(4,1)} %broadcast_compare_fusion) | copy-start | bytes 1156
  86.2 2.9 %copy-start.28 = (s32[128]{0:T(128)S(1)}, s32[128]{0:T(128)}, u32[]{:S(2)}) copy-start(s32[128]{0:T(128)} %iota_add_fusion) | copy-start | bytes 1540
  87.0 3.9 %copy-start.7 = (bf16[512,128]{1,0:T(8,128)(2,1)S(1)}, bf16[512,128]{1,0:T(8,128)(2,1)}, u32[]{:S(2)}) copy-start(bf16[512,128]{1,0:T(8,128)(2,1)} %param.12) | copy-start | bytes 393220
  89.9 8.5 %copy-start.26 = (pred[3]{0:T(512)(128)(4,1)S(1)}, pred[3]{0:T(512)(128)(4,1)}, u32[]{:S(2)}) copy-start(pred[3]{0:T(512)(128)(4,1)} %get-tuple-element.16) | copy-start | bytes 13
  90.9 8.2 %copy-start.15 = (pred[128,384]{0,1:T(8,128)(4,1)S(1)}, pred[128,384]{0,1:T(8,128)(4,1)}, u32[]{:S(2)}) copy-start(pred[128,384]{0,1:T(8,128)(4,1)} %compare_and_fusion.2) | copy-start | bytes 147460
  99.1 0.6 copy-start.25
  99.1 1.3 copy-start.5
  99.1 1.3 copy-start.14
  100.4 0.9 copy-start.10
  100.4 1.0 copy-start.11
  100.4 1.0 copy-start.24
  100.4 1.1 copy-start.4
  100.4 1.1 copy-start.13
  101.5 0.9 copy-start.9
  101.5 0.9 copy-start.23
  101.5 1.6 copy-start.16
  103.2 0.7 copy-start.20
  103.5 3.4 %copy-start.1 = (f32[128,8,384]{0,2,1:T(8,128)}, f32[128,8,384]{0,2,1:T(8,128)S(1)}, u32[]{:S(2)}) copy-start(f32[128,8,384]{0,2,1:T(8,128)S(1)} %get-tuple-element.52) | copy-start | bytes 4718596
  104.7 3.3 %copy-start.18 = (bf16[3,128,128]{2,1,0:T(8,128)(2,1)S(1)}, bf16[3,128,128]{2,1,0:T(8,128)(2,1)}, u32[]{:S(2)}) copy-start(bf16[3,128,128]{2,1,0:T(8,128)(2,1)} %get-tuple-element.46) | copy-start | bytes 294916
  112.0 3.4 %copy-start.2 = (f32[128,8,384]{0,2,1:T(8,128)S(1)}, f32[128,8,384]{0,2,1:T(8,128)}, u32[]{:S(2)}) copy-start(f32[128,8,384]{0,2,1:T(8,128)} %copy-done.1) | copy-start | bytes 4718596
  112.0 3.4 %copy-start.19 = (bf16[3,128,128]{2,1,0:T(8,128)(2,1)S(1)}, bf16[3,128,128]{2,1,0:T(8,128)(2,1)}, u32[]{:S(2)}) copy-start(bf16[3,128,128]{2,1,0:T(8,128)(2,1)} %get-tuple-element.50) | copy-start | bytes 294916
  115.4 1.7 copy-start.6
  117.2 20.9 %collective-permute-start.1 = (bf16[512,1024]{1,0:T(8,128)(2,1)S(1)}, bf16[512,1024]{1,0:T(8,128)(2,1)S(1)}, u32[]{:S(2)}, u32[]{:S(2)}) collective-permute-start(bf16[512,1024]{1,0:T(8,128)(2,1)S(1)} %get-tuple-element.30), channel_id=1, source_target_pairs={{0,1},{1,2},{2,3},{3,0},{4,5},{5,6},{6,7},{7,4},{8,9},{9,10},{10,1... | collective-permute-start | bytes 3145736 | tf_op jit(solution)/shard_map/ppermute | solution.py:145
  121.0 40.5 %collective-permute-start.2 = (bf16[512,1024]{1,0:T(8,128)(2,1)S(1)}, bf16[512,1024]{1,0:T(8,128)(2,1)S(1)}, u32[]{:S(2)}, u32[]{:S(2)}) collective-permute-start(bf16[512,1024]{1,0:T(8,128)(2,1)S(1)} %get-tuple-element.30), channel_id=1, source_target_pairs={{0,2},{1,3},{2,0},{3,1},{4,6},{5,7},{6,4},{7,5},{8,10},{9,11},{10,... | collective-permute-start | bytes 3145736 | tf_op jit(solution)/shard_map/ppermute | solution.py:145
  122.3 44.6 %collective-permute-start.3 = (bf16[512,1024]{1,0:T(8,128)(2,1)S(1)}, bf16[512,1024]{1,0:T(8,128)(2,1)}, u32[]{:S(2)}, u32[]{:S(2)}) collective-permute-start(bf16[512,1024]{1,0:T(8,128)(2,1)S(1)} %get-tuple-element.30), channel_id=1, source_target_pairs={{0,3},{1,0},{2,1},{3,2},{4,7},{5,4},{6,5},{7,6},{8,11},{9,8},{10,9... | collective-permute-start | bytes 3145736 | tf_op jit(solution)/shard_map/ppermute | solution.py:145
Sparse Core Ops, SparseCore 0:
  10.1 118.3 all-gather.7

commit v5 on v1

--- a/solution.py
+++ b/solution.py
@@ -87,9 +87,21 @@
     norm_terms = [jnp.sum(key_feats, axis=0)]
     totals = jnp.stack(state_terms)
     counts = jnp.stack(norm_terms)
-    states, norms = carried_in(
-        (totals, counts), CTX, add_pair, (jnp.zeros_like(totals), jnp.zeros_like(counts))
-    )
+    packed = jnp.concatenate(
+        [totals[0], jnp.pad(counts, ((0, 0), (0, totals.shape[2] - counts.shape[1])))], axis=0
+    ).astype(jnp.float32)
+    before = jnp.zeros_like(packed)
+    running = packed
+    for axis in reversed(CTX):
+        size, here = (lax.axis_size(axis), lax.axis_index(axis))
+        whole = running
+        for shift in range(1, size):
+            arrived = lax.ppermute(running, axis, [(i, (i + shift) % size) for i in range(size)])
+            before = before + jnp.where(shift <= here, arrived, 0.0)
+            whole = whole + arrived
+        running = whole
+    states = before[None, : totals.shape[1]]
+    norms = before[None, totals.shape[1], : counts.shape[1]]
     scale = head_dim ** (-0.5)
     offsets = jnp.arange(block_rows, dtype=jnp.int32)
     group = 0

time: 173 us -> 167 us (0.965)
  the two profiles are of different devices: /device:TPU:8 before, /device:TPU:1 now
where the time goes in v5:
time: 167 us; the launch traced here: 166 us
  starting transfers between devices  47.7 us (29%)
  waiting for transfers between devices  40.6 us (24%)
  matrix products  34.3 us (21%)
  local copies, waits for them, and re-layouts  16.7 us (10%)
  between operations  14.6 us (9%)
  other arithmetic  12.4 us (7%)
    ppermute x11, starting transfers between devices, body(): lax.ppermute(running, axis, [(i, (i + shift) % size) for i in range(size)])  37.4 us
    dot_general x4, matrix products, body(): jnp.dot(rows_in, gathered[:, shift * width:(shift + 1) * width], preferre...  20.5 us
    all_gather x1, waiting for transfers between devices, body(): gathered = lax.all_gather(moved, CTX, axis=1, tiled=True)  20 us
    ppermute x3, waiting for transfers between devices, body(): lax.ppermute(group_cols, 'tp', [(i, (i + shift) % n_tp) for i in range(n_...  19.9 us
    gather x4, local copies, waits for them, and re-layouts, body(): key_rows = jnp.take(window_keys, chosen, axis=0).reshape(-1, head_dim)  4.78 us
    unnamed x44, local copies, waits for them, and re-layouts  4.56 us
    ppermute x1, starting transfers between devices, passed_along(): return lax.ppermute(block, axis, route)  4.54 us
    gather x4, local copies, waits for them, and re-layouts, body(): value_rows = jnp.take(window_values, chosen, axis=0).reshape(-1, head_dim)  4.01 us
  transfers between devices with their start and end apart: 17, of which 3 were waited for; matrix products, arithmetic and copies ran while one was open for 33% of the time, Pallas kernels for 0%

profile of v5, /device:TPU:1, one launch (start us, length us, event | category | flops | bytes accessed | tf_op | source)
XLA Modules:
  0.0 166.2 jit_solution(2092512514743972706)
XLA Ops:
  6.5 1.7 %collective-permute-start.12 = (bf16[1024,128]{1,0:T(8,128)(2,1)}, bf16[1024,128]{1,0:T(8,128)(2,1)S(1)}, u32[]{:S(2)}, u32[]{:S(2)}) collective-permute-start(bf16[1024,128]{1,0:T(8,128)(2,1)} %param.19), channel_id=1, source_target_pairs={{0,0},{64,65},{128,130},{192,195},{1,192},{65,1},{129,66},{193,131... | collective-permute-start | bytes 786440 | tf_op jit(solution)/shard_map/ppermute | solution.py:153
  8.3 0.7 copy-done.11
  9.0 0.7 convert_element_type.46
  9.7 1.2 fusion.55
  10.9 1.2 fusion.56
  12.1 3.3 %collective-permute-start.1 = (f32[65,128]{1,0:T(8,128)S(1)}, f32[65,128]{1,0:T(8,128)S(1)}, u32[]{:S(2)}, u32[]{:S(2)}) collective-permute-start(f32[65,128]{1,0:T(8,128)S(1)} %select_maximum_fusion), channel_id=1, source_target_pairs={{0,4},{4,0},{1,5},{5,1},{2,6},{6,2},{3,7},{7,3},{8,12},{12,8},{9,1... | collective-permute-start | bytes 99848 | tf_op jit(solution)/shard_map/ppermute | solution.py:99
  15.4 1.0 slice_reduce_fusion.3
  16.6 0.7 compare_and_fusion.6
  17.9 1.7 %pad_maximum_fusion.1 = bf16[512,256]{1,0:T(8,128)(2,1)} fusion(bf16[512,128]{1,0:T(8,128)(2,1)} %param.13, bf16[512,128]{1,0:T(8,128)(2,1)} %param.12), kind=kLoop, calls=%fused_computation.74 | loop fusion | flops 524288 | bytes 524288 | tf_op jit(solution)/shard_map/concatenate | solution.py:79
  20.2 0.8 compare_and_fusion.2
  20.9 0.8 compare_and_fusion.3
  21.7 0.8 compare_and_fusion
  22.5 0.8 compare_and_fusion.1
  24.5 3.9 %collective-permute-start.8 = (f32[65,128]{1,0:T(8,128)S(1)}, f32[65,128]{1,0:T(8,128)S(1)}, u32[]{:S(2)}, u32[]{:S(2)}) collective-permute-start(f32[65,128]{1,0:T(8,128)S(1)} %fusion.76), channel_id=1, source_target_pairs={{0,56},{8,0},{16,8},{24,16},{32,24},{40,32},{48,40},{56,48},{1,57}... | collective-permute-start | bytes 99848 | tf_op jit(solution)/shard_map/ppermute | solution.py:99
  28.5 1.2 collective-permute-start.7
  29.7 0.7 compare_and_fusion.4
  30.8 4.5 %collective-permute-start.5 = (f32[65,128]{1,0:T(8,128)S(1)}, f32[65,128]{1,0:T(8,128)S(1)}, u32[]{:S(2)}, u32[]{:S(2)}) collective-permute-start(f32[65,128]{1,0:T(8,128)S(1)} %fusion.76), channel_id=1, source_target_pairs={{0,32},{8,40},{16,48},{24,56},{32,0},{40,8},{48,16},{56,24},{1,33}... | collective-permute-start | bytes 99848 | tf_op jit(solution)/shard_map/ppermute | solution.py:99
  35.3 2.2 %collective-permute-start.3 = (f32[65,128]{1,0:T(8,128)S(1)}, f32[65,128]{1,0:T(8,128)S(1)}, u32[]{:S(2)}, u32[]{:S(2)}) collective-permute-start(f32[65,128]{1,0:T(8,128)S(1)} %fusion.76), channel_id=1, source_target_pairs={{0,16},{8,24},{16,32},{24,40},{32,48},{40,56},{48,0},{56,8},{1,17}... | collective-permute-start | bytes 99848 | tf_op jit(solution)/shard_map/ppermute | solution.py:99
  37.4 1.4 collective-permute-start.2
  39.4 4.5 %collective-permute-start = (bf16[512,256]{1,0:T(8,128)(2,1)}, bf16[512,256]{1,0:T(8,128)(2,1)}, u32[]{:S(2)}, u32[]{:S(2)}) collective-permute-start(bf16[512,256]{1,0:T(8,128)(2,1)} %pad_maximum_fusion.1), channel_id=1, source_target_pairs={{0,4},{4,8},{8,12},{12,16},{16,20},{20,24},{24,28},{28,32},{32,36}... | collective-permute-start | bytes 786440 | tf_op jit(solution)/shard_map/ppermute | solution.py:13
  44.0 18.8 %collective-permute-start.11 = (f32[65,128]{1,0:T(8,128)S(1)}, f32[65,128]{1,0:T(8,128)S(1)}, u32[]{:S(2)}, u32[]{:S(2)}) collective-permute-start(f32[65,128]{1,0:T(8,128)S(1)} %add_add_fusion), channel_id=1, source_target_pairs={{0,192},{64,0},{128,64},{192,128},{1,193},{65,1},{129,65},{193,129... | collective-permute-start | bytes 99848 | tf_op jit(solution)/shard_map/ppermute | solution.py:99
  62.8 1.7 %collective-permute-start.10 = (f32[65,128]{1,0:T(8,128)S(1)}, f32[65,128]{1,0:T(8,128)S(1)}, u32[]{:S(2)}, u32[]{:S(2)}) collective-permute-start(f32[65,128]{1,0:T(8,128)S(1)} %add_add_fusion), channel_id=1, source_target_pairs={{0,128},{64,192},{128,0},{192,64},{1,129},{65,193},{129,1},{193,65... | collective-permute-start | bytes 99848 | tf_op jit(solution)/shard_map/ppermute | solution.py:99
  65.9 0.8 copy.55
  66.8 0.8 copy.54
  67.6 0.8 copy.56
  68.5 0.6 collective-permute-done.9
  69.8 3.7 %fusion.39 = f32[1,512,8]{0,1,2:T(8,128)S(1)} fusion(f32[512,8,64]{0,2,1:T(8,128)S(1)} %get-tuple-element.49, u8[512,64]{0,1:T(8,128)(4,1)S(1)} %get-tuple-element.48, f32[65,128]{1,0:T(8,128)S(1)} %select_add_fusion), kind=kOutput, calls=%fused_computation.59 | convolution fusion | flops 4980736 | bytes 1098240 | tf_op jit(solution)/shard_map/qhr,r->qh/dot_general | solution.py:117
  73.5 1.2 copy.39
  74.7 3.2 %fusion.41 = f32[512,8,128]{0,2,1:T(8,128)S(1)} fusion(f32[512,8,64]{0,2,1:T(8,128)S(1)} %get-tuple-element.49, u8[512,64]{0,1:T(8,128)(4,1)} %copy-done.10, f32[65,128]{1,0:T(8,128)} %copy-done.15), kind=kOutput, calls=%fused_computation.60 | convolution fusion | flops 404488192 | bytes 3211264 | tf_op jit(solution)/shard_map/qhr,rd->qhd/dot_general | solution.py:116
  77.9 1.0 fusion.78
  79.0 1.5 gather_fusion.6
  80.4 1.3 gather_fusion.4
  81.8 1.3 gather_fusion.7
  83.1 0.7 gather_fusion.5
  83.8 1.3 gather_fusion.2
  85.1 1.3 gather_fusion.3
  86.4 0.7 gather_fusion
  87.1 0.7 gather_fusion.1
  87.8 1.0 broadcast_select_fusion.1
  88.9 1.2 fusion.79
  94.9 1.2 collective-permute-start.13
  96.1 2.8 %collective-permute-start.14 = (bf16[512,1024]{0,1:T(8,128)(2,1)S(1)}, bf16[512,1024]{0,1:T(8,128)(2,1)}, u32[]{:S(2)}, u32[]{:S(2)}) collective-permute-start(bf16[512,1024]{0,1:T(8,128)(2,1)S(1)} %pad_maximum_fusion), channel_id=1, source_target_pairs={{0,2},{1,3},{2,0},{3,1},{4,6},{5,7},{6,4},{7,5},{8,10},{9,11},{10,... | collective-permute-start | bytes 3145736 | tf_op jit(solution)/shard_map/ppermute | solution.py:161
  98.9 19.9 %collective-permute-done.13 = bf16[512,1024]{0,1:T(8,128)(2,1)} collective-permute-done((bf16[512,1024]{0,1:T(8,128)(2,1)S(1)}, bf16[512,1024]{0,1:T(8,128)(2,1)}, u32[]{:S(2)}, u32[]{:S(2)}) %collective-permute-start.13) | collective-permute-done | bytes 1048608 | tf_op jit(solution)/shard_map/ppermute | solution.py:161
  118.8 20.0 %all-gather.2.cloned.1.call-done = bf16[1024,8192]{1,0:T(8,128)(2,1)} async-done(((bf16[1024,128]{1,0:T(8,128)(2,1)}), bf16[1024,8192]{1,0:T(8,128)(2,1)}) %all-gather.2.cloned.1.call-update) | async-done | bytes 16777232 | tf_op jit(solution)/shard_map/all_gather | solution.py:154
  138.8 4.9 %fusion.4 = f32[512,2048]{1,0:T(8,128)S(1)} fusion(bf16[512,1024]{0,1:T(8,128)(2,1)} %collective-permute-done.13, bf16[1024,8192]{1,0:T(8,128)(2,1)} %all-gather.2.cloned.1.call-done), kind=kOutput, calls=%fused_computation.12 | convolution fusion | flops 2147483648 | bytes 9437184 | tf_op jit(solution)/shard_map/dot_general | solution.py:164
  143.7 4.9 %fusion.2 = f32[512,2048]{1,0:T(8,128)S(1)} fusion(bf16[512,1024]{0,1:T(8,128)(2,1)} %collective-permute-done.14, bf16[1024,8192]{1,0:T(8,128)(2,1)} %all-gather.2.cloned.1.call-done), kind=kOutput, calls=%fused_computation.10 | convolution fusion | flops 2147483648 | bytes 9437184 | tf_op jit(solution)/shard_map/dot_general | solution.py:164
  148.6 4.6 %fusion.6 = f32[512,2048]{1,0:T(8,128)S(1)} fusion(bf16[1024,8192]{1,0:T(8,128)(2,1)} %all-gather.2.cloned.1.call-done, bf16[128,1024]{0,1:T(8,128)(2,1)S(1)} %bitcast.129, bf16[128,1024]{0,1:T(8,128)(2,1)S(1)} %bitcast.127, bf16[128,1024]{0,1:T(8,128)(2,1)S(1)} %bitcast.125, bf16[128,1024]{0,1:T(8,128)(2,1)S(1)} %bitcast.131), kind=kOutput, calls=%fused_computation.14 | convolution fusion | flops 2151677952 | bytes 9437184 | tf_op jit(solution)/shard_map/dot_general | solution.py:164
  153.2 6.2 %add_convert_fusion = bf16[512,2048]{1,0:T(8,128)(2,1)} fusion(f32[512,2048]{1,0:T(8,128)S(1)} %fusion.2, f32[512,2048]{1,0:T(8,128)S(1)} %fusion.6, f32[512,2048]{1,0:T(8,128)S(1)} %fusion.4, bf16[512,1024]{0,1:T(8,128)(2,1)S(1)} %collective-permute-done.15, bf16[1024,8192]{1,0:T(8,128)(2,1)} %all-gather.2.cloned.1.call-done), kind=kOutput, calls=%fused_computation.16 | convolution fusion | flops 2151677952 | bytes 19922944 | tf_op jit(solution)/shard_map/dot_general | solution.py:164
  (102 shorter events, 9.7 us)
Async XLA Ops:
  6.5 16.8 %copy-start = (bf16[1,128,64]{1,2,0:T(8,128)(2,1)S(1)}, bf16[1,128,64]{1,2,0:T(8,128)(2,1)}, u32[]{:S(2)}) copy-start(bf16[1,128,64]{1,2,0:T(8,128)(2,1)} %param.16) | copy-start | bytes 49156
  6.5 16.8 %copy-start.1 = (bf16[512,1024]{1,0:T(8,128)(2,1)S(1)}, bf16[512,1024]{1,0:T(8,128)(2,1)}, u32[]{:S(2)}) copy-start(bf16[512,1024]{1,0:T(8,128)(2,1)} %param.11) | copy-start | bytes 3145732
  6.5 132.2 %all-gather.2.cloned.1.call-start = ((), (), s32[]{:S(2)}) async-start(), calls=%async_computation | async-start | bytes 17039360 | tf_op jit(solution)/shard_map/all_gather | solution.py:154
  6.5 1.7 %collective-permute-start.12 = (bf16[1024,128]{1,0:T(8,128)(2,1)}, bf16[1024,128]{1,0:T(8,128)(2,1)S(1)}, u32[]{:S(2)}, u32[]{:S(2)}) collective-permute-start(bf16[1024,128]{1,0:T(8,128)(2,1)} %param.19), channel_id=1, source_target_pairs={{0,0},{64,65},{128,130},{192,195},{1,192},{65,1},{129,66},{193,131... | collective-permute-start | bytes 786440 | tf_op jit(solution)/shard_map/ppermute | solution.py:153
  8.3 0.7 copy-start.11
  12.1 12.4 %collective-permute-start.1 = (f32[65,128]{1,0:T(8,128)S(1)}, f32[65,128]{1,0:T(8,128)S(1)}, u32[]{:S(2)}, u32[]{:S(2)}) collective-permute-start(f32[65,128]{1,0:T(8,128)S(1)} %select_maximum_fusion), channel_id=1, source_target_pairs={{0,4},{4,0},{1,5},{5,1},{2,6},{6,2},{3,7},{7,3},{8,12},{12,8},{9,1... | collective-permute-start | bytes 99848 | tf_op jit(solution)/shard_map/ppermute | solution.py:99
  23.9 49.6 %copy-start.10 = (u8[512,64]{0,1:T(8,128)(4,1)}, u8[512,64]{0,1:T(8,128)(4,1)S(1)}, u32[]{:S(2)}) copy-start(u8[512,64]{0,1:T(8,128)(4,1)S(1)} %get-tuple-element.48) | copy-start | bytes 98308
  24.5 10.7 %collective-permute-start.8 = (f32[65,128]{1,0:T(8,128)S(1)}, f32[65,128]{1,0:T(8,128)S(1)}, u32[]{:S(2)}, u32[]{:S(2)}) collective-permute-start(f32[65,128]{1,0:T(8,128)S(1)} %fusion.76), channel_id=1, source_target_pairs={{0,56},{8,0},{16,8},{24,16},{32,24},{40,32},{48,40},{56,48},{1,57}... | collective-permute-start | bytes 99848 | tf_op jit(solution)/shard_map/ppermute | solution.py:99
  28.5 8.9 %collective-permute-start.7 = (f32[65,128]{1,0:T(8,128)S(1)}, f32[65,128]{1,0:T(8,128)S(1)}, u32[]{:S(2)}, u32[]{:S(2)}) collective-permute-start(f32[65,128]{1,0:T(8,128)S(1)} %fusion.76), channel_id=1, source_target_pairs={{0,48},{8,56},{16,0},{24,8},{32,16},{40,24},{48,32},{56,40},{1,49}... | collective-permute-start | bytes 99848 | tf_op jit(solution)/shard_map/ppermute | solution.py:99
  30.3 9.1 %collective-permute-start.6 = (f32[65,128]{1,0:T(8,128)S(1)}, f32[65,128]{1,0:T(8,128)S(1)}, u32[]{:S(2)}, u32[]{:S(2)}) collective-permute-start(f32[65,128]{1,0:T(8,128)S(1)} %fusion.76), channel_id=1, source_target_pairs={{0,40},{8,48},{16,56},{24,0},{32,8},{40,16},{48,24},{56,32},{1,41}... | collective-permute-start | bytes 99848 | tf_op jit(solution)/shard_map/ppermute | solution.py:99
  30.8 13.2 %collective-permute-start.5 = (f32[65,128]{1,0:T(8,128)S(1)}, f32[65,128]{1,0:T(8,128)S(1)}, u32[]{:S(2)}, u32[]{:S(2)}) collective-permute-start(f32[65,128]{1,0:T(8,128)S(1)} %fusion.76), channel_id=1, source_target_pairs={{0,32},{8,40},{16,48},{24,56},{32,0},{40,8},{48,16},{56,24},{1,33}... | collective-permute-start | bytes 99848 | tf_op jit(solution)/shard_map/ppermute | solution.py:99
  35.3 8.7 %collective-permute-start.4 = (f32[65,128]{1,0:T(8,128)S(1)}, f32[65,128]{1,0:T(8,128)S(1)}, u32[]{:S(2)}, u32[]{:S(2)}) collective-permute-start(f32[65,128]{1,0:T(8,128)S(1)} %fusion.76), channel_id=1, source_target_pairs={{0,24},{8,32},{16,40},{24,48},{32,56},{40,0},{48,8},{56,16},{1,25}... | collective-permute-start | bytes 99848 | tf_op jit(solution)/shard_map/ppermute | solution.py:99
  35.3 8.7 %collective-permute-start.3 = (f32[65,128]{1,0:T(8,128)S(1)}, f32[65,128]{1,0:T(8,128)S(1)}, u32[]{:S(2)}, u32[]{:S(2)}) collective-permute-start(f32[65,128]{1,0:T(8,128)S(1)} %fusion.76), channel_id=1, source_target_pairs={{0,16},{8,24},{16,32},{24,40},{32,48},{40,56},{48,0},{56,8},{1,17}... | collective-permute-start | bytes 99848 | tf_op jit(solution)/shard_map/ppermute | solution.py:99
  37.4 6.6 %collective-permute-start.2 = (f32[65,128]{1,0:T(8,128)S(1)}, f32[65,128]{1,0:T(8,128)S(1)}, u32[]{:S(2)}, u32[]{:S(2)}) collective-permute-start(f32[65,128]{1,0:T(8,128)S(1)} %fusion.76), channel_id=1, source_target_pairs={{0,8},{8,16},{16,24},{24,32},{32,40},{40,48},{48,56},{56,0},{1,9},... | collective-permute-start | bytes 99848 | tf_op jit(solution)/shard_map/ppermute | solution.py:99
  39.4 38.5 %collective-permute-start = (bf16[512,256]{1,0:T(8,128)(2,1)}, bf16[512,256]{1,0:T(8,128)(2,1)}, u32[]{:S(2)}, u32[]{:S(2)}) collective-permute-start(bf16[512,256]{1,0:T(8,128)(2,1)} %pad_maximum_fusion.1), channel_id=1, source_target_pairs={{0,4},{4,8},{8,12},{12,16},{16,20},{20,24},{24,28},{28,32},{32,36}... | collective-permute-start | bytes 786440 | tf_op jit(solution)/shard_map/ppermute | solution.py:13
  44.0 24.5 %collective-permute-start.11 = (f32[65,128]{1,0:T(8,128)S(1)}, f32[65,128]{1,0:T(8,128)S(1)}, u32[]{:S(2)}, u32[]{:S(2)}) collective-permute-start(f32[65,128]{1,0:T(8,128)S(1)} %add_add_fusion), channel_id=1, source_target_pairs={{0,192},{64,0},{128,64},{192,128},{1,193},{65,1},{129,65},{193,129... | collective-permute-start | bytes 99848 | tf_op jit(solution)/shard_map/ppermute | solution.py:99
  62.8 5.7 %collective-permute-start.10 = (f32[65,128]{1,0:T(8,128)S(1)}, f32[65,128]{1,0:T(8,128)S(1)}, u32[]{:S(2)}, u32[]{:S(2)}) collective-permute-start(f32[65,128]{1,0:T(8,128)S(1)} %add_add_fusion), channel_id=1, source_target_pairs={{0,128},{64,192},{128,0},{192,64},{1,129},{65,193},{129,1},{193,65... | collective-permute-start | bytes 99848 | tf_op jit(solution)/shard_map/ppermute | solution.py:99
  64.5 4.6 %collective-permute-start.9 = (f32[65,128]{1,0:T(8,128)S(1)}, f32[65,128]{1,0:T(8,128)S(1)}, u32[]{:S(2)}, u32[]{:S(2)}) collective-permute-start(f32[65,128]{1,0:T(8,128)S(1)} %add_add_fusion), channel_id=1, source_target_pairs={{0,64},{64,128},{128,192},{192,0},{1,65},{65,129},{129,193},{193,1... | collective-permute-start | bytes 99848 | tf_op jit(solution)/shard_map/ppermute | solution.py:99
  69.2 0.6 copy-start.15
  74.7 4.2 %copy-start.5 = (bf16[512,128]{1,0:T(8,128)(2,1)S(1)}, bf16[512,128]{1,0:T(8,128)(2,1)}, u32[]{:S(2)}) copy-start(bf16[512,128]{1,0:T(8,128)(2,1)} %param.12) | copy-start | bytes 393220
  74.7 7.0 %copy-start.6 = (bf16[512,128]{1,0:T(8,128)(2,1)S(1)}, bf16[512,128]{1,0:T(8,128)(2,1)}, u32[]{:S(2)}) copy-start(bf16[512,128]{1,0:T(8,128)(2,1)} %param.13) | copy-start | bytes 393220
  78.9 9.9 %copy-start.4 = (bf16[128,1024]{0,1:T(8,128)(2,1)S(1)}, bf16[128,1024]{0,1:T(8,128)(2,1)}, u32[]{:S(2)}) copy-start(bf16[128,1024]{0,1:T(8,128)(2,1)} %copy.56) | copy-start | bytes 786436
  88.9 1.5 copy-start.8
  88.9 1.5 copy-start.9
  88.9 1.5 copy-start.18
  88.9 1.6 copy-start.3
  88.9 1.6 copy-start.14
  90.5 0.9 copy-start.7
  90.5 0.9 copy-start.19
  90.6 1.0 copy-start.2
  90.6 1.0 copy-start.13
  91.6 0.6 copy-start.17
  91.6 0.8 copy-start.12
  92.4 0.7 copy-start.16
  94.9 23.9 %collective-permute-start.13 = (bf16[512,1024]{0,1:T(8,128)(2,1)S(1)}, bf16[512,1024]{0,1:T(8,128)(2,1)}, u32[]{:S(2)}, u32[]{:S(2)}) collective-permute-start(bf16[512,1024]{0,1:T(8,128)(2,1)S(1)} %pad_maximum_fusion), channel_id=1, source_target_pairs={{0,1},{1,2},{2,3},{3,0},{4,5},{5,6},{6,7},{7,4},{8,9},{9,10},{10,1... | collective-permute-start | bytes 3145736 | tf_op jit(solution)/shard_map/ppermute | solution.py:161
  96.1 47.6 %collective-permute-start.14 = (bf16[512,1024]{0,1:T(8,128)(2,1)S(1)}, bf16[512,1024]{0,1:T(8,128)(2,1)}, u32[]{:S(2)}, u32[]{:S(2)}) collective-permute-start(bf16[512,1024]{0,1:T(8,128)(2,1)S(1)} %pad_maximum_fusion), channel_id=1, source_target_pairs={{0,2},{1,3},{2,0},{3,1},{4,6},{5,7},{6,4},{7,5},{8,10},{9,11},{10,... | collective-permute-start | bytes 3145736 | tf_op jit(solution)/shard_map/ppermute | solution.py:161
  98.9 54.3 %collective-permute-start.15 = (bf16[512,1024]{0,1:T(8,128)(2,1)S(1)}, bf16[512,1024]{0,1:T(8,128)(2,1)S(1)}, u32[]{:S(2)}, u32[]{:S(2)}) collective-permute-start(bf16[512,1024]{0,1:T(8,128)(2,1)S(1)} %pad_maximum_fusion), channel_id=1, source_target_pairs={{0,3},{1,0},{2,1},{3,2},{4,7},{5,4},{6,5},{7,6},{8,11},{9,8},{10,9... | collective-permute-start | bytes 3145736 | tf_op jit(solution)/shard_map/ppermute | solution.py:161
Sparse Core Ops, SparseCore 0:
  9.9 128.8 all-gather.1

commit v6 on v4

--- a/solution.py
+++ b/solution.py
@@ -87,9 +87,21 @@
     norm_terms = [jnp.sum(key_feats, axis=0)]
     totals = jnp.stack(state_terms)
     counts = jnp.stack(norm_terms)
-    states, norms = carried_in(
-        (totals, counts), CTX, add_pair, (jnp.zeros_like(totals), jnp.zeros_like(counts))
-    )
+    packed = jnp.concatenate(
+        [totals[0], jnp.pad(counts, ((0, 0), (0, totals.shape[2] - counts.shape[1])))], axis=0
+    ).astype(jnp.float32)
+    before = jnp.zeros_like(packed)
+    running = packed
+    for axis in reversed(CTX):
+        size, here = (lax.axis_size(axis), lax.axis_index(axis))
+        whole = running
+        for shift in range(1, size):
+            arrived = lax.ppermute(running, axis, [(i, (i + shift) % size) for i in range(size)])
+            before = before + jnp.where(shift <= here, arrived, 0.0)
+            whole = whole + arrived
+        running = whole
+    states = before[None, : totals.shape[1]]
+    norms = before[None, totals.shape[1], : counts.shape[1]]
     scale = head_dim ** (-0.5)
     offsets = jnp.arange(block_rows, dtype=jnp.int32)
     group = 0
@@ -145,10 +157,9 @@
         lax.ppermute(group_cols, "tp", [(i, (i + shift) % n_tp) for i in range(n_tp)])
         for shift in range(1, n_tp)
     ]
-    every_group = jnp.stack(rows_by_shift, axis=1)
     summed = jnp.einsum(
-        "tsk,ksn->tn",
-        every_group,
+        "stk,ksn->tn",
+        jnp.stack(rows_by_shift),
         gathered.reshape(gathered.shape[0], n_tp, width),
         preferred_element_type=jnp.float32,
     )

time: 189 us -> 179 us (0.947)
  blocking collectives: 49.4 us -> 0 us
  starting transfers between devices: 11.9 us -> 48.8 us
  matrix products: 33.5 us -> 35.9 us
    all_gather x3 -> x0, blocking collectives: 49.4 us -> none  [all_in_one(): both, at, found = (lax.all_gather(jnp.concatenate(lines), axis), 0, {})]
    ppermute x0 -> x11, starting transfers between devices: none -> 38.8 us  [body(): lax.ppermute(running, axis, [(i, (i + shift) % size) for i in range(size)])]
    unnamed x66 -> x63, local copies, waits for them, and re-layouts: 4.82 us -> 6 us
  transfers between devices with their start and end apart: 6 -> 17, of which waited for: 3 -> 3; matrix products, arithmetic and copies ran while one was open for 28% -> 30% of each run, Pallas kernels for 0% -> 0%
where the time goes in v6:
time: 179 us; the launch traced here: 178 us
  starting transfers between devices  48.8 us (27%)
  waiting for transfers between devices  44.6 us (25%)
  matrix products  35.9 us (20%)
  local copies, waits for them, and re-layouts  20.1 us (11%)
  between operations  14.6 us (8%)
  other arithmetic  13.9 us (8%)
    ppermute x3, waiting for transfers between devices, body(): lax.ppermute(group_cols, 'tp', [(i, (i + shift) % n_tp) for i in range(n_...  44.6 us
    ppermute x11, starting transfers between devices, body(): lax.ppermute(running, axis, [(i, (i + shift) % size) for i in range(size)])  38.8 us
    dot_general x1, matrix products, body(): jnp.einsum('stk,ksn->tn', jnp.stack(rows_by_shift), gathered.reshape(gath...  13.6 us
    dot_general x4, matrix products, body(): jnp.einsum('qhk,kd->qhd', probs, value_rows, preferred_element_type=jnp.f...  8.29 us
    unnamed x63, local copies, waits for them, and re-layouts  6 us
    ppermute x3, starting transfers between devices, body(): lax.ppermute(group_cols, 'tp', [(i, (i + shift) % n_tp) for i in range(n_...  4.73 us
    ppermute x1, starting transfers between devices, passed_along(): return lax.ppermute(block, axis, route)  4.53 us
    dot_general x1, matrix products, body(): jnp.einsum('qhr,rd->qhd', query_feats, states[group], precision=highest)  4.49 us
  transfers between devices with their start and end apart: 17, of which 3 were waited for; matrix products, arithmetic and copies ran while one was open for 30% of the time, Pallas kernels for 0%

profile of v6, /device:TPU:1, one launch (start us, length us, event | category | flops | bytes accessed | tf_op | source)
XLA Modules:
  0.0 177.9 jit_solution(8262841418917025983)
XLA Ops:
  6.6 1.2 copy.44
  9.2 0.7 convert_element_type.46
  9.9 1.2 fusion.57
  11.1 1.2 fusion.58
  12.3 3.3 %collective-permute-start.1 = (f32[65,128]{1,0:T(8,128)S(1)}, f32[65,128]{1,0:T(8,128)S(1)}, u32[]{:S(2)}, u32[]{:S(2)}) collective-permute-start(f32[65,128]{1,0:T(8,128)S(1)} %select_maximum_fusion), channel_id=1, source_target_pairs={{0,4},{4,0},{1,5},{5,1},{2,6},{6,2},{3,7},{7,3},{8,12},{12,8},{9,1... | collective-permute-start | bytes 99848 | tf_op jit(solution)/shard_map/ppermute | solution.py:99
  17.2 0.7 pad_maximum_fusion.1
  18.5 0.8 compare_and_fusion.2
  19.3 0.8 compare_and_fusion.1
  20.1 0.8 compare_and_fusion.3
  20.9 0.8 compare_and_fusion
  21.8 1.1 fusion.51
  23.6 2.9 %collective-permute-start.3 = (f32[65,128]{1,0:T(8,128)S(1)}, f32[65,128]{1,0:T(8,128)S(1)}, u32[]{:S(2)}, u32[]{:S(2)}) collective-permute-start(f32[65,128]{1,0:T(8,128)S(1)} %fusion.79), channel_id=1, source_target_pairs={{0,16},{8,24},{16,32},{24,40},{32,48},{40,56},{48,0},{56,8},{1,17}... | collective-permute-start | bytes 99848 | tf_op jit(solution)/shard_map/ppermute | solution.py:99
  27.1 3.8 %collective-permute-start.4 = (f32[65,128]{1,0:T(8,128)S(1)}, f32[65,128]{1,0:T(8,128)S(1)}, u32[]{:S(2)}, u32[]{:S(2)}) collective-permute-start(f32[65,128]{1,0:T(8,128)S(1)} %fusion.79), channel_id=1, source_target_pairs={{0,24},{8,32},{16,40},{24,48},{32,56},{40,0},{48,8},{56,16},{1,25}... | collective-permute-start | bytes 99848 | tf_op jit(solution)/shard_map/ppermute | solution.py:99
  31.4 4.5 %collective-permute-start.6 = (f32[65,128]{1,0:T(8,128)S(1)}, f32[65,128]{1,0:T(8,128)S(1)}, u32[]{:S(2)}, u32[]{:S(2)}) collective-permute-start(f32[65,128]{1,0:T(8,128)S(1)} %fusion.79), channel_id=1, source_target_pairs={{0,40},{8,48},{16,56},{24,0},{32,8},{40,16},{48,24},{56,32},{1,41}... | collective-permute-start | bytes 99848 | tf_op jit(solution)/shard_map/ppermute | solution.py:99
  35.8 2.4 %collective-permute-start.7 = (f32[65,128]{1,0:T(8,128)S(1)}, f32[65,128]{1,0:T(8,128)S(1)}, u32[]{:S(2)}, u32[]{:S(2)}) collective-permute-start(f32[65,128]{1,0:T(8,128)S(1)} %fusion.79), channel_id=1, source_target_pairs={{0,48},{8,56},{16,0},{24,8},{32,16},{40,24},{48,32},{56,40},{1,49}... | collective-permute-start | bytes 99848 | tf_op jit(solution)/shard_map/ppermute | solution.py:99
  38.2 0.7 collective-permute-start.8
  39.5 4.5 %collective-permute-start = (bf16[512,256]{1,0:T(8,128)(2,1)}, bf16[512,256]{1,0:T(8,128)(2,1)}, u32[]{:S(2)}, u32[]{:S(2)}) collective-permute-start(bf16[512,256]{1,0:T(8,128)(2,1)} %pad_maximum_fusion.1), channel_id=1, source_target_pairs={{0,4},{4,8},{8,12},{12,16},{16,20},{20,24},{24,28},{28,32},{32,36}... | collective-permute-start | bytes 786440 | tf_op jit(solution)/shard_map/ppermute | solution.py:13
  44.2 16.3 %collective-permute-start.10 = (f32[65,128]{1,0:T(8,128)S(1)}, f32[65,128]{1,0:T(8,128)S(1)}, u32[]{:S(2)}, u32[]{:S(2)}) collective-permute-start(f32[65,128]{1,0:T(8,128)S(1)} %add_add_fusion), channel_id=1, source_target_pairs={{0,128},{64,192},{128,0},{192,64},{1,129},{65,193},{129,1},{193,65... | collective-permute-start | bytes 99848 | tf_op jit(solution)/shard_map/ppermute | solution.py:99
  60.4 4.5 %collective-permute-start.11 = (f32[65,128]{1,0:T(8,128)S(1)}, f32[65,128]{1,0:T(8,128)S(1)}, u32[]{:S(2)}, u32[]{:S(2)}) collective-permute-start(f32[65,128]{1,0:T(8,128)S(1)} %add_add_fusion), channel_id=1, source_target_pairs={{0,192},{64,0},{128,64},{192,128},{1,193},{65,1},{129,65},{193,129... | collective-permute-start | bytes 99848 | tf_op jit(solution)/shard_map/ppermute | solution.py:99
  65.5 0.8 copy.65
  66.4 0.8 copy.66
  67.2 0.9 copy.64
  68.9 0.8 select_add_fusion
  70.4 4.5 %fusion.41 = f32[1,512,8]{0,1,2:T(8,128)S(1)} fusion(f32[512,8,64]{0,2,1:T(8,128)S(1)} %get-tuple-element.51, u8[512,64]{0,1:T(8,128)(4,1)} %get-tuple-element.50, f32[65,128]{1,0:T(8,128)S(1)} %select_add_fusion), kind=kOutput, calls=%fused_computation.59 | convolution fusion | flops 4980736 | bytes 1098240 | tf_op jit(solution)/shard_map/qhr,r->qh/dot_general | solution.py:117
  74.8 1.2 copy.49
  76.1 4.5 %fusion.43 = f32[512,8,128]{0,2,1:T(8,128)} fusion(f32[512,8,64]{0,2,1:T(8,128)S(1)} %get-tuple-element.51, u8[512,64]{0,1:T(8,128)(4,1)} %get-tuple-element.50, f32[65,128]{1,0:T(8,128)} %copy-done.19), kind=kOutput, calls=%fused_computation.60 | convolution fusion | flops 404488192 | bytes 3211264 | tf_op jit(solution)/shard_map/qhr,rd->qhd/dot_general | solution.py:116
  80.5 1.0 fusion.82
  81.6 0.8 gather_fusion.2
  82.4 0.7 gather_fusion.3
  84.5 1.3 gather_fusion
  85.9 1.3 gather_fusion.1
  87.9 1.3 gather_fusion.7
  89.2 0.7 broadcast_select_fusion.5
  90.6 0.7 broadcast_select_fusion.3
  93.3 0.7 broadcast_select_fusion.1
  94.7 0.8 fusion.69
  95.5 2.2 %fusion.22 = bf16[128,8,128]{0,2,1:T(8,128)(2,1)} fusion(bf16[384,128,1]{1,0,2:T(8,128)(2,1)S(1)} %bitcast.137, f32[128,8,384]{0,2,1:T(8,128)S(1)} %get-tuple-element.55, f32[128,8]{0,1:T(8,128)S(1)} %get-tuple-element.54, f32[512,8,128]{0,2,1:T(8,128)} %fusion.43, f32[128,8]{0,1:T(8,128)S(1)} %get-tuple-element.10, f32[128,8]{0,1:T(8,128)S(1)} %get-tuple-element.11), kind=kOutput, calls=%fused_computation.41 | convolution fusion | flops 101974016 | bytes 2469888 | tf_op jit(solution)/shard_map/qhk,kd->qhd/dot_general | solution.py:140
  97.7 1.1 copy.40
  98.8 2.2 %fusion.23 = bf16[128,8,128]{0,2,1:T(8,128)(2,1)} fusion(bf16[384,128,1]{1,0,2:T(8,128)(2,1)S(1)} %bitcast.134, f32[128,8,384]{0,2,1:T(8,128)S(1)} %get-tuple-element.59, f32[128,8]{0,1:T(8,128)S(1)} %get-tuple-element.58, f32[512,8,128]{0,2,1:T(8,128)} %fusion.43, f32[128,8]{0,1:T(8,128)S(1)} %get-tuple-element.38, f32[128,8]{0,1:T(8,128)} %get-tuple-element.39), kind=kOutput, calls=%fused_computation.42 | convolution fusion | flops 101974016 | bytes 2469888 | tf_op jit(solution)/shard_map/qhk,kd->qhd/dot_general | solution.py:140
  100.9 1.8 %copy.41 = bf16[128,1024]{1,0:T(8,128)(2,1)} copy(bf16[128,1024]{0,1:T(8,128)(2,1)} %bitcast.132) | data formatting | bytes 524288 | tf_op jit(solution)/shard_map/convert_element_type | solution.py:145
  102.7 2.5 %fusion.24 = bf16[128,8,128]{0,2,1:T(8,128)(2,1)} fusion(bf16[384,128,1]{1,0,2:T(8,128)(2,1)} %bitcast.135, f32[128,8,384]{0,2,1:T(8,128)S(1)} %get-tuple-element.57, f32[128,8]{0,1:T(8,128)S(1)} %get-tuple-element.56, f32[512,8,128]{0,2,1:T(8,128)} %fusion.43, f32[128,8]{0,1:T(8,128)S(1)} %get-tuple-element.36, f32[128,8]{0,1:T(8,128)S(1)} %get-tuple-element.37), kind=kOutput, calls=%fused_computation.43 | convolution fusion | flops 101974016 | bytes 2469888 | tf_op jit(solution)/shard_map/qhk,kd->qhd/dot_general | solution.py:140
  105.2 1.1 copy.42
  106.3 1.5 fusion.25
  108.1 1.5 collective-permute-start.12
  109.6 3.3 %collective-permute-start.13 = (bf16[512,1024]{1,0:T(8,128)(2,1)S(1)}, bf16[512,1024]{1,0:T(8,128)(2,1)S(1)}, u32[]{:S(2)}, u32[]{:S(2)}) collective-permute-start(bf16[512,1024]{1,0:T(8,128)(2,1)S(1)} %get-tuple-element.27), channel_id=1, source_target_pairs={{0,2},{1,3},{2,0},{3,1},{4,6},{5,7},{6,4},{7,5},{8,10},{9,11},{10,... | collective-permute-start | bytes 3145736 | tf_op jit(solution)/shard_map/ppermute | solution.py:157
  112.8 20.7 %collective-permute-done.12 = bf16[512,1024]{1,0:T(8,128)(2,1)S(1)} collective-permute-done((bf16[512,1024]{1,0:T(8,128)(2,1)S(1)}, bf16[512,1024]{1,0:T(8,128)(2,1)S(1)}, u32[]{:S(2)}, u32[]{:S(2)}) %collective-permute-start.12) | collective-permute-done | bytes 1048608 | tf_op jit(solution)/shard_map/ppermute | solution.py:157
  133.6 23.4 %collective-permute-done.13 = bf16[512,1024]{1,0:T(8,128)(2,1)S(1)} collective-permute-done((bf16[512,1024]{1,0:T(8,128)(2,1)S(1)}, bf16[512,1024]{1,0:T(8,128)(2,1)S(1)}, u32[]{:S(2)}, u32[]{:S(2)}) %collective-permute-start.13) | collective-permute-done | bytes 1048608 | tf_op jit(solution)/shard_map/ppermute | solution.py:157
  157.4 13.6 %bitcast_convert_fusion = bf16[512,2048]{1,0:T(8,128)(2,1)} fusion(bf16[1024,4,2048]{0,2,1:T(8,128)(2,1)} %bitcast.143, bf16[1,512,1024]{2,1,0:T(8,128)(2,1)} %bitcast.47, bf16[1,512,1024]{2,1,0:T(8,128)(2,1)S(1)} %bitcast.145, bf16[1,512,1024]{2,1,0:T(8,128)(2,1)S(1)} %bitcast.144, bf16[1,512,1024]{2,1,0:T(8,128)(2,1)S(1)} %get-tuple-element.26), kind=kOutput, calls=%fused_computation.16 | convolution fusion | flops 8597274624 | bytes 23068672 | tf_op jit(solution)/shard_map/stk,ksn->tn/dot_general | solution.py:160
  (122 shorter events, 13.6 us)
Async XLA Ops:
  6.5 15.2 %copy-start = (bf16[1,128,64]{1,2,0:T(8,128)(2,1)S(1)}, bf16[1,128,64]{1,2,0:T(8,128)(2,1)}, u32[]{:S(2)}) copy-start(bf16[1,128,64]{1,2,0:T(8,128)(2,1)} %param.16) | copy-start | bytes 49156
  6.5 10.7 %copy-start.8 = (bf16[512,128]{1,0:T(8,128)(2,1)S(1)}, bf16[512,128]{1,0:T(8,128)(2,1)}, u32[]{:S(2)}) copy-start(bf16[512,128]{1,0:T(8,128)(2,1)} %param.12) | copy-start | bytes 393220
  6.5 10.7 %copy-start.9 = (bf16[512,128]{1,0:T(8,128)(2,1)S(1)}, bf16[512,128]{1,0:T(8,128)(2,1)}, u32[]{:S(2)}) copy-start(bf16[512,128]{1,0:T(8,128)(2,1)} %param.13) | copy-start | bytes 393220
  6.5 9.1 %copy-start.24 = (s32[4,2]{0,1:T(2,128)S(1)}, s32[4,2]{0,1:T(2,128)}, u32[]{:S(2)}) copy-start(s32[4,2]{0,1:T(2,128)} %param.15) | copy-start | bytes 100
  6.5 15.1 %copy-start.3 = (bf16[512,1024]{1,0:T(8,128)(2,1)S(1)}, bf16[512,1024]{1,0:T(8,128)(2,1)}, u32[]{:S(2)}) copy-start(bf16[512,1024]{1,0:T(8,128)(2,1)} %param.11) | copy-start | bytes 3145732
  6.5 150.9 %all-gather.2.cloned.1.call-start = ((), (), s32[]{:S(2)}) async-start(), calls=%async_computation | async-start | bytes 17039360 | tf_op jit(solution)/shard_map/all_gather | solution.py:154
  7.8 0.7 collective-permute-start.15
  8.5 0.7 copy-start.14
  12.3 11.2 %collective-permute-start.1 = (f32[65,128]{1,0:T(8,128)S(1)}, f32[65,128]{1,0:T(8,128)S(1)}, u32[]{:S(2)}, u32[]{:S(2)}) collective-permute-start(f32[65,128]{1,0:T(8,128)S(1)} %select_maximum_fusion), channel_id=1, source_target_pairs={{0,4},{4,0},{1,5},{5,1},{2,6},{6,2},{3,7},{7,3},{8,12},{12,8},{9,1... | collective-permute-start | bytes 99848 | tf_op jit(solution)/shard_map/ppermute | solution.py:99
  23.5 44.5 %copy-start.20 = (f32[65,128]{1,0:T(8,128)}, f32[65,128]{1,0:T(8,128)S(1)}, u32[]{:S(2)}) copy-start(f32[65,128]{1,0:T(8,128)S(1)} %collective-permute-done.1) | copy-start | bytes 99844
  23.6 12.3 %collective-permute-start.2 = (f32[65,128]{1,0:T(8,128)S(1)}, f32[65,128]{1,0:T(8,128)S(1)}, u32[]{:S(2)}, u32[]{:S(2)}) collective-permute-start(f32[65,128]{1,0:T(8,128)S(1)} %fusion.79), channel_id=1, source_target_pairs={{0,8},{8,16},{16,24},{24,32},{32,40},{40,48},{48,56},{56,0},{1,9},... | collective-permute-start | bytes 99848 | tf_op jit(solution)/shard_map/ppermute | solution.py:99
  23.6 14.6 %collective-permute-start.3 = (f32[65,128]{1,0:T(8,128)S(1)}, f32[65,128]{1,0:T(8,128)S(1)}, u32[]{:S(2)}, u32[]{:S(2)}) collective-permute-start(f32[65,128]{1,0:T(8,128)S(1)} %fusion.79), channel_id=1, source_target_pairs={{0,16},{8,24},{16,32},{24,40},{32,48},{40,56},{48,0},{56,8},{1,17}... | collective-permute-start | bytes 99848 | tf_op jit(solution)/shard_map/ppermute | solution.py:99
  27.1 12.4 %collective-permute-start.4 = (f32[65,128]{1,0:T(8,128)S(1)}, f32[65,128]{1,0:T(8,128)S(1)}, u32[]{:S(2)}, u32[]{:S(2)}) collective-permute-start(f32[65,128]{1,0:T(8,128)S(1)} %fusion.79), channel_id=1, source_target_pairs={{0,24},{8,32},{16,40},{24,48},{32,56},{40,0},{48,8},{56,16},{1,25}... | collective-permute-start | bytes 99848 | tf_op jit(solution)/shard_map/ppermute | solution.py:99
  30.9 13.2 %collective-permute-start.5 = (f32[65,128]{1,0:T(8,128)S(1)}, f32[65,128]{1,0:T(8,128)S(1)}, u32[]{:S(2)}, u32[]{:S(2)}) collective-permute-start(f32[65,128]{1,0:T(8,128)S(1)} %fusion.79), channel_id=1, source_target_pairs={{0,32},{8,40},{16,48},{24,56},{32,0},{40,8},{48,16},{56,24},{1,33}... | collective-permute-start | bytes 99848 | tf_op jit(solution)/shard_map/ppermute | solution.py:99
  31.4 12.7 %collective-permute-start.6 = (f32[65,128]{1,0:T(8,128)S(1)}, f32[65,128]{1,0:T(8,128)S(1)}, u32[]{:S(2)}, u32[]{:S(2)}) collective-permute-start(f32[65,128]{1,0:T(8,128)S(1)} %fusion.79), channel_id=1, source_target_pairs={{0,40},{8,48},{16,56},{24,0},{32,8},{40,16},{48,24},{56,32},{1,41}... | collective-permute-start | bytes 99848 | tf_op jit(solution)/shard_map/ppermute | solution.py:99
  35.8 8.3 %collective-permute-start.7 = (f32[65,128]{1,0:T(8,128)S(1)}, f32[65,128]{1,0:T(8,128)S(1)}, u32[]{:S(2)}, u32[]{:S(2)}) collective-permute-start(f32[65,128]{1,0:T(8,128)S(1)} %fusion.79), channel_id=1, source_target_pairs={{0,48},{8,56},{16,0},{24,8},{32,16},{40,24},{48,32},{56,40},{1,49}... | collective-permute-start | bytes 99848 | tf_op jit(solution)/shard_map/ppermute | solution.py:99
  38.2 5.9 %collective-permute-start.8 = (f32[65,128]{1,0:T(8,128)S(1)}, f32[65,128]{1,0:T(8,128)S(1)}, u32[]{:S(2)}, u32[]{:S(2)}) collective-permute-start(f32[65,128]{1,0:T(8,128)S(1)} %fusion.79), channel_id=1, source_target_pairs={{0,56},{8,0},{16,8},{24,16},{32,24},{40,32},{48,40},{56,48},{1,57}... | collective-permute-start | bytes 99848 | tf_op jit(solution)/shard_map/ppermute | solution.py:99
  39.5 41.0 %collective-permute-start = (bf16[512,256]{1,0:T(8,128)(2,1)}, bf16[512,256]{1,0:T(8,128)(2,1)}, u32[]{:S(2)}, u32[]{:S(2)}) collective-permute-start(bf16[512,256]{1,0:T(8,128)(2,1)} %pad_maximum_fusion.1), channel_id=1, source_target_pairs={{0,4},{4,8},{8,12},{12,16},{16,20},{20,24},{24,28},{28,32},{32,36}... | collective-permute-start | bytes 786440 | tf_op jit(solution)/shard_map/ppermute | solution.py:13
  44.2 24.7 %collective-permute-start.10 = (f32[65,128]{1,0:T(8,128)S(1)}, f32[65,128]{1,0:T(8,128)S(1)}, u32[]{:S(2)}, u32[]{:S(2)}) collective-permute-start(f32[65,128]{1,0:T(8,128)S(1)} %add_add_fusion), channel_id=1, source_target_pairs={{0,128},{64,192},{128,0},{192,64},{1,129},{65,193},{129,1},{193,65... | collective-permute-start | bytes 99848 | tf_op jit(solution)/shard_map/ppermute | solution.py:99
  60.4 8.4 %collective-permute-start.11 = (f32[65,128]{1,0:T(8,128)S(1)}, f32[65,128]{1,0:T(8,128)S(1)}, u32[]{:S(2)}, u32[]{:S(2)}) collective-permute-start(f32[65,128]{1,0:T(8,128)S(1)} %add_add_fusion), channel_id=1, source_target_pairs={{0,192},{64,0},{128,64},{192,128},{1,193},{65,1},{129,65},{193,129... | collective-permute-start | bytes 99848 | tf_op jit(solution)/shard_map/ppermute | solution.py:99
  64.9 4.0 %collective-permute-start.9 = (f32[65,128]{1,0:T(8,128)S(1)}, f32[65,128]{1,0:T(8,128)S(1)}, u32[]{:S(2)}, u32[]{:S(2)}) collective-permute-start(f32[65,128]{1,0:T(8,128)S(1)} %add_add_fusion), channel_id=1, source_target_pairs={{0,64},{64,128},{128,192},{192,0},{1,65},{65,129},{129,193},{193,1... | collective-permute-start | bytes 99848 | tf_op jit(solution)/shard_map/ppermute | solution.py:99
  69.7 0.6 copy-start.19
  76.0 6.4 %copy-start.10 = (bf16[512,128]{1,0:T(8,128)(2,1)S(1)}, bf16[512,128]{1,0:T(8,128)(2,1)}, u32[]{:S(2)}) copy-start(bf16[512,128]{1,0:T(8,128)(2,1)} %param.13) | copy-start | bytes 393220
  80.5 8.7 %copy-start.26 = (pred[3]{0:T(512)(128)(4,1)S(1)}, pred[3]{0:T(512)(128)(4,1)}, u32[]{:S(2)}) copy-start(pred[3]{0:T(512)(128)(4,1)} %get-tuple-element.16) | copy-start | bytes 13
  81.5 8.4 %copy-start.6 = (bf16[128,1024]{0,1:T(8,128)(2,1)S(1)}, bf16[128,1024]{0,1:T(8,128)(2,1)}, u32[]{:S(2)}) copy-start(bf16[128,1024]{0,1:T(8,128)(2,1)} %copy.65) | copy-start | bytes 786436
  81.5 8.4 %copy-start.18 = (pred[128,384]{0,1:T(8,128)(4,1)S(1)}, pred[128,384]{0,1:T(8,128)(4,1)}, u32[]{:S(2)}) copy-start(pred[128,384]{0,1:T(8,128)(4,1)} %compare_and_fusion.2) | copy-start | bytes 147460
  89.9 0.6 copy-start.28
  89.9 1.4 copy-start.5
  89.9 1.4 copy-start.17
  91.3 0.9 copy-start.12
  91.3 1.0 copy-start.13
  91.3 1.0 copy-start.25
  91.3 1.1 copy-start.4
  91.3 1.1 copy-start.16
  92.4 0.9 copy-start.11
  92.4 0.9 copy-start.27
  92.4 1.6 copy-start.15
  94.0 0.7 copy-start.23
  94.4 3.3 %copy-start.1 = (f32[128,8,384]{0,2,1:T(8,128)}, f32[128,8,384]{0,2,1:T(8,128)S(1)}, u32[]{:S(2)}) copy-start(f32[128,8,384]{0,2,1:T(8,128)S(1)} %get-tuple-element.49) | copy-start | bytes 4718596
  95.5 3.3 %copy-start.21 = (bf16[3,128,128]{2,1,0:T(8,128)(2,1)S(1)}, bf16[3,128,128]{2,1,0:T(8,128)(2,1)}, u32[]{:S(2)}) copy-start(bf16[3,128,128]{2,1,0:T(8,128)(2,1)} %get-tuple-element.43) | copy-start | bytes 294916
  102.7 3.6 %copy-start.2 = (f32[128,8,384]{0,2,1:T(8,128)S(1)}, f32[128,8,384]{0,2,1:T(8,128)}, u32[]{:S(2)}) copy-start(f32[128,8,384]{0,2,1:T(8,128)} %copy-done.1) | copy-start | bytes 4718596
  102.7 3.6 %copy-start.22 = (bf16[3,128,128]{2,1,0:T(8,128)(2,1)S(1)}, bf16[3,128,128]{2,1,0:T(8,128)(2,1)}, u32[]{:S(2)}) copy-start(bf16[3,128,128]{2,1,0:T(8,128)(2,1)} %get-tuple-element.47) | copy-start | bytes 294916
  106.3 1.7 copy-start.7
  108.1 25.4 %collective-permute-start.12 = (bf16[512,1024]{1,0:T(8,128)(2,1)S(1)}, bf16[512,1024]{1,0:T(8,128)(2,1)S(1)}, u32[]{:S(2)}, u32[]{:S(2)}) collective-permute-start(bf16[512,1024]{1,0:T(8,128)(2,1)S(1)} %get-tuple-element.27), channel_id=1, source_target_pairs={{0,1},{1,2},{2,3},{3,0},{4,5},{5,6},{6,7},{7,4},{8,9},{9,10},{10,1... | collective-permute-start | bytes 3145736 | tf_op jit(solution)/shard_map/ppermute | solution.py:157
  109.6 47.4 %collective-permute-start.13 = (bf16[512,1024]{1,0:T(8,128)(2,1)S(1)}, bf16[512,1024]{1,0:T(8,128)(2,1)S(1)}, u32[]{:S(2)}, u32[]{:S(2)}) collective-permute-start(bf16[512,1024]{1,0:T(8,128)(2,1)S(1)} %get-tuple-element.27), channel_id=1, source_target_pairs={{0,2},{1,3},{2,0},{3,1},{4,6},{5,7},{6,4},{7,5},{8,10},{9,11},{10,... | collective-permute-start | bytes 3145736 | tf_op jit(solution)/shard_map/ppermute | solution.py:157
  112.8 44.6 %collective-permute-start.14 = (bf16[512,1024]{1,0:T(8,128)(2,1)S(1)}, bf16[512,1024]{1,0:T(8,128)(2,1)}, u32[]{:S(2)}, u32[]{:S(2)}) collective-permute-start(bf16[512,1024]{1,0:T(8,128)(2,1)S(1)} %get-tuple-element.27), channel_id=1, source_target_pairs={{0,3},{1,0},{2,1},{3,2},{4,7},{5,4},{6,5},{7,6},{8,11},{9,8},{10,9... | collective-permute-start | bytes 3145736 | tf_op jit(solution)/shard_map/ppermute | solution.py:157
Sparse Core Ops, SparseCore 0:
  10.1 121.0 all-gather.1

commit v7 on v5

--- a/solution.py
+++ b/solution.py
@@ -164,8 +164,8 @@
         term = jnp.dot(
             rows_in,
             gathered[:, shift * width : (shift + 1) * width],
-            preferred_element_type=jnp.float32,
-        )
+            preferred_element_type=jnp.bfloat16,
+        ).astype(jnp.float32)
         summed = term if summed is None else summed + term
     return summed.astype(jnp.bfloat16)
 

time: 167 us -> 169 us (1.012)
    unnamed x44 -> x56, local copies, waits for them, and re-layouts: 4.56 us -> 4.85 us
where the time goes in v7:
time: 169 us; the launch traced here: 168 us
  starting transfers between devices  49.2 us (29%)
  waiting for transfers between devices  40 us (24%)
  matrix products  34.7 us (21%)
  local copies, waits for them, and re-layouts  16.9 us (10%)
  between operations  14.7 us (9%)
  other arithmetic  12.4 us (7%)
    ppermute x11, starting transfers between devices, body(): lax.ppermute(running, axis, [(i, (i + shift) % size) for i in range(size)])  38.1 us
    dot_general x4, matrix products, body(): jnp.dot(rows_in, gathered[:, shift * width:(shift + 1) * width], preferre...  21 us
    all_gather x1, waiting for transfers between devices, body(): gathered = lax.all_gather(moved, CTX, axis=1, tiled=True)  20.4 us
    ppermute x3, waiting for transfers between devices, body(): lax.ppermute(group_cols, 'tp', [(i, (i + shift) % n_tp) for i in range(n_...  19.5 us
    unnamed x56, local copies, waits for them, and re-layouts  4.85 us
    ppermute x3, starting transfers between devices, body(): lax.ppermute(group_cols, 'tp', [(i, (i + shift) % n_tp) for i in range(n_...  4.82 us
    gather x4, local copies, waits for them, and re-layouts, body(): value_rows = jnp.take(window_values, chosen, axis=0).reshape(-1, head_dim)  4.64 us
    ppermute x1, starting transfers between devices, passed_along(): return lax.ppermute(block, axis, route)  4.53 us
  transfers between devices with their start and end apart: 17, of which 3 were waited for; matrix products, arithmetic and copies ran while one was open for 33% of the time, Pallas kernels for 0%

profile of v7, /device:TPU:1, one launch (start us, length us, event | category | flops | bytes accessed | tf_op | source)
XLA Modules:
  0.0 168.0 jit_solution(12062898460422342455)
XLA Ops:
  6.5 1.7 %collective-permute-start.12 = (bf16[1024,128]{1,0:T(8,128)(2,1)}, bf16[1024,128]{1,0:T(8,128)(2,1)S(1)}, u32[]{:S(2)}, u32[]{:S(2)}) collective-permute-start(bf16[1024,128]{1,0:T(8,128)(2,1)} %param.19), channel_id=1, source_target_pairs={{0,0},{64,65},{128,130},{192,195},{1,192},{65,1},{129,66},{193,131... | collective-permute-start | bytes 786440 | tf_op jit(solution)/shard_map/ppermute | solution.py:153
  8.3 0.7 copy-done.11
  9.0 0.7 convert_element_type.58
  9.7 1.2 fusion.57
  10.9 1.2 fusion.58
  12.1 3.3 %collective-permute-start.1 = (f32[65,128]{1,0:T(8,128)S(1)}, f32[65,128]{1,0:T(8,128)S(1)}, u32[]{:S(2)}, u32[]{:S(2)}) collective-permute-start(f32[65,128]{1,0:T(8,128)S(1)} %select_maximum_fusion), channel_id=1, source_target_pairs={{0,4},{4,0},{1,5},{5,1},{2,6},{6,2},{3,7},{7,3},{8,12},{12,8},{9,1... | collective-permute-start | bytes 99848 | tf_op jit(solution)/shard_map/ppermute | solution.py:99
  15.4 1.0 slice_reduce_fusion.3
  16.6 0.7 compare_and_fusion.6
  17.9 1.7 %pad_maximum_fusion.1 = bf16[512,256]{1,0:T(8,128)(2,1)} fusion(bf16[512,128]{1,0:T(8,128)(2,1)} %param.13, bf16[512,128]{1,0:T(8,128)(2,1)} %param.12), kind=kLoop, calls=%fused_computation.74 | loop fusion | flops 524288 | bytes 524288 | tf_op jit(solution)/shard_map/concatenate | solution.py:79
  20.2 0.8 compare_and_fusion.2
  21.0 0.8 compare_and_fusion.1
  21.8 0.8 compare_and_fusion.3
  22.5 0.8 compare_and_fusion
  23.9 0.7 compare_and_fusion.4
  24.7 2.9 %collective-permute-start.3 = (f32[65,128]{1,0:T(8,128)S(1)}, f32[65,128]{1,0:T(8,128)S(1)}, u32[]{:S(2)}, u32[]{:S(2)}) collective-permute-start(f32[65,128]{1,0:T(8,128)S(1)} %fusion.78), channel_id=1, source_target_pairs={{0,16},{8,24},{16,32},{24,40},{32,48},{40,56},{48,0},{56,8},{1,17}... | collective-permute-start | bytes 99848 | tf_op jit(solution)/shard_map/ppermute | solution.py:99
  28.2 3.8 %collective-permute-start.4 = (f32[65,128]{1,0:T(8,128)S(1)}, f32[65,128]{1,0:T(8,128)S(1)}, u32[]{:S(2)}, u32[]{:S(2)}) collective-permute-start(f32[65,128]{1,0:T(8,128)S(1)} %fusion.78), channel_id=1, source_target_pairs={{0,24},{8,32},{16,40},{24,48},{32,56},{40,0},{48,8},{56,16},{1,25}... | collective-permute-start | bytes 99848 | tf_op jit(solution)/shard_map/ppermute | solution.py:99
  32.4 4.5 %collective-permute-start.6 = (f32[65,128]{1,0:T(8,128)S(1)}, f32[65,128]{1,0:T(8,128)S(1)}, u32[]{:S(2)}, u32[]{:S(2)}) collective-permute-start(f32[65,128]{1,0:T(8,128)S(1)} %fusion.78), channel_id=1, source_target_pairs={{0,40},{8,48},{16,56},{24,0},{32,8},{40,16},{48,24},{56,32},{1,41}... | collective-permute-start | bytes 99848 | tf_op jit(solution)/shard_map/ppermute | solution.py:99
  36.9 2.4 %collective-permute-start.7 = (f32[65,128]{1,0:T(8,128)S(1)}, f32[65,128]{1,0:T(8,128)S(1)}, u32[]{:S(2)}, u32[]{:S(2)}) collective-permute-start(f32[65,128]{1,0:T(8,128)S(1)} %fusion.78), channel_id=1, source_target_pairs={{0,48},{8,56},{16,0},{24,8},{32,16},{40,24},{48,32},{56,40},{1,49}... | collective-permute-start | bytes 99848 | tf_op jit(solution)/shard_map/ppermute | solution.py:99
  39.3 0.7 collective-permute-start.8
  40.6 4.5 %collective-permute-start = (bf16[512,256]{1,0:T(8,128)(2,1)}, bf16[512,256]{1,0:T(8,128)(2,1)}, u32[]{:S(2)}, u32[]{:S(2)}) collective-permute-start(bf16[512,256]{1,0:T(8,128)(2,1)} %pad_maximum_fusion.1), channel_id=1, source_target_pairs={{0,4},{4,8},{8,12},{12,16},{16,20},{20,24},{24,28},{28,32},{32,36}... | collective-permute-start | bytes 786440 | tf_op jit(solution)/shard_map/ppermute | solution.py:13
  45.2 15.5 %collective-permute-start.10 = (f32[65,128]{1,0:T(8,128)S(1)}, f32[65,128]{1,0:T(8,128)S(1)}, u32[]{:S(2)}, u32[]{:S(2)}) collective-permute-start(f32[65,128]{1,0:T(8,128)S(1)} %add_add_fusion), channel_id=1, source_target_pairs={{0,128},{64,192},{128,0},{192,64},{1,129},{65,193},{129,1},{193,65... | collective-permute-start | bytes 99848 | tf_op jit(solution)/shard_map/ppermute | solution.py:99
  60.8 4.5 %collective-permute-start.11 = (f32[65,128]{1,0:T(8,128)S(1)}, f32[65,128]{1,0:T(8,128)S(1)}, u32[]{:S(2)}, u32[]{:S(2)}) collective-permute-start(f32[65,128]{1,0:T(8,128)S(1)} %add_add_fusion), channel_id=1, source_target_pairs={{0,192},{64,0},{128,64},{192,128},{1,193},{65,1},{129,65},{193,129... | collective-permute-start | bytes 99848 | tf_op jit(solution)/shard_map/ppermute | solution.py:99
  65.9 0.8 copy.54
  66.7 0.8 copy.55
  67.5 0.8 copy.53
  70.0 3.7 %fusion.41 = f32[1,512,8]{0,1,2:T(8,128)S(1)} fusion(f32[512,8,64]{0,2,1:T(8,128)S(1)} %get-tuple-element.49, u8[512,64]{0,1:T(8,128)(4,1)S(1)} %get-tuple-element.48, f32[65,128]{1,0:T(8,128)S(1)} %select_add_fusion), kind=kOutput, calls=%fused_computation.59 | convolution fusion | flops 4980736 | bytes 1098240 | tf_op jit(solution)/shard_map/qhr,r->qh/dot_general | solution.py:117
  73.7 1.2 copy.39
  74.9 3.2 %fusion.43 = f32[512,8,128]{0,2,1:T(8,128)S(1)} fusion(f32[512,8,64]{0,2,1:T(8,128)S(1)} %get-tuple-element.49, u8[512,64]{0,1:T(8,128)(4,1)} %copy-done.10, f32[65,128]{1,0:T(8,128)} %copy-done.21), kind=kOutput, calls=%fused_computation.60 | convolution fusion | flops 404488192 | bytes 3211264 | tf_op jit(solution)/shard_map/qhr,rd->qhd/dot_general | solution.py:116
  78.1 1.0 fusion.80
  79.2 1.5 gather_fusion.2
  80.6 1.3 gather_fusion.3
  81.9 1.3 gather_fusion.4
  83.3 1.3 gather_fusion.5
  84.6 0.7 gather_fusion
  85.3 1.3 gather_fusion.1
  86.6 0.7 gather_fusion.7
  87.3 0.7 gather_fusion.6
  88.0 1.0 broadcast_select_fusion.5
  89.1 1.2 fusion.84
  95.3 2.1 %collective-permute-start.14 = (bf16[512,1024]{0,1:T(8,128)(2,1)S(1)}, bf16[512,1024]{0,1:T(8,128)(2,1)}, u32[]{:S(2)}, u32[]{:S(2)}) collective-permute-start(bf16[512,1024]{0,1:T(8,128)(2,1)S(1)} %pad_maximum_fusion), channel_id=1, source_target_pairs={{0,2},{1,3},{2,0},{3,1},{4,6},{5,7},{6,4},{7,5},{8,10},{9,11},{10,... | collective-permute-start | bytes 3145736 | tf_op jit(solution)/shard_map/ppermute | solution.py:161
  97.5 1.7 %collective-permute-start.13 = (bf16[512,1024]{0,1:T(8,128)(2,1)S(1)}, bf16[512,1024]{0,1:T(8,128)(2,1)}, u32[]{:S(2)}, u32[]{:S(2)}) collective-permute-start(bf16[512,1024]{0,1:T(8,128)(2,1)S(1)} %pad_maximum_fusion), channel_id=1, source_target_pairs={{0,1},{1,2},{2,3},{3,0},{4,5},{5,6},{6,7},{7,4},{8,9},{9,10},{10,1... | collective-permute-start | bytes 3145736 | tf_op jit(solution)/shard_map/ppermute | solution.py:161
  99.2 1.0 collective-permute-start.15
  100.2 19.4 %collective-permute-done.14 = bf16[512,1024]{0,1:T(8,128)(2,1)} collective-permute-done((bf16[512,1024]{0,1:T(8,128)(2,1)S(1)}, bf16[512,1024]{0,1:T(8,128)(2,1)}, u32[]{:S(2)}, u32[]{:S(2)}) %collective-permute-start.14) | collective-permute-done | bytes 1048608 | tf_op jit(solution)/shard_map/ppermute | solution.py:161
  119.6 20.4 %all-gather.2.cloned.1.call-done = bf16[1024,8192]{1,0:T(8,128)(2,1)} async-done(((bf16[1024,128]{1,0:T(8,128)(2,1)}), bf16[1024,8192]{1,0:T(8,128)(2,1)}) %all-gather.2.cloned.1.call-update) | async-done | bytes 16777232 | tf_op jit(solution)/shard_map/all_gather | solution.py:154
  140.1 4.9 %fusion.2 = bf16[512,2048]{1,0:T(8,128)(2,1)S(1)} fusion(bf16[512,1024]{0,1:T(8,128)(2,1)} %collective-permute-done.14, bf16[1024,8192]{1,0:T(8,128)(2,1)} %all-gather.2.cloned.1.call-done), kind=kOutput, calls=%fused_computation.10 | convolution fusion | flops 2147483648 | bytes 7340032 | tf_op jit(solution)/shard_map/dot_general | solution.py:164
  145.0 4.9 %fusion.4 = bf16[512,2048]{1,0:T(8,128)(2,1)S(1)} fusion(bf16[512,1024]{0,1:T(8,128)(2,1)} %collective-permute-done.13, bf16[1024,8192]{1,0:T(8,128)(2,1)} %all-gather.2.cloned.1.call-done), kind=kOutput, calls=%fused_computation.12 | convolution fusion | flops 2147483648 | bytes 7340032 | tf_op jit(solution)/shard_map/dot_general | solution.py:164
  150.0 4.6 %fusion.6 = bf16[512,2048]{1,0:T(8,128)(2,1)S(1)} fusion(bf16[1024,8192]{1,0:T(8,128)(2,1)} %all-gather.2.cloned.1.call-done, bf16[128,1024]{0,1:T(8,128)(2,1)S(1)} %bitcast.131, bf16[128,1024]{0,1:T(8,128)(2,1)S(1)} %bitcast.129, bf16[128,1024]{0,1:T(8,128)(2,1)S(1)} %bitcast.127, bf16[128,1024]{0,1:T(8,128)(2,1)S(1)} %bitcast.125), kind=kOutput, calls=%fused_computation.14 | convolution fusion | flops 2151677952 | bytes 7340032 | tf_op jit(solution)/shard_map/dot_general | solution.py:164
  154.5 6.6 %add_convert_fusion = bf16[512,2048]{1,0:T(8,128)(2,1)} fusion(bf16[512,2048]{1,0:T(8,128)(2,1)S(1)} %fusion.2, bf16[512,2048]{1,0:T(8,128)(2,1)S(1)} %fusion.4, bf16[512,2048]{1,0:T(8,128)(2,1)S(1)} %fusion.6, bf16[512,1024]{0,1:T(8,128)(2,1)S(1)} %collective-permute-done.15, bf16[1024,8192]{1,0:T(8,128)(2,1)} %all-gather.2.cloned.1.call-done), kind=kOutput, calls=%fused_computation.16 | convolution fusion | flops 2155872256 | bytes 13631488 | tf_op jit(solution)/shard_map/dot_general | solution.py:164
  (114 shorter events, 10.1 us)
Async XLA Ops:
  6.5 16.9 %copy-start = (bf16[1,128,64]{1,2,0:T(8,128)(2,1)S(1)}, bf16[1,128,64]{1,2,0:T(8,128)(2,1)}, u32[]{:S(2)}) copy-start(bf16[1,128,64]{1,2,0:T(8,128)(2,1)} %param.16) | copy-start | bytes 49156
  6.5 16.8 %copy-start.1 = (bf16[512,1024]{1,0:T(8,128)(2,1)S(1)}, bf16[512,1024]{1,0:T(8,128)(2,1)}, u32[]{:S(2)}) copy-start(bf16[512,1024]{1,0:T(8,128)(2,1)} %param.11) | copy-start | bytes 3145732
  6.5 133.5 %all-gather.2.cloned.1.call-start = ((), (), s32[]{:S(2)}) async-start(), calls=%async_computation | async-start | bytes 17039360 | tf_op jit(solution)/shard_map/all_gather | solution.py:154
  6.5 1.7 %collective-permute-start.12 = (bf16[1024,128]{1,0:T(8,128)(2,1)}, bf16[1024,128]{1,0:T(8,128)(2,1)S(1)}, u32[]{:S(2)}, u32[]{:S(2)}) collective-permute-start(bf16[1024,128]{1,0:T(8,128)(2,1)} %param.19), channel_id=1, source_target_pairs={{0,0},{64,65},{128,130},{192,195},{1,192},{65,1},{129,66},{193,131... | collective-permute-start | bytes 786440 | tf_op jit(solution)/shard_map/ppermute | solution.py:153
  8.3 0.7 copy-start.11
  12.1 12.5 %collective-permute-start.1 = (f32[65,128]{1,0:T(8,128)S(1)}, f32[65,128]{1,0:T(8,128)S(1)}, u32[]{:S(2)}, u32[]{:S(2)}) collective-permute-start(f32[65,128]{1,0:T(8,128)S(1)} %select_maximum_fusion), channel_id=1, source_target_pairs={{0,4},{4,0},{1,5},{5,1},{2,6},{6,2},{3,7},{7,3},{8,12},{12,8},{9,1... | collective-permute-start | bytes 99848 | tf_op jit(solution)/shard_map/ppermute | solution.py:99
  23.9 49.8 %copy-start.10 = (u8[512,64]{0,1:T(8,128)(4,1)}, u8[512,64]{0,1:T(8,128)(4,1)S(1)}, u32[]{:S(2)}) copy-start(u8[512,64]{0,1:T(8,128)(4,1)S(1)} %get-tuple-element.48) | copy-start | bytes 98308
  24.6 12.3 %collective-permute-start.2 = (f32[65,128]{1,0:T(8,128)S(1)}, f32[65,128]{1,0:T(8,128)S(1)}, u32[]{:S(2)}, u32[]{:S(2)}) collective-permute-start(f32[65,128]{1,0:T(8,128)S(1)} %fusion.78), channel_id=1, source_target_pairs={{0,8},{8,16},{16,24},{24,32},{32,40},{40,48},{48,56},{56,0},{1,9},... | collective-permute-start | bytes 99848 | tf_op jit(solution)/shard_map/ppermute | solution.py:99
  24.7 14.6 %collective-permute-start.3 = (f32[65,128]{1,0:T(8,128)S(1)}, f32[65,128]{1,0:T(8,128)S(1)}, u32[]{:S(2)}, u32[]{:S(2)}) collective-permute-start(f32[65,128]{1,0:T(8,128)S(1)} %fusion.78), channel_id=1, source_target_pairs={{0,16},{8,24},{16,32},{24,40},{32,48},{40,56},{48,0},{56,8},{1,17}... | collective-permute-start | bytes 99848 | tf_op jit(solution)/shard_map/ppermute | solution.py:99
  28.2 12.4 %collective-permute-start.4 = (f32[65,128]{1,0:T(8,128)S(1)}, f32[65,128]{1,0:T(8,128)S(1)}, u32[]{:S(2)}, u32[]{:S(2)}) collective-permute-start(f32[65,128]{1,0:T(8,128)S(1)} %fusion.78), channel_id=1, source_target_pairs={{0,24},{8,32},{16,40},{24,48},{32,56},{40,0},{48,8},{56,16},{1,25}... | collective-permute-start | bytes 99848 | tf_op jit(solution)/shard_map/ppermute | solution.py:99
  32.0 13.2 %collective-permute-start.5 = (f32[65,128]{1,0:T(8,128)S(1)}, f32[65,128]{1,0:T(8,128)S(1)}, u32[]{:S(2)}, u32[]{:S(2)}) collective-permute-start(f32[65,128]{1,0:T(8,128)S(1)} %fusion.78), channel_id=1, source_target_pairs={{0,32},{8,40},{16,48},{24,56},{32,0},{40,8},{48,16},{56,24},{1,33}... | collective-permute-start | bytes 99848 | tf_op jit(solution)/shard_map/ppermute | solution.py:99
  32.4 12.7 %collective-permute-start.6 = (f32[65,128]{1,0:T(8,128)S(1)}, f32[65,128]{1,0:T(8,128)S(1)}, u32[]{:S(2)}, u32[]{:S(2)}) collective-permute-start(f32[65,128]{1,0:T(8,128)S(1)} %fusion.78), channel_id=1, source_target_pairs={{0,40},{8,48},{16,56},{24,0},{32,8},{40,16},{48,24},{56,32},{1,41}... | collective-permute-start | bytes 99848 | tf_op jit(solution)/shard_map/ppermute | solution.py:99
  36.9 8.3 %collective-permute-start.7 = (f32[65,128]{1,0:T(8,128)S(1)}, f32[65,128]{1,0:T(8,128)S(1)}, u32[]{:S(2)}, u32[]{:S(2)}) collective-permute-start(f32[65,128]{1,0:T(8,128)S(1)} %fusion.78), channel_id=1, source_target_pairs={{0,48},{8,56},{16,0},{24,8},{32,16},{40,24},{48,32},{56,40},{1,49}... | collective-permute-start | bytes 99848 | tf_op jit(solution)/shard_map/ppermute | solution.py:99
  39.3 5.9 %collective-permute-start.8 = (f32[65,128]{1,0:T(8,128)S(1)}, f32[65,128]{1,0:T(8,128)S(1)}, u32[]{:S(2)}, u32[]{:S(2)}) collective-permute-start(f32[65,128]{1,0:T(8,128)S(1)} %fusion.78), channel_id=1, source_target_pairs={{0,56},{8,0},{16,8},{24,16},{32,24},{40,32},{48,40},{56,48},{1,57}... | collective-permute-start | bytes 99848 | tf_op jit(solution)/shard_map/ppermute | solution.py:99
  40.6 37.5 %collective-permute-start = (bf16[512,256]{1,0:T(8,128)(2,1)}, bf16[512,256]{1,0:T(8,128)(2,1)}, u32[]{:S(2)}, u32[]{:S(2)}) collective-permute-start(bf16[512,256]{1,0:T(8,128)(2,1)} %pad_maximum_fusion.1), channel_id=1, source_target_pairs={{0,4},{4,8},{8,12},{12,16},{16,20},{20,24},{24,28},{28,32},{32,36}... | collective-permute-start | bytes 786440 | tf_op jit(solution)/shard_map/ppermute | solution.py:13
  45.2 24.0 %collective-permute-start.10 = (f32[65,128]{1,0:T(8,128)S(1)}, f32[65,128]{1,0:T(8,128)S(1)}, u32[]{:S(2)}, u32[]{:S(2)}) collective-permute-start(f32[65,128]{1,0:T(8,128)S(1)} %add_add_fusion), channel_id=1, source_target_pairs={{0,128},{64,192},{128,0},{192,64},{1,129},{65,193},{129,1},{193,65... | collective-permute-start | bytes 99848 | tf_op jit(solution)/shard_map/ppermute | solution.py:99
  60.8 8.4 %collective-permute-start.11 = (f32[65,128]{1,0:T(8,128)S(1)}, f32[65,128]{1,0:T(8,128)S(1)}, u32[]{:S(2)}, u32[]{:S(2)}) collective-permute-start(f32[65,128]{1,0:T(8,128)S(1)} %add_add_fusion), channel_id=1, source_target_pairs={{0,192},{64,0},{128,64},{192,128},{1,193},{65,1},{129,65},{193,129... | collective-permute-start | bytes 99848 | tf_op jit(solution)/shard_map/ppermute | solution.py:99
  65.3 4.0 %collective-permute-start.9 = (f32[65,128]{1,0:T(8,128)S(1)}, f32[65,128]{1,0:T(8,128)S(1)}, u32[]{:S(2)}, u32[]{:S(2)}) collective-permute-start(f32[65,128]{1,0:T(8,128)S(1)} %add_add_fusion), channel_id=1, source_target_pairs={{0,64},{64,128},{128,192},{192,0},{1,65},{65,129},{129,193},{193,1... | collective-permute-start | bytes 99848 | tf_op jit(solution)/shard_map/ppermute | solution.py:99
  69.3 0.6 copy-start.21
  74.9 4.2 %copy-start.5 = (bf16[512,128]{1,0:T(8,128)(2,1)S(1)}, bf16[512,128]{1,0:T(8,128)(2,1)}, u32[]{:S(2)}) copy-start(bf16[512,128]{1,0:T(8,128)(2,1)} %param.12) | copy-start | bytes 393220
  74.9 5.7 %copy-start.6 = (bf16[512,128]{1,0:T(8,128)(2,1)S(1)}, bf16[512,128]{1,0:T(8,128)(2,1)}, u32[]{:S(2)}) copy-start(bf16[512,128]{1,0:T(8,128)(2,1)} %param.13) | copy-start | bytes 393220
  79.1 9.9 %copy-start.4 = (bf16[128,1024]{0,1:T(8,128)(2,1)S(1)}, bf16[128,1024]{0,1:T(8,128)(2,1)}, u32[]{:S(2)}) copy-start(bf16[128,1024]{0,1:T(8,128)(2,1)} %copy.54) | copy-start | bytes 786436
  89.0 1.5 copy-start.8
  89.0 1.5 copy-start.9
  89.1 1.5 copy-start.25
  89.1 1.6 copy-start.3
  89.1 1.6 copy-start.20
  90.7 0.9 copy-start.7
  90.7 0.9 copy-start.23
  90.7 1.0 copy-start.2
  90.7 1.0 copy-start.19
  91.7 0.7 copy-start.24
  91.7 0.8 copy-start.18
  92.5 0.7 copy-start.22
  94.1 0.9 copy-start.12
  94.5 0.7 copy-start.14
  94.9 5.2 %copy-start.16 = (bf16[128,8,128]{0,2,1:T(8,128)(2,1)}, bf16[128,8,128]{0,2,1:T(8,128)(2,1)S(1)}, u32[]{:S(2)}) copy-start(bf16[128,8,128]{0,2,1:T(8,128)(2,1)S(1)} %fusion.25) | copy-start | bytes 786436
  95.3 24.3 %collective-permute-start.14 = (bf16[512,1024]{0,1:T(8,128)(2,1)S(1)}, bf16[512,1024]{0,1:T(8,128)(2,1)}, u32[]{:S(2)}, u32[]{:S(2)}) collective-permute-start(bf16[512,1024]{0,1:T(8,128)(2,1)S(1)} %pad_maximum_fusion), channel_id=1, source_target_pairs={{0,2},{1,3},{2,0},{3,1},{4,6},{5,7},{6,4},{7,5},{8,10},{9,11},{10,... | collective-permute-start | bytes 3145736 | tf_op jit(solution)/shard_map/ppermute | solution.py:161
  97.5 47.5 %collective-permute-start.13 = (bf16[512,1024]{0,1:T(8,128)(2,1)S(1)}, bf16[512,1024]{0,1:T(8,128)(2,1)}, u32[]{:S(2)}, u32[]{:S(2)}) collective-permute-start(bf16[512,1024]{0,1:T(8,128)(2,1)S(1)} %pad_maximum_fusion), channel_id=1, source_target_pairs={{0,1},{1,2},{2,3},{3,0},{4,5},{5,6},{6,7},{7,4},{8,9},{9,10},{10,1... | collective-permute-start | bytes 3145736 | tf_op jit(solution)/shard_map/ppermute | solution.py:161
  99.2 55.4 %collective-permute-start.15 = (bf16[512,1024]{0,1:T(8,128)(2,1)S(1)}, bf16[512,1024]{0,1:T(8,128)(2,1)S(1)}, u32[]{:S(2)}, u32[]{:S(2)}) collective-permute-start(bf16[512,1024]{0,1:T(8,128)(2,1)S(1)} %pad_maximum_fusion), channel_id=1, source_target_pairs={{0,3},{1,0},{2,1},{3,2},{4,7},{5,4},{6,5},{7,6},{8,11},{9,8},{10,9... | collective-permute-start | bytes 3145736 | tf_op jit(solution)/shard_map/ppermute | solution.py:161
  144.9 5.0 %copy-start.13 = (bf16[128,8,128]{0,2,1:T(8,128)(2,1)S(1)}, bf16[128,8,128]{0,2,1:T(8,128)(2,1)}, u32[]{:S(2)}) copy-start(bf16[128,8,128]{0,2,1:T(8,128)(2,1)} %copy-done.12) | copy-start | bytes 786436
  145.0 5.0 %copy-start.15 = (bf16[128,8,128]{0,2,1:T(8,128)(2,1)S(1)}, bf16[128,8,128]{0,2,1:T(8,128)(2,1)}, u32[]{:S(2)}) copy-start(bf16[128,8,128]{0,2,1:T(8,128)(2,1)} %copy-done.14) | copy-start | bytes 786436
  145.0 5.0 %copy-start.17 = (bf16[128,8,128]{0,2,1:T(8,128)(2,1)S(1)}, bf16[128,8,128]{0,2,1:T(8,128)(2,1)}, u32[]{:S(2)}) copy-start(bf16[128,8,128]{0,2,1:T(8,128)(2,1)} %copy-done.16) | copy-start | bytes 786436
Sparse Core Ops, SparseCore 0:
  9.9 130.1 all-gather.1

commit v8 on v5

--- a/solution.py
+++ b/solution.py
@@ -92,7 +92,7 @@
     ).astype(jnp.float32)
     before = jnp.zeros_like(packed)
     running = packed
-    for axis in reversed(CTX):
+    for axis in reversed(CTX[1:]):
         size, here = (lax.axis_size(axis), lax.axis_index(axis))
         whole = running
         for shift in range(1, size):
@@ -100,6 +100,13 @@
             before = before + jnp.where(shift <= here, arrived, 0.0)
             whole = whole + arrived
         running = whole
+    size = lax.axis_size(CTX[0])
+    upto = running
+    shift = 1
+    while shift < size:
+        upto = upto + lax.ppermute(upto, CTX[0], [(i, i + shift) for i in range(size - shift)])
+        shift *= 2
+    before = before + (upto - running)
     states = before[None, : totals.shape[1]]
     norms = before[None, totals.shape[1], : counts.shape[1]]
     scale = head_dim ** (-0.5)

time: 167 us -> 173 us (1.036)
  starting transfers between devices: 47.7 us -> 51.5 us
    ppermute x0 -> x2, starting transfers between devices: none -> 22.9 us  [body(): lax.ppermute(upto, CTX[0], [(i, i + shift) for i in range(size - shift)])]
    ppermute x11 -> x8, starting transfers between devices: 37.4 us -> 16.9 us  [body(): lax.ppermute(running, axis, [(i, (i + shift) % size) for i in range(size)])]
    all_gather x1, waiting for transfers between devices: 20 us -> 14.2 us  [body(): gathered = lax.all_gather(moved, CTX, axis=1, tiled=True)]
    ppermute x3, waiting for transfers between devices: 19.9 us -> 25 us  [body(): lax.ppermute(group_cols, 'tp', [(i, (i + shift) % n_tp) for i in range(n_...]
    ppermute x0 -> x2, waiting for transfers between devices: none -> 1.93 us  [body(): lax.ppermute(upto, CTX[0], [(i, i + shift) for i in range(size - shift)])]
  transfers between devices with their start and end apart: 17 -> 16, of which waited for: 3 -> 4; matrix products, arithmetic and copies ran while one was open for 33% -> 32% of each run, Pallas kernels for 0% -> 0%
where the time goes in v8:
time: 173 us; the launch traced here: 171 us
  starting transfers between devices  51.5 us (30%)
  waiting for transfers between devices  41.2 us (24%)
  matrix products  34.3 us (20%)
  local copies, waits for them, and re-layouts  16.7 us (10%)
  between operations  14.6 us (8%)
  other arithmetic  12.4 us (7%)
    ppermute x3, waiting for transfers between devices, body(): lax.ppermute(group_cols, 'tp', [(i, (i + shift) % n_tp) for i in range(n_...  25 us
    ppermute x2, starting transfers between devices, body(): lax.ppermute(upto, CTX[0], [(i, i + shift) for i in range(size - shift)])  22.9 us
    dot_general x4, matrix products, body(): jnp.dot(rows_in, gathered[:, shift * width:(shift + 1) * width], preferre...  20.5 us
    ppermute x8, starting transfers between devices, body(): lax.ppermute(running, axis, [(i, (i + shift) % size) for i in range(size)])  16.9 us
    all_gather x1, waiting for transfers between devices, body(): gathered = lax.all_gather(moved, CTX, axis=1, tiled=True)  14.2 us
    ppermute x3, starting transfers between devices, body(): lax.ppermute(group_cols, 'tp', [(i, (i + shift) % n_tp) for i in range(n_...  5.41 us
    gather x4, local copies, waits for them, and re-layouts, body(): key_rows = jnp.take(window_keys, chosen, axis=0).reshape(-1, head_dim)  4.81 us
    unnamed x44, local copies, waits for them, and re-layouts  4.6 us
  transfers between devices with their start and end apart: 16, of which 4 were waited for; matrix products, arithmetic and copies ran while one was open for 32% of the time, Pallas kernels for 0%

profile of v8, /device:TPU:1, one launch (start us, length us, event | category | flops | bytes accessed | tf_op | source)
XLA Modules:
  0.0 170.6 jit_solution(15308843227289237597)
XLA Ops:
  6.5 1.7 %collective-permute-start.11 = (bf16[1024,128]{1,0:T(8,128)(2,1)}, bf16[1024,128]{1,0:T(8,128)(2,1)S(1)}, u32[]{:S(2)}, u32[]{:S(2)}) collective-permute-start(bf16[1024,128]{1,0:T(8,128)(2,1)} %param.19), channel_id=1, source_target_pairs={{0,0},{64,65},{128,130},{192,195},{1,192},{65,1},{129,66},{193,131... | collective-permute-start | bytes 786440 | tf_op jit(solution)/shard_map/ppermute | solution.py:160
  8.3 0.7 copy-done.11
  9.0 0.7 convert_element_type.46
  9.7 1.2 fusion.55
  10.9 1.2 fusion.56
  12.1 3.3 %collective-permute-start.1 = (f32[65,128]{1,0:T(8,128)S(1)}, f32[65,128]{1,0:T(8,128)S(1)}, u32[]{:S(2)}, u32[]{:S(2)}) collective-permute-start(f32[65,128]{1,0:T(8,128)S(1)} %select_maximum_fusion), channel_id=1, source_target_pairs={{0,4},{4,0},{1,5},{5,1},{2,6},{6,2},{3,7},{7,3},{8,12},{12,8},{9,1... | collective-permute-start | bytes 99848 | tf_op jit(solution)/shard_map/ppermute | solution.py:99
  15.4 1.0 slice_reduce_fusion.3
  16.6 0.7 compare_and_fusion.6
  17.3 1.7 pad_maximum_fusion.1
  19.6 0.8 compare_and_fusion.2
  20.4 0.8 compare_and_fusion.3
  21.1 0.8 compare_and_fusion
  21.9 0.8 compare_and_fusion.1
  24.0 3.9 %collective-permute-start.8 = (f32[65,128]{1,0:T(8,128)S(1)}, f32[65,128]{1,0:T(8,128)S(1)}, u32[]{:S(2)}, u32[]{:S(2)}) collective-permute-start(f32[65,128]{1,0:T(8,128)S(1)} %fusion.76), channel_id=1, source_target_pairs={{0,56},{8,0},{16,8},{24,16},{32,24},{40,32},{48,40},{56,48},{1,57}... | collective-permute-start | bytes 99848 | tf_op jit(solution)/shard_map/ppermute | solution.py:99
  27.9 1.2 collective-permute-start.7
  30.1 4.5 %collective-permute-start.5 = (f32[65,128]{1,0:T(8,128)S(1)}, f32[65,128]{1,0:T(8,128)S(1)}, u32[]{:S(2)}, u32[]{:S(2)}) collective-permute-start(f32[65,128]{1,0:T(8,128)S(1)} %fusion.76), channel_id=1, source_target_pairs={{0,32},{8,40},{16,48},{24,56},{32,0},{40,8},{48,16},{56,24},{1,33}... | collective-permute-start | bytes 99848 | tf_op jit(solution)/shard_map/ppermute | solution.py:99
  34.6 2.2 %collective-permute-start.3 = (f32[65,128]{1,0:T(8,128)S(1)}, f32[65,128]{1,0:T(8,128)S(1)}, u32[]{:S(2)}, u32[]{:S(2)}) collective-permute-start(f32[65,128]{1,0:T(8,128)S(1)} %fusion.76), channel_id=1, source_target_pairs={{0,16},{8,24},{16,32},{24,40},{32,48},{40,56},{48,0},{56,8},{1,17}... | collective-permute-start | bytes 99848 | tf_op jit(solution)/shard_map/ppermute | solution.py:99
  36.8 1.4 collective-permute-start.2
  38.8 4.5 %collective-permute-start = (bf16[512,256]{1,0:T(8,128)(2,1)}, bf16[512,256]{1,0:T(8,128)(2,1)}, u32[]{:S(2)}, u32[]{:S(2)}) collective-permute-start(bf16[512,256]{1,0:T(8,128)(2,1)} %pad_maximum_fusion.1), channel_id=1, source_target_pairs={{0,4},{4,8},{8,12},{12,16},{16,20},{20,24},{24,28},{28,32},{32,36}... | collective-permute-start | bytes 786440 | tf_op jit(solution)/shard_map/ppermute | solution.py:13
  43.4 19.5 %collective-permute-start.9 = (f32[65,128]{1,0:T(8,128)S(1)}, f32[65,128]{1,0:T(8,128)S(1)}, u32[]{:S(2)}, u32[]{:S(2)}) collective-permute-start(f32[65,128]{1,0:T(8,128)S(1)} %add_add_fusion), channel_id=1, source_target_pairs={{0,64},{64,128},{128,192},{1,65},{65,129},{129,193},{2,66},{66,130... | collective-permute-start | bytes 99848 | tf_op jit(solution)/shard_map/ppermute | solution.py:107
  63.5 1.9 %collective-permute-done.9 = f32[65,128]{1,0:T(8,128)S(1)} collective-permute-done((f32[65,128]{1,0:T(8,128)S(1)}, f32[65,128]{1,0:T(8,128)S(1)}, u32[]{:S(2)}, u32[]{:S(2)}) %collective-permute-start.9) | collective-permute-done | bytes 33312 | tf_op jit(solution)/shard_map/ppermute | solution.py:107
  65.4 3.5 %collective-permute-start.10 = (f32[65,128]{1,0:T(8,128)S(1)}, f32[65,128]{1,0:T(8,128)S(1)}, u32[]{:S(2)}, u32[]{:S(2)}) collective-permute-start(f32[65,128]{1,0:T(8,128)S(1)} %add.319), channel_id=1, source_target_pairs={{0,128},{64,192},{1,129},{65,193},{2,130},{66,194},{3,131},{67,195... | collective-permute-start | bytes 99848 | tf_op jit(solution)/shard_map/ppermute | solution.py:107
  70.3 0.8 copy.55
  71.1 0.8 copy.54
  72.0 0.9 copy.56
  73.5 3.7 %fusion.39 = f32[1,512,8]{0,1,2:T(8,128)S(1)} fusion(f32[512,8,64]{0,2,1:T(8,128)S(1)} %get-tuple-element.49, u8[512,64]{0,1:T(8,128)(4,1)S(1)} %get-tuple-element.48, f32[65,128]{1,0:T(8,128)S(1)} %subtract_add_fusion), kind=kOutput, calls=%fused_computation.59 | convolution fusion | flops 4980736 | bytes 1098240 | tf_op jit(solution)/shard_map/qhr,r->qh/dot_general | solution.py:124
  77.2 1.2 copy.39
  78.5 3.2 %fusion.41 = f32[512,8,128]{0,2,1:T(8,128)S(1)} fusion(f32[512,8,64]{0,2,1:T(8,128)S(1)} %get-tuple-element.49, u8[512,64]{0,1:T(8,128)(4,1)} %copy-done.10, f32[65,128]{1,0:T(8,128)} %copy-done.15), kind=kOutput, calls=%fused_computation.60 | convolution fusion | flops 404488192 | bytes 3211264 | tf_op jit(solution)/shard_map/qhr,rd->qhd/dot_general | solution.py:123
  81.7 1.0 fusion.78
  82.7 1.5 gather_fusion.6
  84.2 1.3 gather_fusion.4
  85.5 1.3 gather_fusion.7
  86.8 0.7 gather_fusion.5
  87.5 1.3 gather_fusion.2
  88.9 1.3 gather_fusion.3
  90.2 0.7 gather_fusion
  90.9 0.7 gather_fusion.1
  91.6 1.0 broadcast_select_fusion.1
  92.7 1.2 fusion.79
  98.6 2.7 %collective-permute-start.12 = (bf16[512,1024]{0,1:T(8,128)(2,1)S(1)}, bf16[512,1024]{0,1:T(8,128)(2,1)}, u32[]{:S(2)}, u32[]{:S(2)}) collective-permute-start(bf16[512,1024]{0,1:T(8,128)(2,1)S(1)} %pad_maximum_fusion), channel_id=1, source_target_pairs={{0,1},{1,2},{2,3},{3,0},{4,5},{5,6},{6,7},{7,4},{8,9},{9,10},{10,1... | collective-permute-start | bytes 3145736 | tf_op jit(solution)/shard_map/ppermute | solution.py:168
  101.3 2.6 %collective-permute-start.13 = (bf16[512,1024]{0,1:T(8,128)(2,1)S(1)}, bf16[512,1024]{0,1:T(8,128)(2,1)}, u32[]{:S(2)}, u32[]{:S(2)}) collective-permute-start(bf16[512,1024]{0,1:T(8,128)(2,1)S(1)} %pad_maximum_fusion), channel_id=1, source_target_pairs={{0,2},{1,3},{2,0},{3,1},{4,6},{5,7},{6,4},{7,5},{8,10},{9,11},{10,... | collective-permute-start | bytes 3145736 | tf_op jit(solution)/shard_map/ppermute | solution.py:168
  104.0 20.7 %collective-permute-done.12 = bf16[512,1024]{0,1:T(8,128)(2,1)} collective-permute-done((bf16[512,1024]{0,1:T(8,128)(2,1)S(1)}, bf16[512,1024]{0,1:T(8,128)(2,1)}, u32[]{:S(2)}, u32[]{:S(2)}) %collective-permute-start.12) | collective-permute-done | bytes 1048608 | tf_op jit(solution)/shard_map/ppermute | solution.py:168
  124.7 14.2 %all-gather.2.cloned.1.call-done = bf16[1024,8192]{1,0:T(8,128)(2,1)} async-done(((bf16[1024,128]{1,0:T(8,128)(2,1)}), bf16[1024,8192]{1,0:T(8,128)(2,1)}) %all-gather.2.cloned.1.call-update) | async-done | bytes 16777232 | tf_op jit(solution)/shard_map/all_gather | solution.py:161
  138.9 4.9 %fusion.4 = f32[512,2048]{1,0:T(8,128)S(1)} fusion(bf16[512,1024]{0,1:T(8,128)(2,1)} %collective-permute-done.12, bf16[1024,8192]{1,0:T(8,128)(2,1)} %all-gather.2.cloned.1.call-done), kind=kOutput, calls=%fused_computation.12 | convolution fusion | flops 2147483648 | bytes 9437184 | tf_op jit(solution)/shard_map/dot_general | solution.py:171
  143.8 4.3 %collective-permute-done.13 = bf16[512,1024]{0,1:T(8,128)(2,1)} collective-permute-done((bf16[512,1024]{0,1:T(8,128)(2,1)S(1)}, bf16[512,1024]{0,1:T(8,128)(2,1)}, u32[]{:S(2)}, u32[]{:S(2)}) %collective-permute-start.13) | collective-permute-done | bytes 1048608 | tf_op jit(solution)/shard_map/ppermute | solution.py:168
  148.1 4.9 %fusion.2 = f32[512,2048]{1,0:T(8,128)S(1)} fusion(bf16[512,1024]{0,1:T(8,128)(2,1)} %collective-permute-done.13, bf16[1024,8192]{1,0:T(8,128)(2,1)} %all-gather.2.cloned.1.call-done), kind=kOutput, calls=%fused_computation.10 | convolution fusion | flops 2147483648 | bytes 9437184 | tf_op jit(solution)/shard_map/dot_general | solution.py:171
  153.0 4.6 %fusion.6 = f32[512,2048]{1,0:T(8,128)S(1)} fusion(bf16[1024,8192]{1,0:T(8,128)(2,1)} %all-gather.2.cloned.1.call-done, bf16[128,1024]{0,1:T(8,128)(2,1)S(1)} %bitcast.129, bf16[128,1024]{0,1:T(8,128)(2,1)S(1)} %bitcast.127, bf16[128,1024]{0,1:T(8,128)(2,1)S(1)} %bitcast.125, bf16[128,1024]{0,1:T(8,128)(2,1)S(1)} %bitcast.131), kind=kOutput, calls=%fused_computation.14 | convolution fusion | flops 2151677952 | bytes 9437184 | tf_op jit(solution)/shard_map/dot_general | solution.py:171
  157.6 6.2 %add_convert_fusion = bf16[512,2048]{1,0:T(8,128)(2,1)} fusion(f32[512,2048]{1,0:T(8,128)S(1)} %fusion.2, f32[512,2048]{1,0:T(8,128)S(1)} %fusion.6, f32[512,2048]{1,0:T(8,128)S(1)} %fusion.4, bf16[512,1024]{0,1:T(8,128)(2,1)S(1)} %collective-permute-done.14, bf16[1024,8192]{1,0:T(8,128)(2,1)} %all-gather.2.cloned.1.call-done), kind=kOutput, calls=%fused_computation.16 | convolution fusion | flops 2151677952 | bytes 19922944 | tf_op jit(solution)/shard_map/dot_general | solution.py:171
  (101 shorter events, 10.4 us)
Async XLA Ops:
  6.5 16.3 %copy-start = (bf16[1,128,64]{1,2,0:T(8,128)(2,1)S(1)}, bf16[1,128,64]{1,2,0:T(8,128)(2,1)}, u32[]{:S(2)}) copy-start(bf16[1,128,64]{1,2,0:T(8,128)(2,1)} %param.16) | copy-start | bytes 49156
  6.5 16.2 %copy-start.1 = (bf16[512,1024]{1,0:T(8,128)(2,1)S(1)}, bf16[512,1024]{1,0:T(8,128)(2,1)}, u32[]{:S(2)}) copy-start(bf16[512,1024]{1,0:T(8,128)(2,1)} %param.11) | copy-start | bytes 3145732
  6.5 132.4 %all-gather.2.cloned.1.call-start = ((), (), s32[]{:S(2)}) async-start(), calls=%async_computation | async-start | bytes 17039360 | tf_op jit(solution)/shard_map/all_gather | solution.py:161
  6.5 1.7 %collective-permute-start.11 = (bf16[1024,128]{1,0:T(8,128)(2,1)}, bf16[1024,128]{1,0:T(8,128)(2,1)S(1)}, u32[]{:S(2)}, u32[]{:S(2)}) collective-permute-start(bf16[1024,128]{1,0:T(8,128)(2,1)} %param.19), channel_id=1, source_target_pairs={{0,0},{64,65},{128,130},{192,195},{1,192},{65,1},{129,66},{193,131... | collective-permute-start | bytes 786440 | tf_op jit(solution)/shard_map/ppermute | solution.py:160
  8.3 0.7 copy-start.11
  12.1 11.8 %collective-permute-start.1 = (f32[65,128]{1,0:T(8,128)S(1)}, f32[65,128]{1,0:T(8,128)S(1)}, u32[]{:S(2)}, u32[]{:S(2)}) collective-permute-start(f32[65,128]{1,0:T(8,128)S(1)} %select_maximum_fusion), channel_id=1, source_target_pairs={{0,4},{4,0},{1,5},{5,1},{2,6},{6,2},{3,7},{7,3},{8,12},{12,8},{9,1... | collective-permute-start | bytes 99848 | tf_op jit(solution)/shard_map/ppermute | solution.py:99
  23.3 53.9 %copy-start.10 = (u8[512,64]{0,1:T(8,128)(4,1)}, u8[512,64]{0,1:T(8,128)(4,1)S(1)}, u32[]{:S(2)}) copy-start(u8[512,64]{0,1:T(8,128)(4,1)S(1)} %get-tuple-element.48) | copy-start | bytes 98308
  24.0 10.7 %collective-permute-start.8 = (f32[65,128]{1,0:T(8,128)S(1)}, f32[65,128]{1,0:T(8,128)S(1)}, u32[]{:S(2)}, u32[]{:S(2)}) collective-permute-start(f32[65,128]{1,0:T(8,128)S(1)} %fusion.76), channel_id=1, source_target_pairs={{0,56},{8,0},{16,8},{24,16},{32,24},{40,32},{48,40},{56,48},{1,57}... | collective-permute-start | bytes 99848 | tf_op jit(solution)/shard_map/ppermute | solution.py:99
  27.9 8.9 %collective-permute-start.7 = (f32[65,128]{1,0:T(8,128)S(1)}, f32[65,128]{1,0:T(8,128)S(1)}, u32[]{:S(2)}, u32[]{:S(2)}) collective-permute-start(f32[65,128]{1,0:T(8,128)S(1)} %fusion.76), channel_id=1, source_target_pairs={{0,48},{8,56},{16,0},{24,8},{32,16},{40,24},{48,32},{56,40},{1,49}... | collective-permute-start | bytes 99848 | tf_op jit(solution)/shard_map/ppermute | solution.py:99
  29.7 9.1 %collective-permute-start.6 = (f32[65,128]{1,0:T(8,128)S(1)}, f32[65,128]{1,0:T(8,128)S(1)}, u32[]{:S(2)}, u32[]{:S(2)}) collective-permute-start(f32[65,128]{1,0:T(8,128)S(1)} %fusion.76), channel_id=1, source_target_pairs={{0,40},{8,48},{16,56},{24,0},{32,8},{40,16},{48,24},{56,32},{1,41}... | collective-permute-start | bytes 99848 | tf_op jit(solution)/shard_map/ppermute | solution.py:99
  30.1 13.2 %collective-permute-start.5 = (f32[65,128]{1,0:T(8,128)S(1)}, f32[65,128]{1,0:T(8,128)S(1)}, u32[]{:S(2)}, u32[]{:S(2)}) collective-permute-start(f32[65,128]{1,0:T(8,128)S(1)} %fusion.76), channel_id=1, source_target_pairs={{0,32},{8,40},{16,48},{24,56},{32,0},{40,8},{48,16},{56,24},{1,33}... | collective-permute-start | bytes 99848 | tf_op jit(solution)/shard_map/ppermute | solution.py:99
  34.6 8.7 %collective-permute-start.4 = (f32[65,128]{1,0:T(8,128)S(1)}, f32[65,128]{1,0:T(8,128)S(1)}, u32[]{:S(2)}, u32[]{:S(2)}) collective-permute-start(f32[65,128]{1,0:T(8,128)S(1)} %fusion.76), channel_id=1, source_target_pairs={{0,24},{8,32},{16,40},{24,48},{32,56},{40,0},{48,8},{56,16},{1,25}... | collective-permute-start | bytes 99848 | tf_op jit(solution)/shard_map/ppermute | solution.py:99
  34.6 8.7 %collective-permute-start.3 = (f32[65,128]{1,0:T(8,128)S(1)}, f32[65,128]{1,0:T(8,128)S(1)}, u32[]{:S(2)}, u32[]{:S(2)}) collective-permute-start(f32[65,128]{1,0:T(8,128)S(1)} %fusion.76), channel_id=1, source_target_pairs={{0,16},{8,24},{16,32},{24,40},{32,48},{40,56},{48,0},{56,8},{1,17}... | collective-permute-start | bytes 99848 | tf_op jit(solution)/shard_map/ppermute | solution.py:99
  36.8 6.6 %collective-permute-start.2 = (f32[65,128]{1,0:T(8,128)S(1)}, f32[65,128]{1,0:T(8,128)S(1)}, u32[]{:S(2)}, u32[]{:S(2)}) collective-permute-start(f32[65,128]{1,0:T(8,128)S(1)} %fusion.76), channel_id=1, source_target_pairs={{0,8},{8,16},{16,24},{24,32},{32,40},{40,48},{48,56},{56,0},{1,9},... | collective-permute-start | bytes 99848 | tf_op jit(solution)/shard_map/ppermute | solution.py:99
  38.8 42.9 %collective-permute-start = (bf16[512,256]{1,0:T(8,128)(2,1)}, bf16[512,256]{1,0:T(8,128)(2,1)}, u32[]{:S(2)}, u32[]{:S(2)}) collective-permute-start(bf16[512,256]{1,0:T(8,128)(2,1)} %pad_maximum_fusion.1), channel_id=1, source_target_pairs={{0,4},{4,8},{8,12},{12,16},{16,20},{20,24},{24,28},{28,32},{32,36}... | collective-permute-start | bytes 786440 | tf_op jit(solution)/shard_map/ppermute | solution.py:13
  43.4 22.0 %collective-permute-start.9 = (f32[65,128]{1,0:T(8,128)S(1)}, f32[65,128]{1,0:T(8,128)S(1)}, u32[]{:S(2)}, u32[]{:S(2)}) collective-permute-start(f32[65,128]{1,0:T(8,128)S(1)} %add_add_fusion), channel_id=1, source_target_pairs={{0,64},{64,128},{128,192},{1,65},{65,129},{129,193},{2,66},{66,130... | collective-permute-start | bytes 99848 | tf_op jit(solution)/shard_map/ppermute | solution.py:107
  65.4 7.5 %collective-permute-start.10 = (f32[65,128]{1,0:T(8,128)S(1)}, f32[65,128]{1,0:T(8,128)S(1)}, u32[]{:S(2)}, u32[]{:S(2)}) collective-permute-start(f32[65,128]{1,0:T(8,128)S(1)} %add.319), channel_id=1, source_target_pairs={{0,128},{64,192},{1,129},{65,193},{2,130},{66,194},{3,131},{67,195... | collective-permute-start | bytes 99848 | tf_op jit(solution)/shard_map/ppermute | solution.py:107
  72.9 0.6 copy-start.15
  78.5 4.2 %copy-start.5 = (bf16[512,128]{1,0:T(8,128)(2,1)S(1)}, bf16[512,128]{1,0:T(8,128)(2,1)}, u32[]{:S(2)}) copy-start(bf16[512,128]{1,0:T(8,128)(2,1)} %param.12) | copy-start | bytes 393220
  78.5 7.0 %copy-start.6 = (bf16[512,128]{1,0:T(8,128)(2,1)S(1)}, bf16[512,128]{1,0:T(8,128)(2,1)}, u32[]{:S(2)}) copy-start(bf16[512,128]{1,0:T(8,128)(2,1)} %param.13) | copy-start | bytes 393220
  82.7 10.0 %copy-start.4 = (bf16[128,1024]{0,1:T(8,128)(2,1)S(1)}, bf16[128,1024]{0,1:T(8,128)(2,1)}, u32[]{:S(2)}) copy-start(bf16[128,1024]{0,1:T(8,128)(2,1)} %copy.56) | copy-start | bytes 786436
  92.6 1.5 copy-start.8
  92.6 1.5 copy-start.9
  92.6 1.5 copy-start.18
  92.7 1.6 copy-start.3
  92.7 1.6 copy-start.14
  94.3 0.9 copy-start.7
  94.3 0.9 copy-start.19
  94.3 1.0 copy-start.2
  94.3 1.0 copy-start.13
  95.3 0.7 copy-start.17
  95.3 0.8 copy-start.12
  96.1 0.7 copy-start.16
  98.6 26.1 %collective-permute-start.12 = (bf16[512,1024]{0,1:T(8,128)(2,1)S(1)}, bf16[512,1024]{0,1:T(8,128)(2,1)}, u32[]{:S(2)}, u32[]{:S(2)}) collective-permute-start(bf16[512,1024]{0,1:T(8,128)(2,1)S(1)} %pad_maximum_fusion), channel_id=1, source_target_pairs={{0,1},{1,2},{2,3},{3,0},{4,5},{5,6},{6,7},{7,4},{8,9},{9,10},{10,1... | collective-permute-start | bytes 3145736 | tf_op jit(solution)/shard_map/ppermute | solution.py:168
  101.3 46.8 %collective-permute-start.13 = (bf16[512,1024]{0,1:T(8,128)(2,1)S(1)}, bf16[512,1024]{0,1:T(8,128)(2,1)}, u32[]{:S(2)}, u32[]{:S(2)}) collective-permute-start(bf16[512,1024]{0,1:T(8,128)(2,1)S(1)} %pad_maximum_fusion), channel_id=1, source_target_pairs={{0,2},{1,3},{2,0},{3,1},{4,6},{5,7},{6,4},{7,5},{8,10},{9,11},{10,... | collective-permute-start | bytes 3145736 | tf_op jit(solution)/shard_map/ppermute | solution.py:168
  103.9 53.7 %collective-permute-start.14 = (bf16[512,1024]{0,1:T(8,128)(2,1)S(1)}, bf16[512,1024]{0,1:T(8,128)(2,1)S(1)}, u32[]{:S(2)}, u32[]{:S(2)}) collective-permute-start(bf16[512,1024]{0,1:T(8,128)(2,1)S(1)} %pad_maximum_fusion), channel_id=1, source_target_pairs={{0,3},{1,0},{2,1},{3,2},{4,7},{5,4},{6,5},{7,6},{8,11},{9,8},{10,9... | collective-permute-start | bytes 3145736 | tf_op jit(solution)/shard_map/ppermute | solution.py:168
Sparse Core Ops, SparseCore 0:
  9.9 128.9 all-gather.1

commit v9 on v5

--- a/solution.py
+++ b/solution.py
@@ -146,24 +146,21 @@
     group_cols = jnp.concatenate(row_pieces, axis=0)
     n_tp = lax.axis_size("tp")
     swap = [
-        (rows * n_tp + group, ((rows - group) % n_tp) * n_tp + rows)
+        (rows * n_tp + group, group * n_tp + rows)
         for group in range(n_tp)
         for rows in range(n_tp)
     ]
     moved = lax.ppermute(out_weight, ("ctx_0", "tp"), swap)
     gathered = lax.all_gather(moved, CTX, axis=1, tiled=True)
     width = gathered.shape[1] // n_tp
+    every_group = lax.all_to_all(
+        jnp.broadcast_to(group_cols, (n_tp, *group_cols.shape)), "tp", 0, 0
+    )
     summed = None
-    for shift in range(n_tp):
-        if shift == 0:
-            rows_in = group_cols
-        else:
-            rows_in = lax.ppermute(
-                group_cols, "tp", [(i, (i + shift) % n_tp) for i in range(n_tp)]
-            )
+    for group in range(n_tp):
         term = jnp.dot(
-            rows_in,
-            gathered[:, shift * width : (shift + 1) * width],
+            every_group[group],
+            gathered[:, group * width : (group + 1) * width],
             preferred_element_type=jnp.float32,
         )
         summed = term if summed is None else summed + term

time: 167 us -> 176 us (1.054)
  blocking collectives: 0 us -> 50.6 us
  waiting for transfers between devices: 40.6 us -> 1.34 us
  starting transfers between devices: 47.7 us -> 44.8 us
    all_to_all x0 -> x1, blocking collectives: none -> 50.6 us  [body(): lax.all_to_all(jnp.broadcast_to(group_cols, (n_tp, *group_cols.shape)), '...]
    all_gather x1, waiting for transfers between devices: 20 us -> 0.01 us  [body(): gathered = lax.all_gather(moved, CTX, axis=1, tiled=True)]
    ppermute x3 -> x0, waiting for transfers between devices: 19.9 us -> none  [body(): lax.ppermute(group_cols, 'tp', [(i, (i + shift) % n_tp) for i in range(n_...]
    ppermute x3 -> x0, starting transfers between devices: 4.01 us -> none  [body(): lax.ppermute(group_cols, 'tp', [(i, (i + shift) % n_tp) for i in range(n_...]
    unnamed x44 -> x46, local copies, waits for them, and re-layouts: 4.56 us -> 4.55 us
  transfers between devices with their start and end apart: 17 -> 14, of which waited for: 3 -> 1; matrix products, arithmetic and copies ran while one was open for 33% -> 24% of each run, Pallas kernels for 0% -> 0%
where the time goes in v9:
time: 176 us; the launch traced here: 175 us
  blocking collectives  50.6 us (29%)
  starting transfers between devices  44.8 us (25%)
  matrix products  33.7 us (19%)
  local copies, waits for them, and re-layouts  17.7 us (10%)
  between operations  14.6 us (8%)
  other arithmetic  12.4 us (7%)
    all_to_all x1, blocking collectives, body(): lax.all_to_all(jnp.broadcast_to(group_cols, (n_tp, *group_cols.shape)), '...  50.6 us
    ppermute x11, starting transfers between devices, body(): lax.ppermute(running, axis, [(i, (i + shift) % size) for i in range(size)])  38.5 us
    dot_general x4, matrix products, body(): jnp.dot(every_group[group], gathered[:, group * width:(group + 1) * width...  20 us
    gather x4, local copies, waits for them, and re-layouts, body(): key_rows = jnp.take(window_keys, chosen, axis=0).reshape(-1, head_dim)  4.75 us
    unnamed x46, local copies, waits for them, and re-layouts  4.55 us
    ppermute x1, starting transfers between devices, passed_along(): return lax.ppermute(block, axis, route)  4.54 us
    gather x4, local copies, waits for them, and re-layouts, body(): value_rows = jnp.take(window_values, chosen, axis=0).reshape(-1, head_dim)  4 us
    dot_general x1, matrix products, body(): mass = jnp.einsum('qhr,r->qh', query_feats, norms[group], precision=highest)  3.72 us
  transfers between devices with their start and end apart: 14, of which 1 were waited for; matrix products, arithmetic and copies ran while one was open for 24% of the time, Pallas kernels for 0%

profile of v9, /device:TPU:1, one launch (start us, length us, event | category | flops | bytes accessed | tf_op | source)
XLA Modules:
  0.0 175.0 jit_solution(17950612397384050479)
XLA Ops:
  6.5 1.7 collective-permute-start.12
  8.3 0.7 copy-done.12
  9.0 0.7 convert_element_type.46
  9.7 1.2 fusion.57
  10.9 1.2 fusion.58
  12.1 3.3 %collective-permute-start.1 = (f32[65,128]{1,0:T(8,128)S(1)}, f32[65,128]{1,0:T(8,128)S(1)}, u32[]{:S(2)}, u32[]{:S(2)}) collective-permute-start(f32[65,128]{1,0:T(8,128)S(1)} %select_maximum_fusion), channel_id=1, source_target_pairs={{0,4},{4,0},{1,5},{5,1},{2,6},{6,2},{3,7},{7,3},{8,12},{12,8},{9,1... | collective-permute-start | bytes 99848 | tf_op jit(solution)/shard_map/ppermute | solution.py:99
  15.4 1.0 slice_reduce_fusion.3
  16.6 0.7 compare_and_fusion.6
  17.9 1.7 pad_maximum_fusion.1
  20.2 0.8 compare_and_fusion.2
  20.9 0.8 compare_and_fusion.3
  21.7 0.8 compare_and_fusion
  22.5 0.8 compare_and_fusion.1
  23.9 0.6 pad_clamp_fusion.3
  24.5 3.9 %collective-permute-start.8 = (f32[65,128]{1,0:T(8,128)S(1)}, f32[65,128]{1,0:T(8,128)S(1)}, u32[]{:S(2)}, u32[]{:S(2)}) collective-permute-start(f32[65,128]{1,0:T(8,128)S(1)} %fusion.78), channel_id=1, source_target_pairs={{0,56},{8,0},{16,8},{24,16},{32,24},{40,32},{48,40},{56,48},{1,57}... | collective-permute-start | bytes 99848 | tf_op jit(solution)/shard_map/ppermute | solution.py:99
  28.5 1.2 collective-permute-start.7
  29.6 0.6 compare_and_fusion.4
  30.7 4.5 %collective-permute-start.5 = (f32[65,128]{1,0:T(8,128)S(1)}, f32[65,128]{1,0:T(8,128)S(1)}, u32[]{:S(2)}, u32[]{:S(2)}) collective-permute-start(f32[65,128]{1,0:T(8,128)S(1)} %fusion.78), channel_id=1, source_target_pairs={{0,32},{8,40},{16,48},{24,56},{32,0},{40,8},{48,16},{56,24},{1,33}... | collective-permute-start | bytes 99848 | tf_op jit(solution)/shard_map/ppermute | solution.py:99
  35.2 2.2 %collective-permute-start.3 = (f32[65,128]{1,0:T(8,128)S(1)}, f32[65,128]{1,0:T(8,128)S(1)}, u32[]{:S(2)}, u32[]{:S(2)}) collective-permute-start(f32[65,128]{1,0:T(8,128)S(1)} %fusion.78), channel_id=1, source_target_pairs={{0,16},{8,24},{16,32},{24,40},{32,48},{40,56},{48,0},{56,8},{1,17}... | collective-permute-start | bytes 99848 | tf_op jit(solution)/shard_map/ppermute | solution.py:99
  37.4 1.4 collective-permute-start.2
  39.4 4.5 %collective-permute-start = (bf16[512,256]{1,0:T(8,128)(2,1)}, bf16[512,256]{1,0:T(8,128)(2,1)}, u32[]{:S(2)}, u32[]{:S(2)}) collective-permute-start(bf16[512,256]{1,0:T(8,128)(2,1)} %pad_maximum_fusion.1), channel_id=1, source_target_pairs={{0,4},{4,8},{8,12},{12,16},{16,20},{20,24},{24,28},{28,32},{32,36}... | collective-permute-start | bytes 786440 | tf_op jit(solution)/shard_map/ppermute | solution.py:13
  44.0 21.0 %collective-permute-start.11 = (f32[65,128]{1,0:T(8,128)S(1)}, f32[65,128]{1,0:T(8,128)S(1)}, u32[]{:S(2)}, u32[]{:S(2)}) collective-permute-start(f32[65,128]{1,0:T(8,128)S(1)} %add_add_fusion), channel_id=1, source_target_pairs={{0,192},{64,0},{128,64},{192,128},{1,193},{65,1},{129,65},{193,129... | collective-permute-start | bytes 99848 | tf_op jit(solution)/shard_map/ppermute | solution.py:99
  65.0 0.7 collective-permute-start.9
  65.6 0.6 pad_clamp_fusion.1
  67.1 0.8 copy.57
  67.9 0.8 copy.56
  68.7 0.8 copy.58
  69.6 1.3 collective-permute-done.10
  70.9 0.6 copy-done.16
  71.5 3.7 %fusion.41 = f32[1,512,8]{0,1,2:T(8,128)S(1)} fusion(f32[512,8,64]{0,2,1:T(8,128)S(1)} %get-tuple-element.49, u8[512,64]{0,1:T(8,128)(4,1)S(1)} %get-tuple-element.48, f32[65,128]{1,0:T(8,128)S(1)} %select_add_fusion), kind=kOutput, calls=%fused_computation.63 | convolution fusion | flops 4980736 | bytes 1098240 | tf_op jit(solution)/shard_map/qhr,r->qh/dot_general | solution.py:117
  75.3 1.2 copy.41
  76.5 3.2 %fusion.43 = f32[512,8,128]{0,2,1:T(8,128)S(1)} fusion(f32[512,8,64]{0,2,1:T(8,128)S(1)} %get-tuple-element.49, u8[512,64]{0,1:T(8,128)(4,1)} %copy-done.11, f32[65,128]{1,0:T(8,128)} %copy-done.16), kind=kOutput, calls=%fused_computation.64 | convolution fusion | flops 404488192 | bytes 3211264 | tf_op jit(solution)/shard_map/qhr,rd->qhd/dot_general | solution.py:116
  79.7 1.0 fusion.80
  80.7 1.4 gather_fusion.6
  82.2 1.3 gather_fusion.4
  83.5 1.3 gather_fusion.7
  84.8 0.7 gather_fusion.5
  85.5 1.3 gather_fusion.2
  86.8 1.3 gather_fusion.3
  88.1 0.7 gather_fusion
  88.8 0.7 gather_fusion.1
  89.5 1.0 broadcast_select_fusion.1
  90.6 1.2 fusion.81
  97.6 50.6 %all_to_all.5 = bf16[4,512,1024]{2,1,0:T(8,128)(2,1)} all-to-all(bf16[4,512,1024]{2,1,0:T(8,128)(2,1)S(1)} %broadcast_in_dim.96), channel_id=1, replica_groups=mesh['ctx_0'=4,'ctx_1'=8,'ctx_2'=2,'tp'=4] {'tp'}, dimensions={0} | all-to-all | bytes 8388608 | tf_op jit(solution)/shard_map/all_to_all | solution.py:156
  148.2 5.0 %fusion.2 = f32[512,2048]{1,0:T(8,128)S(1)} fusion(bf16[1024,8192]{1,0:T(8,128)(2,1)} %all-gather.2.cloned.1.call-done, bf16[4,512,1024]{2,1,0:T(8,128)(2,1)} %all_to_all.5), kind=kOutput, calls=%fused_computation.10 | convolution fusion | flops 2147483648 | bytes 9437184 | tf_op jit(solution)/shard_map/dot_general | solution.py:161
  153.2 4.5 %fusion.4 = f32[512,2048]{1,0:T(8,128)S(1)} fusion(bf16[1024,8192]{1,0:T(8,128)(2,1)} %all-gather.2.cloned.1.call-done, bf16[4,512,1024]{2,1,0:T(8,128)(2,1)S(1)} %copy-done.1), kind=kOutput, calls=%fused_computation.12 | convolution fusion | flops 2147483648 | bytes 9437184 | tf_op jit(solution)/shard_map/dot_general | solution.py:161
  157.7 4.5 %fusion.6 = f32[512,2048]{1,0:T(8,128)S(1)} fusion(bf16[1024,8192]{1,0:T(8,128)(2,1)} %all-gather.2.cloned.1.call-done, bf16[4,512,1024]{2,1,0:T(8,128)(2,1)S(1)} %copy-done.1), kind=kOutput, calls=%fused_computation.14 | convolution fusion | flops 2147483648 | bytes 9437184 | tf_op jit(solution)/shard_map/dot_general | solution.py:161
  162.2 5.9 %add_convert_fusion = bf16[512,2048]{1,0:T(8,128)(2,1)} fusion(f32[512,2048]{1,0:T(8,128)S(1)} %fusion.2, f32[512,2048]{1,0:T(8,128)S(1)} %fusion.6, f32[512,2048]{1,0:T(8,128)S(1)} %fusion.4, bf16[1024,8192]{1,0:T(8,128)(2,1)} %all-gather.2.cloned.1.call-done, bf16[4,512,1024]{2,1,0:T(8,128)(2,1)S(1)} %copy-done.1), kind=kOutput, calls=%fused_computation.16 | convolution fusion | flops 2151677952 | bytes 19922944 | tf_op jit(solution)/shard_map/dot_general | solution.py:161
  (101 shorter events, 8.9 us)
Async XLA Ops:
  6.5 16.8 %copy-start = (bf16[1,128,64]{1,2,0:T(8,128)(2,1)S(1)}, bf16[1,128,64]{1,2,0:T(8,128)(2,1)}, u32[]{:S(2)}) copy-start(bf16[1,128,64]{1,2,0:T(8,128)(2,1)} %param.16) | copy-start | bytes 49156
  6.5 16.8 %copy-start.2 = (bf16[512,1024]{1,0:T(8,128)(2,1)S(1)}, bf16[512,1024]{1,0:T(8,128)(2,1)}, u32[]{:S(2)}) copy-start(bf16[512,1024]{1,0:T(8,128)(2,1)} %param.11) | copy-start | bytes 3145732
  6.5 141.6 %all-gather.2.cloned.1.call-start = ((), (), s32[]{:S(2)}) async-start(), calls=%async_computation.1 | async-start | bytes 17039360 | tf_op jit(solution)/shard_map/all_gather | solution.py:154
  6.5 1.7 collective-permute-start.12
  8.3 0.7 copy-start.12
  12.1 12.4 %collective-permute-start.1 = (f32[65,128]{1,0:T(8,128)S(1)}, f32[65,128]{1,0:T(8,128)S(1)}, u32[]{:S(2)}, u32[]{:S(2)}) collective-permute-start(f32[65,128]{1,0:T(8,128)S(1)} %select_maximum_fusion), channel_id=1, source_target_pairs={{0,4},{4,0},{1,5},{5,1},{2,6},{6,2},{3,7},{7,3},{8,12},{12,8},{9,1... | collective-permute-start | bytes 99848 | tf_op jit(solution)/shard_map/ppermute | solution.py:99
  23.9 51.4 %copy-start.11 = (u8[512,64]{0,1:T(8,128)(4,1)}, u8[512,64]{0,1:T(8,128)(4,1)S(1)}, u32[]{:S(2)}) copy-start(u8[512,64]{0,1:T(8,128)(4,1)S(1)} %get-tuple-element.48) | copy-start | bytes 98308
  24.5 10.7 %collective-permute-start.8 = (f32[65,128]{1,0:T(8,128)S(1)}, f32[65,128]{1,0:T(8,128)S(1)}, u32[]{:S(2)}, u32[]{:S(2)}) collective-permute-start(f32[65,128]{1,0:T(8,128)S(1)} %fusion.78), channel_id=1, source_target_pairs={{0,56},{8,0},{16,8},{24,16},{32,24},{40,32},{48,40},{56,48},{1,57}... | collective-permute-start | bytes 99848 | tf_op jit(solution)/shard_map/ppermute | solution.py:99
  28.5 8.9 %collective-permute-start.7 = (f32[65,128]{1,0:T(8,128)S(1)}, f32[65,128]{1,0:T(8,128)S(1)}, u32[]{:S(2)}, u32[]{:S(2)}) collective-permute-start(f32[65,128]{1,0:T(8,128)S(1)} %fusion.78), channel_id=1, source_target_pairs={{0,48},{8,56},{16,0},{24,8},{32,16},{40,24},{48,32},{56,40},{1,49}... | collective-permute-start | bytes 99848 | tf_op jit(solution)/shard_map/ppermute | solution.py:99
  30.3 9.1 %collective-permute-start.6 = (f32[65,128]{1,0:T(8,128)S(1)}, f32[65,128]{1,0:T(8,128)S(1)}, u32[]{:S(2)}, u32[]{:S(2)}) collective-permute-start(f32[65,128]{1,0:T(8,128)S(1)} %fusion.78), channel_id=1, source_target_pairs={{0,40},{8,48},{16,56},{24,0},{32,8},{40,16},{48,24},{56,32},{1,41}... | collective-permute-start | bytes 99848 | tf_op jit(solution)/shard_map/ppermute | solution.py:99
  30.7 13.2 %collective-permute-start.5 = (f32[65,128]{1,0:T(8,128)S(1)}, f32[65,128]{1,0:T(8,128)S(1)}, u32[]{:S(2)}, u32[]{:S(2)}) collective-permute-start(f32[65,128]{1,0:T(8,128)S(1)} %fusion.78), channel_id=1, source_target_pairs={{0,32},{8,40},{16,48},{24,56},{32,0},{40,8},{48,16},{56,24},{1,33}... | collective-permute-start | bytes 99848 | tf_op jit(solution)/shard_map/ppermute | solution.py:99
  35.2 8.7 %collective-permute-start.4 = (f32[65,128]{1,0:T(8,128)S(1)}, f32[65,128]{1,0:T(8,128)S(1)}, u32[]{:S(2)}, u32[]{:S(2)}) collective-permute-start(f32[65,128]{1,0:T(8,128)S(1)} %fusion.78), channel_id=1, source_target_pairs={{0,24},{8,32},{16,40},{24,48},{32,56},{40,0},{48,8},{56,16},{1,25}... | collective-permute-start | bytes 99848 | tf_op jit(solution)/shard_map/ppermute | solution.py:99
  35.2 8.7 %collective-permute-start.3 = (f32[65,128]{1,0:T(8,128)S(1)}, f32[65,128]{1,0:T(8,128)S(1)}, u32[]{:S(2)}, u32[]{:S(2)}) collective-permute-start(f32[65,128]{1,0:T(8,128)S(1)} %fusion.78), channel_id=1, source_target_pairs={{0,16},{8,24},{16,32},{24,40},{32,48},{40,56},{48,0},{56,8},{1,17}... | collective-permute-start | bytes 99848 | tf_op jit(solution)/shard_map/ppermute | solution.py:99
  37.4 6.6 %collective-permute-start.2 = (f32[65,128]{1,0:T(8,128)S(1)}, f32[65,128]{1,0:T(8,128)S(1)}, u32[]{:S(2)}, u32[]{:S(2)}) collective-permute-start(f32[65,128]{1,0:T(8,128)S(1)} %fusion.78), channel_id=1, source_target_pairs={{0,8},{8,16},{16,24},{24,32},{32,40},{40,48},{48,56},{56,0},{1,9},... | collective-permute-start | bytes 99848 | tf_op jit(solution)/shard_map/ppermute | solution.py:99
  39.4 40.3 %collective-permute-start = (bf16[512,256]{1,0:T(8,128)(2,1)}, bf16[512,256]{1,0:T(8,128)(2,1)}, u32[]{:S(2)}, u32[]{:S(2)}) collective-permute-start(bf16[512,256]{1,0:T(8,128)(2,1)} %pad_maximum_fusion.1), channel_id=1, source_target_pairs={{0,4},{4,8},{8,12},{12,16},{16,20},{20,24},{24,28},{28,32},{32,36}... | collective-permute-start | bytes 786440 | tf_op jit(solution)/shard_map/ppermute | solution.py:13
  44.0 25.6 %collective-permute-start.11 = (f32[65,128]{1,0:T(8,128)S(1)}, f32[65,128]{1,0:T(8,128)S(1)}, u32[]{:S(2)}, u32[]{:S(2)}) collective-permute-start(f32[65,128]{1,0:T(8,128)S(1)} %add_add_fusion), channel_id=1, source_target_pairs={{0,192},{64,0},{128,64},{192,128},{1,193},{65,1},{129,65},{193,129... | collective-permute-start | bytes 99848 | tf_op jit(solution)/shard_map/ppermute | solution.py:99
  64.9 5.9 %collective-permute-start.10 = (f32[65,128]{1,0:T(8,128)S(1)}, f32[65,128]{1,0:T(8,128)S(1)}, u32[]{:S(2)}, u32[]{:S(2)}) collective-permute-start(f32[65,128]{1,0:T(8,128)S(1)} %add_add_fusion), channel_id=1, source_target_pairs={{0,128},{64,192},{128,0},{192,64},{1,129},{65,193},{129,1},{193,65... | collective-permute-start | bytes 99848 | tf_op jit(solution)/shard_map/ppermute | solution.py:99
  65.0 5.9 %collective-permute-start.9 = (f32[65,128]{1,0:T(8,128)S(1)}, f32[65,128]{1,0:T(8,128)S(1)}, u32[]{:S(2)}, u32[]{:S(2)}) collective-permute-start(f32[65,128]{1,0:T(8,128)S(1)} %add_add_fusion), channel_id=1, source_target_pairs={{0,64},{64,128},{128,192},{192,0},{1,65},{65,129},{129,193},{193,1... | collective-permute-start | bytes 99848 | tf_op jit(solution)/shard_map/ppermute | solution.py:99
  70.9 0.6 copy-start.16
  76.5 4.2 %copy-start.6 = (bf16[512,128]{1,0:T(8,128)(2,1)S(1)}, bf16[512,128]{1,0:T(8,128)(2,1)}, u32[]{:S(2)}) copy-start(bf16[512,128]{1,0:T(8,128)(2,1)} %param.12) | copy-start | bytes 393220
  76.5 7.0 %copy-start.7 = (bf16[512,128]{1,0:T(8,128)(2,1)S(1)}, bf16[512,128]{1,0:T(8,128)(2,1)}, u32[]{:S(2)}) copy-start(bf16[512,128]{1,0:T(8,128)(2,1)} %param.13) | copy-start | bytes 393220
  80.7 9.9 %copy-start.5 = (bf16[128,1024]{0,1:T(8,128)(2,1)S(1)}, bf16[128,1024]{0,1:T(8,128)(2,1)}, u32[]{:S(2)}) copy-start(bf16[128,1024]{0,1:T(8,128)(2,1)} %copy.58) | copy-start | bytes 786436
  90.6 1.5 copy-start.9
  90.6 1.5 copy-start.10
  90.6 1.5 copy-start.19
  90.6 1.6 copy-start.4
  90.6 1.6 copy-start.15
  92.2 0.9 copy-start.8
  92.2 0.9 copy-start.20
  92.3 1.0 copy-start.3
  92.3 1.0 copy-start.14
  93.2 0.6 copy-start.18
  93.2 0.8 copy-start.13
  94.1 0.7 copy-start.17
  148.2 5.0 %copy-start.1 = (bf16[4,512,1024]{2,1,0:T(8,128)(2,1)S(1)}, bf16[4,512,1024]{2,1,0:T(8,128)(2,1)}, u32[]{:S(2)}) copy-start(bf16[4,512,1024]{2,1,0:T(8,128)(2,1)} %all_to_all.5) | copy-start | bytes 12582916
Sparse Core Ops, SparseCore 0:
  9.9 128.9 all-gather.1
